TPU v7x, 512 devices: a whole 4x8x8 slice. The times are simulated.
512 devices in a mesh: grp: 16 (over z, core), dev: 32 (over x, y).
Axes of the slice: x: 4, y: 8, z: 8, core: 2. Of those that a mesh axis runs over, the one named last changes fastest.
Arguments:
- ssm_input: bfloat16 [4096, 4096], P('grp', 'dev'), may hold values from -6 to 6
- gate_input: bfloat16 [4096, 4096], P('grp', 'dev'), may hold values from -6 to 6
- step_size: float32 [4096, 64], P('grp', 'dev'), may hold values from 6.1035156e-05 to 0.3375
- decay_rate: float32 [64], P('dev'), may hold values from 0.5 to 2
- in_coeff: bfloat16 [4096, 128], P('grp'), may hold values from -6 to 6
- out_coeff: bfloat16 [4096, 128], P('grp'), may hold values from -6 to 6
- skip_gain: float32 [64], P('dev'), may hold values from 0.5 to 3
- norm_gain: float32 [4096], P('dev'), may hold values from 0.5 to 1.5
- out_proj: bfloat16 [4096, 2048], P(None, 'dev'), may hold values from -0.09375 to 0.09375
- residual: bfloat16 [4096, 2048], P(('grp', 'dev')), may hold values from -6 to 6
- ffn_gain: float32 [2048], replicated, may hold values from 0.5 to 1.5
- router: float32 [2048, 16], replicated, may hold values from -0.125 to 0.125
- routes: int32 [4096, 2], P(('grp', 'dev')), may hold values from 0 to 15, all different within a row; in each aligned block of 8 rows (0 to 7, 8 to 15, ...) at most 2 rows name the same one
- gate_weight: bfloat16 [16, 2048, 8192], P('grp', None, 'dev'), may hold values from -0.125 to 0.125
- up_weight: bfloat16 [16, 2048, 8192], P('grp', None, 'dev'), may hold values from -0.125 to 0.125
- down_weight: bfloat16 [16, 8192, 2048], P('grp', 'dev'), may hold values from -0.0625 to 0.0625
Outputs:
- moe_out: bfloat16 [4096, 2048], P(('grp', 'dev'))
Inputs may be any that keep to these rules, and one draw needn't show every extreme that they name: `routes`: each row names two different experts; among the 8 rows of one dispatch block of consecutive tokens no expert is named more than 2 times, a bound that some block reaches.
All inputs are finite; a program needn't handle non-finite values.
Results may differ from a plain program's by a relative error of at most 0.012.
Values may be sent and summed in bfloat16 or wider, within the bound.
No kernel may reach another device: no remote copies, remote signals or barrier semaphores. Data moves between devices by JAX's collectives and lax.ppermute only.
A program may use at most 64 MiB of HBM per device.

v0:
```python
import jax
import jax.numpy as jnp
from jax import lax
from jax.sharding import Mesh
from jax.sharding import PartitionSpec as P

DEV = ("dev_0", "dev_1")
GRP_DEV = ("grp", "dev_0", "dev_1")


EPSILON = 1e-05
HIGHEST_PREC = lax.Precision.HIGHEST


def side_by_side(arrays, axis, dim, along):
    columns = [a.reshape(*a.shape[:along], -1) for a in arrays]
    both = jnp.concatenate(columns, axis=along)
    filled, at, finished = (lax.all_gather(both, axis, axis=dim, tiled=True), 0, [])
    for a, column in zip(arrays, columns):
        piece = filled[..., at : at + column.shape[along]]
        finished.append(piece.reshape(*piece.shape[:along], *a.shape[along:]))
        at += column.shape[along]
    return tuple(finished)


def sent_to_all(shard, axis):
    peers = lax.axis_size(axis)
    return lax.all_to_all(
        jnp.broadcast_to(shard[None], (peers, *shard.shape)), axis, 0, 0, tiled=True
    )


def of_everyone(shard, axis):
    everything = sent_to_all(shard, axis)
    return jnp.sum(everything, axis=0)


def in_order(tiles, dim):
    dims = list(tiles.shape[1:])
    dims[dim] *= tiles.shape[0]
    return jnp.moveaxis(tiles, 0, dim).reshape(dims)


def collect(shard, axis, dim):
    return in_order(sent_to_all(shard, axis), dim)


def sum_by_axis(terms, axes):
    total = terms.astype(jnp.bfloat16)
    for axis in axes:
        total = lax.psum_scatter(total, axis, scatter_dimension=0, tiled=True)
    return total.astype(jnp.float32)


def rms_scale(values, gain_vec):
    return (
        values * lax.rsqrt(jnp.mean(values * values, axis=-1, keepdims=True) + EPSILON) * gain_vec
    )


def slot_tables(routes_block, expert_count, slot_cap):
    blocks, row_total = (routes_block.shape[0], routes_block.shape[1])
    flat_routes = routes_block.reshape(blocks, row_total * 2)
    onehot = (
        flat_routes[:, :, None] == jnp.arange(expert_count, dtype=jnp.int32)[None, None, :]
    ).astype(jnp.int32)
    earlier = jnp.cumsum(onehot, axis=1) - onehot
    slot_rank = jnp.sum(earlier * onehot, axis=2)
    slot_index = (flat_routes * slot_cap + slot_rank).reshape(blocks, row_total, 2)
    placed = (
        slot_index[:, :, :, None]
        == jnp.arange(expert_count * slot_cap, dtype=jnp.int32)[None, None, None, :]
    )
    return placed.astype(jnp.float32)


def shards(
    ssm_input,
    gate_input,
    step_size,
    decay_rate,
    in_coeff,
    out_coeff,
    skip_gain,
    norm_gain,
    out_proj,
    residual,
    ffn_gain,
    router,
    routes,
    gate_weight,
    up_weight,
    down_weight,
):
    tok_rows = ssm_input.shape[0]
    head_count = step_size.shape[1]
    head_width = ssm_input.shape[1] // head_count
    dev_count = lax.axis_size(DEV)
    inner_dim = ssm_input.shape[1] * dev_count
    block_rows = residual.shape[0]
    model_dim = residual.shape[1]
    experts = lax.axis_size("grp")
    slot_cap = max(2, 4 * block_rows // experts)
    group_slots = experts * slot_cap
    inputs_f = ssm_input.astype(jnp.float32).reshape(tok_rows, head_count, head_width)
    in_float = in_coeff.astype(jnp.float32)
    out_float = out_coeff.astype(jnp.float32)
    log_rate = -(step_size * decay_rate[None, :])
    cumulative = jnp.cumsum(log_rate, axis=0)
    causal = (jnp.arange(tok_rows)[:, None] >= jnp.arange(tok_rows)[None, :])[:, :, None]
    spread = cumulative[:, None, :] - cumulative[None, :, :]
    decay_pair = jnp.where(causal, jnp.exp(jnp.where(causal, spread, 0.0)), 0.0)
    scores = jnp.dot(out_coeff, in_coeff.T, preferred_element_type=jnp.float32)
    mixing = decay_pair * scores[:, :, None] * step_size[None, :, :]
    inside = jnp.einsum("tuh,uhp->thp", mixing, inputs_f, precision=HIGHEST_PREC)
    to_end = jnp.exp(cumulative[-1][None, :] - cumulative) * step_size
    own_state = jnp.einsum("uh,uhp,un->hpn", to_end, inputs_f, in_float, precision=HIGHEST_PREC)
    own_log = cumulative[-1]
    group_logs, group_states = tuple(
        (
            part.astype(jnp.float32)
            for part in side_by_side(
                (own_log[None].astype(jnp.bfloat16), own_state[None].astype(jnp.bfloat16)),
                "grp",
                0,
                2,
            )
        )
    )
    group_index = jnp.arange(group_logs.shape[0])
    my_group = lax.axis_index("grp")
    inclusive = jnp.cumsum(group_logs, axis=0)
    exclusive = inclusive - group_logs
    before_me = jnp.sum(jnp.where((group_index == my_group)[:, None], exclusive, 0.0), axis=0)
    earlier_mask = (group_index < my_group)[:, None]
    weighting = jnp.where(
        earlier_mask, jnp.exp(jnp.where(earlier_mask, before_me[None, :] - inclusive, 0.0)), 0.0
    )
    entering = jnp.einsum("gh,ghpn->hpn", weighting, group_states, precision=HIGHEST_PREC)
    carried = jnp.exp(cumulative)[:, :, None] * jnp.einsum(
        "hpn,tn->thp", entering, out_float, precision=HIGHEST_PREC
    )
    ssm_out = inside + carried + skip_gain[None, :, None] * inputs_f
    gated_out = ssm_out.reshape(tok_rows, head_count * head_width) * jax.nn.silu(
        gate_input.astype(jnp.float32)
    )
    squares = of_everyone(jnp.sum(gated_out * gated_out, axis=1), DEV)
    mixed_rows = (
        gated_out * lax.rsqrt(squares[:, None] / inner_dim + EPSILON) * norm_gain[None, :]
    ).astype(jnp.bfloat16)
    projected = jnp.dot(
        collect(mixed_rows, DEV, 1), out_proj, preferred_element_type=jnp.float32
    ).astype(jnp.bfloat16)
    mamba_out = lax.all_to_all(projected, DEV, split_axis=0, concat_axis=1, tiled=True)
    hidden_res = (residual.astype(jnp.float32) + mamba_out.astype(jnp.float32)).astype(jnp.bfloat16)
    hidden_float = hidden_res.astype(jnp.float32)
    normed = rms_scale(hidden_float, ffn_gain).astype(jnp.bfloat16)
    logits = jnp.dot(normed.astype(jnp.float32), router, precision=HIGHEST_PREC)
    expert_ids = jnp.arange(experts, dtype=jnp.int32)[None, :]
    first_logit = jnp.sum(logits * (routes[:, 0:1] == expert_ids).astype(jnp.float32), axis=1)
    second_logit = jnp.sum(logits * (routes[:, 1:2] == expert_ids).astype(jnp.float32), axis=1)
    first_prob = jax.nn.sigmoid(first_logit - second_logit)
    second_prob = 1.0 - first_prob
    placed = slot_tables(routes[None], experts, slot_cap)[0]
    filled = jnp.sum(placed, axis=1)
    outgoing = jnp.dot(
        filled.T.astype(jnp.bfloat16), normed, preferred_element_type=jnp.float32
    ).astype(jnp.bfloat16)
    outgoing = outgoing.reshape(experts, slot_cap, model_dim)
    arrived = lax.all_to_all(outgoing, "grp", split_axis=0, concat_axis=0, tiled=True)
    all_rows = lax.all_gather(arrived, DEV, axis=0, tiled=True).reshape(-1, model_dim)
    gate_act = jnp.dot(all_rows, gate_weight[0], preferred_element_type=jnp.float32)
    up_act = jnp.dot(all_rows, up_weight[0], preferred_element_type=jnp.float32)
    hidden = (jax.nn.silu(gate_act) * up_act).astype(jnp.bfloat16)
    summed = sum_by_axis(jnp.dot(hidden, down_weight[0], preferred_element_type=jnp.float32), DEV)
    returned = lax.all_to_all(
        summed.astype(jnp.bfloat16).reshape(experts, slot_cap, model_dim),
        "grp",
        split_axis=0,
        concat_axis=0,
        tiled=True,
    )
    weights = first_prob[:, None] * placed[:, 0, :] + second_prob[:, None] * placed[:, 1, :]
    contrib = jnp.dot(
        weights,
        returned.reshape(group_slots, model_dim).astype(jnp.float32),
        precision=HIGHEST_PREC,
    )
    return (hidden_float + contrib).astype(jnp.bfloat16)


def solution(mesh):
    torus = Mesh(mesh.devices.reshape(mesh.shape["grp"], 4, 8), ("grp", "dev_0", "dev_1"))
    in_specs = (
        P("grp", DEV),
        P("grp", DEV),
        P("grp", DEV),
        P(DEV),
        P("grp", None),
        P("grp", None),
        P(DEV),
        P(DEV),
        P(None, DEV),
        P(GRP_DEV, None),
        P(),
        P(),
        P(GRP_DEV, None),
        P("grp", None, DEV),
        P("grp", None, DEV),
        P("grp", DEV, None),
    )
    out_specs = P(GRP_DEV, None)
    return jax.shard_map(
        shards, mesh=torus, in_specs=in_specs, out_specs=out_specs, check_vma=False
    )
```

profile of v0, /device:TPU:1, one launch (start us, length us, event | category | flops | bytes accessed | tf_op | source)
XLA Modules:
  0.0 366.3 jit_solution(13563389187455256031)
XLA Ops:
  6.6 0.9 negate_bitcast_fusion
  7.4 0.6 reduce-window.6
  8.7 0.9 copy.73
  9.7 0.8 fusion.55
  10.4 1.0 convolution_convert_fusion.2
  11.6 26.0 %all_gather.6 = bf16[16,2,8193]{2,1,0:T(2,128)(2,1)S(1)} all-gather(bf16[1,2,8193]{2,1,0:T(2,128)(2,1)S(1)} %pad_maximum_fusion), channel_id=1, replica_groups=mesh['grp'=16,'dev_0'=4,'dev_1'=8] {'grp'}, dimensions={0}, use_global_device_ids=true | all-gather | bytes 557124 | tf_op jit(solution)/shard_map/all_gather | solution.py:18
  37.6 0.7 slice.40
  38.8 0.4 reshape.245
  39.2 1.1 fusion.56
  40.3 0.5 fusion.15
  41.1 0.6 fusion.3
  42.0 18.2 %all_to_all.34 = f32[32,1,256]{2,1,0:T(1,128)S(1)} all-to-all(f32[32,1,256]{2,1,0:T(1,128)S(1)} %broadcast_in_dim.80), channel_id=1, replica_groups=mesh['grp'=16,'dev_0'=4,'dev_1'=8] {'dev_0','dev_1'}, dimensions={0} | all-to-all | bytes 65536 | tf_op jit(solution)/shard_map/all_to_all | solution.py:28
  60.5 1.6 broadcast_in_dim.81
  62.1 4.1 %all-to-all-start.1 = ((bf16[32,256,128]{1,2,0:T(8,128)(2,1)}), bf16[32,256,128]{1,2,0:T(8,128)(2,1)S(1)}, u32[]{:S(2)}, u32[]{:S(2)}) async-start(bf16[32,256,128]{1,2,0:T(8,128)(2,1)} %broadcast_in_dim.81), calls=%async_computation.1 | async-start | bytes 4194304 | tf_op jit(solution)/shard_map/all_to_all | solution.py:28
  66.9 48.6 %all-to-all-done.1 = bf16[32,256,128]{1,2,0:T(8,128)(2,1)S(1)} async-done(((bf16[32,256,128]{1,2,0:T(8,128)(2,1)}), bf16[32,256,128]{1,2,0:T(8,128)(2,1)S(1)}, u32[]{:S(2)}, u32[]{:S(2)}) %all-to-all-start.1) | async-done | bytes 2097184 | tf_op jit(solution)/shard_map/all_to_all | solution.py:28
  115.5 1.5 convolution_convert_fusion.3
  117.1 0.7 reshape.260
  117.9 6.4 %all-to-all-start.2 = ((bf16[32,2,256]{2,1,0:T(2,128)(2,1)}), bf16[32,2,256]{2,1,0:T(2,128)(2,1)S(1)}, u32[]{:S(2)}, u32[]{:S(2)}) async-start(bf16[32,2,256]{2,1,0:T(2,128)(2,1)} %reshape.260), calls=%async_computation.2 | async-start | bytes 65536 | tf_op jit(solution)/shard_map/all_to_all | solution.py:154
  124.4 8.6 %all-to-all-done.2 = bf16[32,2,256]{2,1,0:T(2,128)(2,1)S(1)} async-done(((bf16[32,2,256]{2,1,0:T(2,128)(2,1)}), bf16[32,2,256]{2,1,0:T(2,128)(2,1)S(1)}, u32[]{:S(2)}, u32[]{:S(2)}) %all-to-all-start.2) | async-done | bytes 32800 | tf_op jit(solution)/shard_map/all_to_all | solution.py:154
  133.5 0.2 convolution_convert_fusion.1
  133.8 14.9 %all_to_all.35 = bf16[16,2,2048]{2,1,0:T(2,128)(2,1)} all-to-all(bf16[16,2,2048]{2,1,0:T(2,128)(2,1)S(1)} %reshape.248), channel_id=1, replica_groups=mesh['grp'=16,'dev_0'=4,'dev_1'=8] {'grp'}, dimensions={0} | all-to-all | bytes 262144 | tf_op jit(solution)/shard_map/all_to_all | solution.py:170
  148.8 73.9 %all-gather.2.cloned.1.call-done = bf16[512,2,2048]{2,1,0:T(2,128)(2,1)} async-done(((bf16[16,2,2048]{2,1,0:T(2,128)(2,1)}), bf16[512,2,2048]{2,1,0:T(2,128)(2,1)}) %all-gather.2.cloned.1.call-update) | async-done | bytes 4194320 | tf_op jit(solution)/shard_map/all_gather | solution.py:171
  222.7 7.2 %reshape.249 = bf16[1024,2048]{1,0:T(8,128)(2,1)} reshape(bf16[512,2,2048]{2,1,0:T(2,128)(2,1)} %all-gather.2.cloned.1.call-done) | data formatting | bytes 8388608 | tf_op jit(solution)/shard_map/reshape | solution.py:171
  229.9 4.5 %fusion.8 = f32[1024,256]{1,0:T(8,128)} fusion(bf16[1024,2048]{1,0:T(8,128)(2,1)} %reshape.249, bf16[1,2048,256]{2,1,0:T(8,128)(2,1)S(1)} %copy-done.8), kind=kOutput, calls=%fused_computation.15 | convolution fusion | flops 1073741824 | bytes 6291456 | tf_op jit(solution)/shard_map/dot_general | solution.py:172
  234.4 9.1 %convolution_convert_fusion = bf16[1024,2048]{1,0:T(8,128)(2,1)} fusion(bf16[1024,2048]{1,0:T(8,128)(2,1)} %reshape.249, bf16[1,256,2048]{2,1,0:T(8,128)(2,1)S(1)} %copy-done, bf16[1,2048,256]{2,1,0:T(8,128)(2,1)} %param.30, f32[1024,256]{1,0:T(8,128)} %fusion.8), kind=kOutput, calls=%fused_computation | convolution fusion | flops 2151153664 | bytes 11534336 | tf_op jit(solution)/shard_map/dot_general | solution.py:175
  243.6 52.5 %reduce-scatter.3.cloned.1.call-done = bf16[256,2048]{1,0:T(8,128)(2,1)} async-done(((bf16[1024,2048]{1,0:T(8,128)(2,1)}), bf16[256,2048]{1,0:T(8,128)(2,1)}) %reduce-scatter.3.cloned.1.call-update) | async-done | bytes 1048592 | tf_op jit(solution)/shard_map/reduce_scatter | solution.py:51
  296.2 39.4 %reduce-scatter.5.cloned.1.call-done = bf16[32,2048]{1,0:T(8,128)(2,1)} async-done(((bf16[256,2048]{1,0:T(8,128)(2,1)}), bf16[32,2048]{1,0:T(8,128)(2,1)}) %reduce-scatter.5.cloned.1.call-update) | async-done | bytes 131088 | tf_op jit(solution)/shard_map/reduce_scatter | solution.py:51
  335.6 1.6 reshape.250
  337.2 12.5 %all-to-all-start.4 = ((bf16[16,2,2048]{2,1,0:T(2,128)(2,1)}), bf16[16,2,2048]{2,1,0:T(2,128)(2,1)S(1)}, u32[]{:S(2)}, u32[]{:S(2)}) async-start(bf16[16,2,2048]{2,1,0:T(2,128)(2,1)} %reshape.250), calls=%async_computation.6 | async-start | bytes 262144 | tf_op jit(solution)/shard_map/all_to_all | solution.py:176
  349.7 0.3 select_reduce_fusion.2
  350.1 8.8 %all-to-all-done.4 = bf16[16,2,2048]{2,1,0:T(2,128)(2,1)S(1)} async-done(((bf16[16,2,2048]{2,1,0:T(2,128)(2,1)}), bf16[16,2,2048]{2,1,0:T(2,128)(2,1)S(1)}, u32[]{:S(2)}, u32[]{:S(2)}) %all-to-all-start.4) | async-done | bytes 131104 | tf_op jit(solution)/shard_map/all_to_all | solution.py:176
  358.9 0.9 fusion
  (76 shorter events, 3.7 us)
Async XLA Ops:
  6.5 227.9 %copy-start = (bf16[1,256,2048]{2,1,0:T(8,128)(2,1)S(1)}, bf16[1,256,2048]{2,1,0:T(8,128)(2,1)}, u32[]{:S(2)}) copy-start(bf16[1,256,2048]{2,1,0:T(8,128)(2,1)} %param.31) | copy-start | bytes 3145732
  6.5 34.5 %copy-start.5 = (f32[256,2]{0,1:T(2,128)S(1)}, f32[256,2]{0,1:T(2,128)}, u32[]{:S(2)}) copy-start(f32[256,2]{0,1:T(2,128)} %param.18) | copy-start | bytes 6148
  6.5 34.3 %copy-start.2 = (bf16[256,128]{1,0:T(8,128)(2,1)S(1)}, bf16[256,128]{1,0:T(8,128)(2,1)}, u32[]{:S(2)}) copy-start(bf16[256,128]{1,0:T(8,128)(2,1)} %param.21) | copy-start | bytes 196612
  6.5 34.5 %copy-start.10 = (f32[2]{0:T(128)S(1)}, f32[2]{0:T(128)}, u32[]{:S(2)}) copy-start(f32[2]{0:T(128)} %param.22) | copy-start | bytes 28
  6.5 35.3 %copy-start.1 = (bf16[256,128]{1,0:T(8,128)(2,1)S(1)}, bf16[256,128]{1,0:T(8,128)(2,1)}, u32[]{:S(2)}) copy-start(bf16[256,128]{1,0:T(8,128)(2,1)} %param.17) | copy-start | bytes 196612
  6.5 53.7 %copy-start.7 = (f32[128]{0:T(128)S(1)}, f32[128]{0:T(128)}, u32[]{:S(2)}) copy-start(f32[128]{0:T(128)} %param.23) | copy-start | bytes 1540
  41.1 25.2 %copy-start.6 = (s32[8,2]{0,1:T(2,128)S(1)}, s32[8,2]{0,1:T(2,128)}, u32[]{:S(2)}) copy-start(s32[8,2]{0,1:T(2,128)} %param.28) | copy-start | bytes 196
  62.1 71.2 %copy-start.3 = (bf16[8,2048]{1,0:T(8,128)(2,1)S(1)}, bf16[8,2048]{1,0:T(8,128)(2,1)}, u32[]{:S(2)}) copy-start(bf16[8,2048]{1,0:T(8,128)(2,1)} %param.25) | copy-start | bytes 98308
  62.1 71.4 %copy-start.4 = (f32[2048]{0:T(1024)S(1)}, f32[2048]{0:T(1024)}, u32[]{:S(2)}) copy-start(f32[2048]{0:T(1024)} %param.26) | copy-start | bytes 24580
  62.1 53.4 %all-to-all-start.1 = ((bf16[32,256,128]{1,2,0:T(8,128)(2,1)}), bf16[32,256,128]{1,2,0:T(8,128)(2,1)S(1)}, u32[]{:S(2)}, u32[]{:S(2)}) async-start(bf16[32,256,128]{1,2,0:T(8,128)(2,1)} %broadcast_in_dim.81), calls=%async_computation.1 | async-start | bytes 4194304 | tf_op jit(solution)/shard_map/all_to_all | solution.py:28
  117.9 15.2 %all-to-all-start.2 = ((bf16[32,2,256]{2,1,0:T(2,128)(2,1)}), bf16[32,2,256]{2,1,0:T(2,128)(2,1)S(1)}, u32[]{:S(2)}, u32[]{:S(2)}) async-start(bf16[32,2,256]{2,1,0:T(2,128)(2,1)} %reshape.260), calls=%async_computation.2 | async-start | bytes 65536 | tf_op jit(solution)/shard_map/all_to_all | solution.py:154
  124.3 98.4 %all-gather.2.cloned.1.call-start = ((), (), s32[]{:S(2)}) async-start(), calls=%async_computation.7 | async-start | bytes 4325376 | tf_op jit(solution)/shard_map/all_gather | solution.py:171
  148.8 81.2 %copy-start.8 = (bf16[1,2048,256]{2,1,0:T(8,128)(2,1)S(1)}, bf16[1,2048,256]{2,1,0:T(8,128)(2,1)}, u32[]{:S(2)}) copy-start(bf16[1,2048,256]{2,1,0:T(8,128)(2,1)} %param.29) | copy-start | bytes 3145732
  148.8 147.3 %reduce-scatter.3.cloned.1.call-start = ((), (), s32[]{:S(2)}) async-start(), calls=%async_computation.8 | async-start | bytes 5242880 | tf_op jit(solution)/shard_map/reduce_scatter | solution.py:51
  243.5 106.1 %copy-start.9 = (f32[2048,16]{0,1:T(8,128)S(1)}, f32[2048,16]{0,1:T(8,128)}, u32[]{:S(2)}) copy-start(f32[2048,16]{0,1:T(8,128)} %param.27) | copy-start | bytes 393220
  243.6 92.0 %reduce-scatter.5.cloned.1.call-start = ((), (), s32[]{:S(2)}) async-start(), calls=%async_computation.9 | async-start | bytes 1179648 | tf_op jit(solution)/shard_map/reduce_scatter | solution.py:51
  337.2 21.6 %all-to-all-start.4 = ((bf16[16,2,2048]{2,1,0:T(2,128)(2,1)}), bf16[16,2,2048]{2,1,0:T(2,128)(2,1)S(1)}, u32[]{:S(2)}, u32[]{:S(2)}) async-start(bf16[16,2,2048]{2,1,0:T(2,128)(2,1)} %reshape.250), calls=%async_computation.6 | async-start | bytes 262144 | tf_op jit(solution)/shard_map/all_to_all | solution.py:176
Sparse Core Ops, SparseCore 0:
  148.9 73.7 all-gather.1
  243.7 52.3 reduce-scatter.2
  299.1 36.3 reduce-scatter.4
where the time goes:
time: 367 us; the launch traced here: 366 us
  waiting for transfers between devices  232 us (63%)
  blocking collectives  59.1 us (16%)
  starting transfers between devices  23.1 us (6%)
  matrix products  20.1 us (5%)
  local copies, waits for them, and re-layouts  15 us (4%)
  between operations  13.4 us (4%)
  other arithmetic  3.74 us (1%)
    reduce_scatter x2, waiting for transfers between devices, sum_by_axis(): total = lax.psum_scatter(total, axis, scatter_dimension=0, tiled=True)  91.8 us
    all_gather x1, waiting for transfers between devices, shards(): lax.all_gather(arrived, DEV, axis=0, tiled=True).reshape(-1, model_dim)  73.9 us
    all_to_all x1, waiting for transfers between devices, sent_to_all(): lax.all_to_all(jnp.broadcast_to(shard[None], (peers, *shard.shape)), axis...  48.6 us
    all_gather x1, blocking collectives, side_by_side(): lax.all_gather(both, axis, axis=dim, tiled=True)  26 us
    all_to_all x1, blocking collectives, sent_to_all(): lax.all_to_all(jnp.broadcast_to(shard[None], (peers, *shard.shape)), axis...  18.2 us
    all_to_all x1, blocking collectives, shards(): lax.all_to_all(outgoing, 'grp', split_axis=0, concat_axis=0, tiled=True)  14.9 us
    all_to_all x1, starting transfers between devices, shards(): lax.all_to_all(summed.astype(jnp.bfloat16).reshape(experts, slot_cap, mod...  12.5 us
    dot_general x1, matrix products, shards(): jnp.dot(hidden, down_weight[0], preferred_element_type=jnp.float32)  9.1 us
  transfers between devices with their start and end apart: 6, of which 6 were waited for; matrix products, arithmetic and copies ran while one was open for 0% of the time, Pallas kernels for 0%

commit v1 on v0

--- a/solution.py
+++ b/solution.py
@@ -47,8 +47,7 @@
 
 def sum_by_axis(terms, axes):
     total = terms.astype(jnp.bfloat16)
-    for axis in axes:
-        total = lax.psum_scatter(total, axis, scatter_dimension=0, tiled=True)
+    total = lax.psum_scatter(total, axes, scatter_dimension=0, tiled=True)
     return total.astype(jnp.float32)
 
 
@@ -144,12 +143,16 @@
     gated_out = ssm_out.reshape(tok_rows, head_count * head_width) * jax.nn.silu(
         gate_input.astype(jnp.float32)
     )
-    squares = of_everyone(jnp.sum(gated_out * gated_out, axis=1), DEV)
+    squares = lax.psum(jnp.sum(gated_out * gated_out, axis=1), DEV)
     mixed_rows = (
         gated_out * lax.rsqrt(squares[:, None] / inner_dim + EPSILON) * norm_gain[None, :]
     ).astype(jnp.bfloat16)
-    projected = jnp.dot(
-        collect(mixed_rows, DEV, 1), out_proj, preferred_element_type=jnp.float32
+    gathered = lax.all_gather(mixed_rows, DEV, axis=0)
+    projected = jnp.einsum(
+        "dtc,dcf->tf",
+        gathered,
+        out_proj.reshape(dev_count, -1, out_proj.shape[1]),
+        preferred_element_type=jnp.float32,
     ).astype(jnp.bfloat16)
     mamba_out = lax.all_to_all(projected, DEV, split_axis=0, concat_axis=1, tiled=True)
     hidden_res = (residual.astype(jnp.float32) + mamba_out.astype(jnp.float32)).astype(jnp.bfloat16)

time: 367 us -> 575 us (1.57)
  waiting for transfers between devices: 232 us -> 395 us
  blocking collectives: 59.1 us -> 110 us
    reduce_scatter x2 -> x1, waiting for transfers between devices: 91.8 us -> 222 us  [sum_by_axis(): total = lax.psum_scatter(total, axes, scatter_dimension=0, tiled=True)]
    all_gather x0 -> x1, waiting for transfers between devices: none -> 81.8 us  [shards(): gathered = lax.all_gather(mixed_rows, DEV, axis=0)]
    psum x0 -> x1, blocking collectives: none -> 61.3 us  [shards(): squares = lax.psum(jnp.sum(gated_out * gated_out, axis=1), DEV)]
    all_to_all x1 -> x0, waiting for transfers between devices: 48.6 us -> none  [sent_to_all(): lax.all_to_all(jnp.broadcast_to(shard[None], (peers, *shard.shape)), axis...]
    all_to_all x1 -> x0, blocking collectives: 18.2 us -> none  [sent_to_all(): lax.all_to_all(jnp.broadcast_to(shard[None], (peers, *shard.shape)), axis...]
    all_to_all x1, blocking collectives: 14.9 us -> 22.8 us  [shards(): lax.all_to_all(outgoing, 'grp', split_axis=0, concat_axis=0, tiled=True)]
  transfers between devices with their start and end apart: 6 -> 5, of which waited for: 6 -> 5; matrix products, arithmetic and copies ran while one was open for 0% -> 0% of each run, Pallas kernels for 0% -> 0%
where the time goes in v1:
time: 575 us
  waiting for transfers between devices  395 us (69%)
  blocking collectives  110 us (19%)
  matrix products  20.9 us (4%)
  starting transfers between devices  17.4 us (3%)
  between operations  13.4 us (2%)
  local copies, waits for them, and re-layouts  13.3 us (2%)
    reduce_scatter x1, waiting for transfers between devices, sum_by_axis(): total = lax.psum_scatter(total, axes, scatter_dimension=0, tiled=True)  222 us
    all_gather x1, waiting for transfers between devices, shards(): gathered = lax.all_gather(mixed_rows, DEV, axis=0)  81.8 us
    all_gather x1, waiting for transfers between devices, shards(): lax.all_gather(arrived, DEV, axis=0, tiled=True).reshape(-1, model_dim)  73.9 us
    psum x1, blocking collectives, shards(): squares = lax.psum(jnp.sum(gated_out * gated_out, axis=1), DEV)  61.3 us
    all_gather x1, blocking collectives, side_by_side(): lax.all_gather(both, axis, axis=dim, tiled=True)  26 us
    all_to_all x1, blocking collectives, shards(): lax.all_to_all(outgoing, 'grp', split_axis=0, concat_axis=0, tiled=True)  22.8 us
    all_to_all x1, starting transfers between devices, shards(): lax.all_to_all(summed.astype(jnp.bfloat16).reshape(experts, slot_cap, mod...  12.4 us
  transfers between devices with their start and end apart: 5, of which 5 were waited for; matrix products, arithmetic and copies ran while one was open for 0% of the time, Pallas kernels for 0%

profile of v1, /device:TPU:1, one launch (start us, length us, event | category | flops | bytes accessed | tf_op | source)
XLA Modules:
  0.0 574.6 jit_solution(1486846018110611630)
XLA Ops:
  6.6 0.9 negate_bitcast_fusion
  7.5 0.6 reduce-window.6
  8.5 0.2 slice_reduce_fusion.1
  8.8 0.8 fusion.58
  9.5 0.9 copy.61
  10.5 1.0 convolution_convert_fusion.2
  11.7 26.0 %all_gather.12 = bf16[16,2,8193]{2,1,0:T(2,128)(2,1)S(1)} all-gather(bf16[1,2,8193]{2,1,0:T(2,128)(2,1)S(1)} %pad_maximum_fusion), channel_id=1, replica_groups=mesh['grp'=16,'dev_0'=4,'dev_1'=8] {'grp'}, dimensions={0}, use_global_device_ids=true | all-gather | bytes 557124 | tf_op jit(solution)/shard_map/all_gather | solution.py:18
  37.6 0.7 slice.40
  38.9 0.4 reshape.234
  39.3 1.1 fusion.59
  40.3 0.6 fusion.18
  40.9 0.2 fusion.4
  41.2 0.6 fusion.3
  42.0 61.3 %psum.7 = f32[256]{0:T(256)S(1)} all-reduce(f32[256]{0:T(256)S(1)} %multiply_reduce_fusion), channel_id=1, replica_groups=mesh['grp'=16,'dev_0'=4,'dev_1'=8] {'dev_0','dev_1'}, use_global_device_ids=true, to_apply=%region_5.6 | all-reduce | flops 256 | bytes 2048 | tf_op jit(solution)/shard_map/psum | solution.py:146
  103.4 0.7 multiply_convert_fusion
  104.7 81.8 %all-gather.6.cloned.1.call-done = bf16[8192,128]{1,0:T(8,128)(2,1)} async-done(((bf16[256,128]{1,0:T(8,128)(2,1)}), bf16[8192,128]{1,0:T(8,128)(2,1)}) %all-gather.6.cloned.1.call-update) | async-done | bytes 2097168 | tf_op jit(solution)/shard_map/all_gather | solution.py:150
  186.6 2.3 fusion.5
  189.1 0.7 reshape.251
  189.8 4.9 all-to-all-start
  194.9 8.6 %all-to-all-done = bf16[32,2,256]{2,1,0:T(2,128)(2,1)S(1)} async-done(((bf16[32,2,256]{2,1,0:T(2,128)(2,1)}), bf16[32,2,256]{2,1,0:T(2,128)(2,1)S(1)}, u32[]{:S(2)}, u32[]{:S(2)}) %all-to-all-start) | async-done | bytes 32800 | tf_op jit(solution)/shard_map/all_to_all | solution.py:157
  203.9 0.2 convolution_convert_fusion.1
  204.3 22.8 %all_to_all.23 = bf16[16,2,2048]{2,1,0:T(2,128)(2,1)} all-to-all(bf16[16,2,2048]{2,1,0:T(2,128)(2,1)S(1)} %reshape.237), channel_id=1, replica_groups=mesh['grp'=16,'dev_0'=4,'dev_1'=8] {'grp'}, dimensions={0} | all-to-all | bytes 262144 | tf_op jit(solution)/shard_map/all_to_all | solution.py:173
  227.1 73.9 %all-gather.4.cloned.1.call-done = bf16[512,2,2048]{2,1,0:T(2,128)(2,1)} async-done(((bf16[16,2,2048]{2,1,0:T(2,128)(2,1)}), bf16[512,2,2048]{2,1,0:T(2,128)(2,1)}) %all-gather.4.cloned.1.call-update) | async-done | bytes 4194320 | tf_op jit(solution)/shard_map/all_gather | solution.py:174
  301.0 7.2 %reshape.238 = bf16[1024,2048]{1,0:T(8,128)(2,1)} reshape(bf16[512,2,2048]{2,1,0:T(2,128)(2,1)} %all-gather.4.cloned.1.call-done) | data formatting | bytes 8388608 | tf_op jit(solution)/shard_map/reshape | solution.py:174
  308.2 4.5 fusion.9
  312.8 9.1 %convolution_convert_fusion = bf16[1024,2048]{1,0:T(8,128)(2,1)} fusion(bf16[1024,2048]{1,0:T(8,128)(2,1)} %reshape.238, bf16[1,256,2048]{2,1,0:T(8,128)(2,1)S(1)} %copy-done, bf16[1,2048,256]{2,1,0:T(8,128)(2,1)} %param.30, f32[1024,256]{1,0:T(8,128)} %fusion.9), kind=kOutput, calls=%fused_computation | convolution fusion | flops 2151153664 | bytes 11534336 | tf_op jit(solution)/shard_map/dot_general | solution.py:178
  322.0 222.0 %reduce-scatter.2.cloned.1.call-done = bf16[32,2048]{1,0:T(8,128)(2,1)} async-done(((bf16[1024,2048]{1,0:T(8,128)(2,1)}), bf16[32,2048]{1,0:T(8,128)(2,1)}) %reduce-scatter.2.cloned.1.call-update) | async-done | bytes 131088 | tf_op jit(solution)/shard_map/reduce_scatter | solution.py:50
  544.0 1.7 reshape.239
  545.6 12.4 %all-to-all-start.2 = ((bf16[16,2,2048]{2,1,0:T(2,128)(2,1)}), bf16[16,2,2048]{2,1,0:T(2,128)(2,1)S(1)}, u32[]{:S(2)}, u32[]{:S(2)}) async-start(bf16[16,2,2048]{2,1,0:T(2,128)(2,1)} %reshape.239), calls=%async_computation.3 | async-start | bytes 262144 | tf_op jit(solution)/shard_map/all_to_all | solution.py:179
  558.0 0.3 select_reduce_fusion.2
  558.4 8.8 %all-to-all-done.2 = bf16[16,2,2048]{2,1,0:T(2,128)(2,1)S(1)} async-done(((bf16[16,2,2048]{2,1,0:T(2,128)(2,1)}), bf16[16,2,2048]{2,1,0:T(2,128)(2,1)S(1)}, u32[]{:S(2)}, u32[]{:S(2)}) %all-to-all-start.2) | async-done | bytes 131104 | tf_op jit(solution)/shard_map/all_to_all | solution.py:179
  567.2 0.9 fusion
  (72 shorter events, 3.0 us)
Async XLA Ops:
  6.5 306.2 %copy-start = (bf16[1,256,2048]{2,1,0:T(8,128)(2,1)S(1)}, bf16[1,256,2048]{2,1,0:T(8,128)(2,1)}, u32[]{:S(2)}) copy-start(bf16[1,256,2048]{2,1,0:T(8,128)(2,1)} %param.31) | copy-start | bytes 3145732
  6.5 34.6 %copy-start.6 = (f32[256,2]{0,1:T(2,128)S(1)}, f32[256,2]{0,1:T(2,128)}, u32[]{:S(2)}) copy-start(f32[256,2]{0,1:T(2,128)} %param.18) | copy-start | bytes 6148
  6.5 34.4 %copy-start.3 = (bf16[256,128]{1,0:T(8,128)(2,1)S(1)}, bf16[256,128]{1,0:T(8,128)(2,1)}, u32[]{:S(2)}) copy-start(bf16[256,128]{1,0:T(8,128)(2,1)} %param.21) | copy-start | bytes 196612
  6.5 34.6 %copy-start.11 = (f32[2]{0:T(128)S(1)}, f32[2]{0:T(128)}, u32[]{:S(2)}) copy-start(f32[2]{0:T(128)} %param.22) | copy-start | bytes 28
  6.5 35.3 %copy-start.2 = (bf16[256,128]{1,0:T(8,128)(2,1)S(1)}, bf16[256,128]{1,0:T(8,128)(2,1)}, u32[]{:S(2)}) copy-start(bf16[256,128]{1,0:T(8,128)(2,1)} %param.17) | copy-start | bytes 196612
  6.5 96.8 %copy-start.8 = (f32[128]{0:T(128)S(1)}, f32[128]{0:T(128)}, u32[]{:S(2)}) copy-start(f32[128]{0:T(128)} %param.23) | copy-start | bytes 1540
  6.6 97.5 %copy-start.7 = (s32[8,2]{0,1:T(2,128)S(1)}, s32[8,2]{0,1:T(2,128)}, u32[]{:S(2)}) copy-start(s32[8,2]{0,1:T(2,128)} %param.28) | copy-start | bytes 196
  6.6 180.0 %copy-start.1 = (bf16[4096,64]{0,1:T(8,128)(2,1)S(1)}, bf16[4096,64]{0,1:T(8,128)(2,1)}, u32[]{:S(2)}) copy-start(bf16[4096,64]{0,1:T(8,128)(2,1)} %param.24) | copy-start | bytes 1572868
  6.6 180.0 %all-gather.6.cloned.1.call-start = ((), (), s32[]{:S(2)}) async-start(), calls=%async_computation.6 | async-start | bytes 2162688 | tf_op jit(solution)/shard_map/all_gather | solution.py:150
  38.3 165.4 %copy-start.4 = (bf16[8,2048]{1,0:T(8,128)(2,1)S(1)}, bf16[8,2048]{1,0:T(8,128)(2,1)}, u32[]{:S(2)}) copy-start(bf16[8,2048]{1,0:T(8,128)(2,1)} %param.25) | copy-start | bytes 98308
  38.7 165.2 %copy-start.5 = (f32[2048]{0:T(1024)S(1)}, f32[2048]{0:T(1024)}, u32[]{:S(2)}) copy-start(f32[2048]{0:T(1024)} %param.26) | copy-start | bytes 24580
  189.8 13.7 %all-to-all-start = ((bf16[32,2,256]{2,1,0:T(2,128)(2,1)}), bf16[32,2,256]{2,1,0:T(2,128)(2,1)S(1)}, u32[]{:S(2)}, u32[]{:S(2)}) async-start(bf16[32,2,256]{2,1,0:T(2,128)(2,1)} %reshape.251), calls=%async_computation | async-start | bytes 65536 | tf_op jit(solution)/shard_map/all_to_all | solution.py:157
  194.7 106.3 %all-gather.4.cloned.1.call-start = ((), (), s32[]{:S(2)}) async-start(), calls=%async_computation.4 | async-start | bytes 4325376 | tf_op jit(solution)/shard_map/all_gather | solution.py:174
  227.1 81.2 %copy-start.9 = (bf16[1,2048,256]{2,1,0:T(8,128)(2,1)S(1)}, bf16[1,2048,256]{2,1,0:T(8,128)(2,1)}, u32[]{:S(2)}) copy-start(bf16[1,2048,256]{2,1,0:T(8,128)(2,1)} %param.29) | copy-start | bytes 3145732
  227.1 316.9 %reduce-scatter.2.cloned.1.call-start = ((), (), s32[]{:S(2)}) async-start(), calls=%async_computation.5 | async-start | bytes 4325376 | tf_op jit(solution)/shard_map/reduce_scatter | solution.py:50
  321.9 236.1 %copy-start.10 = (f32[2048,16]{0,1:T(8,128)S(1)}, f32[2048,16]{0,1:T(8,128)}, u32[]{:S(2)}) copy-start(f32[2048,16]{0,1:T(8,128)} %param.27) | copy-start | bytes 393220
  545.6 21.6 %all-to-all-start.2 = ((bf16[16,2,2048]{2,1,0:T(2,128)(2,1)}), bf16[16,2,2048]{2,1,0:T(2,128)(2,1)S(1)}, u32[]{:S(2)}, u32[]{:S(2)}) async-start(bf16[16,2,2048]{2,1,0:T(2,128)(2,1)} %reshape.239), calls=%async_computation.3 | async-start | bytes 262144 | tf_op jit(solution)/shard_map/all_to_all | solution.py:179
Sparse Core Ops, SparseCore 0:
  104.2 82.3 all-gather.5
  227.2 73.7 all-gather.3
  322.0 221.9 reduce-scatter.1

commit v2 on v0

--- a/solution.py
+++ b/solution.py
@@ -50,6 +50,22 @@
     for axis in axes:
         total = lax.psum_scatter(total, axis, scatter_dimension=0, tiled=True)
     return total.astype(jnp.float32)
+
+
+def ring_gather(shard, axis):
+    size = lax.axis_size(axis)
+    forward, backward, pieces = shard, shard, {0: shard}
+    for step in range(1, size // 2 + 1):
+        forward = lax.ppermute(forward, axis, [(i, (i + 1) % size) for i in range(size)])
+        pieces[-step] = forward
+        if step < size - step:
+            backward = lax.ppermute(backward, axis, [(i, (i - 1) % size) for i in range(size)])
+            pieces[step] = backward
+    offsets = list(range(-(size // 2), size - size // 2))
+    stacked = jnp.stack([pieces[o] for o in offsets])
+    doubled = jnp.concatenate([stacked, stacked])
+    start = (-offsets[0] - lax.axis_index(axis)) % size
+    return lax.dynamic_slice_in_dim(doubled, start, size, 0)
 
 
 def rms_scale(values, gain_vec):
@@ -144,14 +160,28 @@
     gated_out = ssm_out.reshape(tok_rows, head_count * head_width) * jax.nn.silu(
         gate_input.astype(jnp.float32)
     )
-    squares = of_everyone(jnp.sum(gated_out * gated_out, axis=1), DEV)
-    mixed_rows = (
-        gated_out * lax.rsqrt(squares[:, None] / inner_dim + EPSILON) * norm_gain[None, :]
+    gated_gain = gated_out * norm_gain[None, :]
+    squares = jnp.sum(gated_out * gated_out, axis=1)
+    squares_hi = squares.astype(jnp.bfloat16)
+    squares_lo = (squares - squares_hi.astype(jnp.float32)).astype(jnp.bfloat16)
+    proj_rows = lax.all_to_all(
+        out_proj.reshape(dev_count, -1, out_proj.shape[1]), DEV, 0, 0, tiled=True
+    )
+    partial = jnp.einsum(
+        "tc,scf->tsf", gated_gain, proj_rows.astype(jnp.float32), precision=HIGHEST_PREC
+    ).reshape(tok_rows, model_dim)
+    lane_pad = jnp.zeros((tok_rows, 126), jnp.bfloat16)
+    payload = jnp.concatenate(
+        [partial.astype(jnp.bfloat16), squares_hi[:, None], squares_lo[:, None], lane_pad], axis=1
+    )
+    landed = lax.all_to_all(
+        payload.reshape(dev_count, block_rows, payload.shape[1]), DEV, 0, 0, tiled=True
+    ).astype(jnp.float32)
+    summed_proj = jnp.sum(landed[:, :, :model_dim], axis=0)
+    token_squares = jnp.sum(landed[:, :, model_dim] + landed[:, :, model_dim + 1], axis=0)
+    mamba_out = (
+        summed_proj * lax.rsqrt(token_squares / inner_dim + EPSILON)[:, None]
     ).astype(jnp.bfloat16)
-    projected = jnp.dot(
-        collect(mixed_rows, DEV, 1), out_proj, preferred_element_type=jnp.float32
-    ).astype(jnp.bfloat16)
-    mamba_out = lax.all_to_all(projected, DEV, split_axis=0, concat_axis=1, tiled=True)
     hidden_res = (residual.astype(jnp.float32) + mamba_out.astype(jnp.float32)).astype(jnp.bfloat16)
     hidden_float = hidden_res.astype(jnp.float32)
     normed = rms_scale(hidden_float, ffn_gain).astype(jnp.bfloat16)
@@ -168,11 +198,15 @@
     ).astype(jnp.bfloat16)
     outgoing = outgoing.reshape(experts, slot_cap, model_dim)
     arrived = lax.all_to_all(outgoing, "grp", split_axis=0, concat_axis=0, tiled=True)
-    all_rows = lax.all_gather(arrived, DEV, axis=0, tiled=True).reshape(-1, model_dim)
+    all_rows = ring_gather(ring_gather(arrived, "dev_1"), "dev_0").reshape(-1, model_dim)
     gate_act = jnp.dot(all_rows, gate_weight[0], preferred_element_type=jnp.float32)
     up_act = jnp.dot(all_rows, up_weight[0], preferred_element_type=jnp.float32)
     hidden = (jax.nn.silu(gate_act) * up_act).astype(jnp.bfloat16)
-    summed = sum_by_axis(jnp.dot(hidden, down_weight[0], preferred_element_type=jnp.float32), DEV)
+    partial_down = jnp.dot(hidden, down_weight[0], preferred_element_type=jnp.float32)
+    spread_down = lax.all_to_all(
+        partial_down.astype(jnp.bfloat16).reshape(dev_count, -1, model_dim), DEV, 0, 0, tiled=True
+    )
+    summed = jnp.sum(spread_down.astype(jnp.float32), axis=0)
     returned = lax.all_to_all(
         summed.astype(jnp.bfloat16).reshape(experts, slot_cap, model_dim),
         "grp",

time: 367 us -> 367 us (level)
  waiting for transfers between devices: 232 us -> 172 us
  local copies, waits for them, and re-layouts: 15 us -> 61.6 us
  starting transfers between devices: 23.1 us -> 65.2 us
  blocking collectives: 59.1 us -> 41.7 us
  between operations: 13.4 us -> 0.68 us
    reduce_scatter x2 -> x0, waiting for transfers between devices: 91.8 us -> none  [sum_by_axis(): total = lax.psum_scatter(total, axis, scatter_dimension=0, tiled=True)]
    all_gather x1 -> x0, waiting for transfers between devices: 73.9 us -> none  [shards(): lax.all_gather(arrived, DEV, axis=0, tiled=True).reshape(-1, model_dim)]
    all_to_all x2 -> x3, waiting for transfers between devices: 57.3 us -> 117 us  [the longest x1 91.3 us: shards(): lax.all_to_all(partial_down.astype(jnp.bfloat16).reshape(dev_count, -1, m...]
    ppermute x0 -> x10, waiting for transfers between devices: none -> 46.4 us  [the longest x6 46.4 us: ring_gather(): lax.ppermute(forward, axis, [(i, (i + 1) % size) for i in range(size)])]
    ppermute x0 -> x10, starting transfers between devices: none -> 31.1 us  [the longest x4 18.6 us: ring_gather(): lax.ppermute(backward, axis, [(i, (i - 1) % size) for i in range(size)])]
    unnamed x28 -> x74, local copies, waits for them, and re-layouts: 2.02 us -> 27.2 us
    all_to_all x1 -> x0, blocking collectives: 18.2 us -> none  [sent_to_all(): lax.all_to_all(jnp.broadcast_to(shard[None], (peers, *shard.shape)), axis...]
    all_to_all x2 -> x3, starting transfers between devices: 10.5 us -> 24.9 us  [the longest x1 10.5 us: shards(): lax.all_to_all(out_proj.reshape(dev_count, -1, out_proj.shape[1]), DEV, 0...]
  transfers between devices with their start and end apart: 6 -> 14, of which waited for: 6 -> 9; matrix products, arithmetic and copies ran while one was open for 0% -> 5% of each run, Pallas kernels for 0% -> 0%
where the time goes in v2:
time: 367 us; the launch traced here: 366 us
  waiting for transfers between devices  172 us (47%)
  starting transfers between devices  65.2 us (18%)
  local copies, waits for them, and re-layouts  61.6 us (17%)
  blocking collectives  41.7 us (11%)
  matrix products  17.6 us (5%)
  other arithmetic  6.72 us (2%)
    all_to_all x1, waiting for transfers between devices, shards(): lax.all_to_all(partial_down.astype(jnp.bfloat16).reshape(dev_count, -1, m...  91.3 us
    ppermute x6, waiting for transfers between devices, ring_gather(): lax.ppermute(forward, axis, [(i, (i + 1) % size) for i in range(size)])  46.4 us
    unnamed x74, local copies, waits for them, and re-layouts  27.2 us
    all_to_all x1, waiting for transfers between devices, shards(): lax.all_to_all(payload.reshape(dev_count, block_rows, payload.shape[1]),...  25.5 us
    all_gather x1, blocking collectives, side_by_side(): lax.all_gather(both, axis, axis=dim, tiled=True)  25.4 us
    ppermute x4, starting transfers between devices, ring_gather(): lax.ppermute(backward, axis, [(i, (i - 1) % size) for i in range(size)])  18.6 us
    all_to_all x1, blocking collectives, shards(): lax.all_to_all(outgoing, 'grp', split_axis=0, concat_axis=0, tiled=True)  16.3 us
    ppermute x6, starting transfers between devices, ring_gather(): lax.ppermute(forward, axis, [(i, (i + 1) % size) for i in range(size)])  12.5 us
  transfers between devices with their start and end apart: 14, of which 9 were waited for; matrix products, arithmetic and copies ran while one was open for 5% of the time, Pallas kernels for 0%

profile of v2, /device:TPU:1, one launch (start us, length us, event | category | flops | bytes accessed | tf_op | source)
XLA Modules:
  0.0 365.7 jit_solution(16350380280948654589)
XLA Ops:
  0.0 2.1 copy_bitcast_fusion
  2.1 10.5 %all-to-all-start = ((bf16[32,128,64]{1,2,0:T(8,128)(2,1)}), bf16[32,128,64]{1,2,0:T(8,128)(2,1)S(1)}, u32[]{:S(2)}, u32[]{:S(2)}) async-start(bf16[32,128,64]{1,2,0:T(8,128)(2,1)} %copy_bitcast_fusion), calls=%async_computation | async-start | bytes 1048576 | tf_op jit(solution)/shard_map/all_to_all | solution.py:167
  14.6 25.4 %all_gather.3 = bf16[16,2,8193]{2,1,0:T(2,128)(2,1)S(1)} all-gather(bf16[1,2,8193]{2,1,0:T(2,128)(2,1)S(1)} %pad_maximum_fusion), channel_id=1, replica_groups=mesh['grp'=16,'dev_0'=4,'dev_1'=8] {'grp'}, dimensions={0}, use_global_device_ids=true | all-gather | bytes 557124 | tf_op jit(solution)/shard_map/all_gather | solution.py:18
  46.1 3.9 %copy.69 = bf16[256,32,64]{2,1,0:T(8,128)(2,1)S(1)} copy(bf16[256,32,64]{0,2,1:T(8,128)(2,1)} %convert_element_type.136) | data formatting | bytes 2097152 | tf_op jit(solution)/shard_map/convert_element_type | solution.py:175
  50.0 2.4 convert_element_type.137
  52.5 3.0 concatenate.16
  55.5 9.5 %all-to-all-start.1 = ((bf16[32,8,2176]{2,1,0:T(8,128)(2,1)}), bf16[32,8,2176]{2,1,0:T(8,128)(2,1)S(1)}, u32[]{:S(2)}, u32[]{:S(2)}) async-start(bf16[32,8,2176]{2,1,0:T(8,128)(2,1)} %concatenate.16), calls=%async_computation.1 | async-start | bytes 2228224 | tf_op jit(solution)/shard_map/all_to_all | solution.py:177
  65.8 25.5 %all-to-all-done.1 = bf16[32,8,2176]{2,1,0:T(8,128)(2,1)S(1)} async-done(((bf16[32,8,2176]{2,1,0:T(8,128)(2,1)}), bf16[32,8,2176]{2,1,0:T(8,128)(2,1)S(1)}, u32[]{:S(2)}, u32[]{:S(2)}) %all-to-all-start.1) | async-done | bytes 1114144 | tf_op jit(solution)/shard_map/all_to_all | solution.py:177
  93.0 16.3 %all_to_all.25 = bf16[16,2,2048]{2,1,0:T(2,128)(2,1)S(1)} all-to-all(bf16[16,2,2048]{2,1,0:T(2,128)(2,1)S(1)} %reshape.276), channel_id=1, replica_groups=mesh['grp'=16,'dev_0'=4,'dev_1'=8] {'grp'}, dimensions={0} | all-to-all | bytes 262144 | tf_op jit(solution)/shard_map/all_to_all | solution.py:200
  109.3 3.0 collective-permute-start
  112.3 5.5 %collective-permute-done = bf16[16,2,2048]{2,1,0:T(2,128)(2,1)S(1)} collective-permute-done((bf16[16,2,2048]{2,1,0:T(2,128)(2,1)S(1)}, bf16[16,2,2048]{2,1,0:T(2,128)(2,1)S(1)}, u32[]{:S(2)}, u32[]{:S(2)}) %collective-permute-start) | collective-permute-done | bytes 131104 | tf_op jit(solution)/shard_map/ppermute | solution.py:59
  119.7 4.6 %collective-permute-start.4 = (bf16[16,2,2048]{2,1,0:T(2,128)(2,1)S(1)}, bf16[16,2,2048]{2,1,0:T(2,128)(2,1)S(1)}, u32[]{:S(2)}, u32[]{:S(2)}) collective-permute-start(bf16[16,2,2048]{2,1,0:T(2,128)(2,1)S(1)} %all_to_all.25), channel_id=1, source_target_pairs={{0,7},{1,0},{2,1},{3,2},{4,3},{5,4},{6,5},{7,6},{8,15},{9,8},{10,9... | collective-permute-start | bytes 393224 | tf_op jit(solution)/shard_map/ppermute | solution.py:62
  127.4 4.6 %collective-permute-start.5 = (bf16[16,2,2048]{2,1,0:T(2,128)(2,1)S(1)}, bf16[16,2,2048]{2,1,0:T(2,128)(2,1)}, u32[]{:S(2)}, u32[]{:S(2)}) collective-permute-start(bf16[16,2,2048]{2,1,0:T(2,128)(2,1)S(1)} %collective-permute-done.4), channel_id=1, source_target_pairs={{0,7},{1,0},{2,1},{3,2},{4,3},{5,4},{6,5},{7,6},{8,15},{9,8},{10,9... | collective-permute-start | bytes 393224 | tf_op jit(solution)/shard_map/ppermute | solution.py:62
  134.3 4.8 %collective-permute-start.6 = (bf16[16,2,2048]{2,1,0:T(2,128)(2,1)}, bf16[16,2,2048]{2,1,0:T(2,128)(2,1)S(1)}, u32[]{:S(2)}, u32[]{:S(2)}) collective-permute-start(bf16[16,2,2048]{2,1,0:T(2,128)(2,1)} %collective-permute-done.5), channel_id=1, source_target_pairs={{0,7},{1,0},{2,1},{3,2},{4,3},{5,4},{6,5},{7,6},{8,15},{9,8},{10,9... | collective-permute-start | bytes 393224 | tf_op jit(solution)/shard_map/ppermute | solution.py:62
  150.5 22.3 %collective-permute-done.7 = bf16[8,16,2,2048]{3,2,1,0:T(2,128)(2,1)} collective-permute-done((bf16[8,16,2,2048]{3,2,1,0:T(2,128)(2,1)S(1)}, bf16[8,16,2,2048]{3,2,1,0:T(2,128)(2,1)}, u32[]{:S(2)}, u32[]{:S(2)}) %collective-permute-start.7) | collective-permute-done | bytes 1048608 | tf_op jit(solution)/shard_map/ppermute | solution.py:59
  174.7 4.6 %collective-permute-start.9 = (bf16[8,16,2,2048]{3,2,1,0:T(2,128)(2,1)}, bf16[8,16,2,2048]{3,2,1,0:T(2,128)(2,1)S(1)}, u32[]{:S(2)}, u32[]{:S(2)}) collective-permute-start(bf16[8,16,2,2048]{3,2,1,0:T(2,128)(2,1)} %copy-done.1), channel_id=1, source_target_pairs={{0,24},{8,0},{16,8},{24,16},{1,25},{9,1},{17,9},{25,17},{2,26},{10... | collective-permute-start | bytes 3145736 | tf_op jit(solution)/shard_map/ppermute | solution.py:62
  179.3 16.9 %collective-permute-done.8 = bf16[8,16,2,2048]{3,2,1,0:T(2,128)(2,1)} collective-permute-done((bf16[8,16,2,2048]{3,2,1,0:T(2,128)(2,1)}, bf16[8,16,2,2048]{3,2,1,0:T(2,128)(2,1)}, u32[]{:S(2)}, u32[]{:S(2)}) %collective-permute-start.8) | collective-permute-done | bytes 1048608 | tf_op jit(solution)/shard_map/ppermute | solution.py:59
  196.2 3.0 bitcast_dynamic-update-slice_fusion.6
  199.2 3.1 bitcast_dynamic-update-slice_fusion.4
  206.4 3.0 bitcast_dynamic-update-slice_fusion.7
  209.4 3.1 bitcast_dynamic-update-slice_fusion.5
  212.5 2.0 bitcast_dynamic-update-slice_fusion.3
  214.5 2.0 bitcast_dynamic-update-slice_fusion.1
  216.5 9.1 %constant_dynamic-slice_fusion.1 = bf16[4,8,16,2,2048]{4,3,2,1,0:T(2,128)(2,1)} fusion(bf16[8,8,16,2,2048]{4,3,2,1,0:T(2,128)(2,1)} %bitcast_dynamic-update-slice_fusion.1, s32[]{:T(128)S(6)} %select_n.42), kind=kLoop, calls=%fused_computation.120 | loop fusion | bytes 8388612 | tf_op jit(solution)/shard_map/dynamic_slice | solution.py:68
  225.6 7.3 %reshape.277 = bf16[1024,2048]{1,0:T(8,128)(2,1)} reshape(bf16[4,8,16,2,2048]{4,3,2,1,0:T(2,128)(2,1)} %constant_dynamic-slice_fusion.1) | data formatting | bytes 8388608 | tf_op jit(solution)/shard_map/reshape | solution.py:201
  232.9 4.6 %fusion.8 = f32[1024,256]{1,0:T(8,128)} fusion(bf16[1024,2048]{1,0:T(8,128)(2,1)} %reshape.277, bf16[1,2048,256]{2,1,0:T(8,128)(2,1)S(1)} %copy-done.20), kind=kOutput, calls=%fused_computation.15 | convolution fusion | flops 1073741824 | bytes 6291456 | tf_op jit(solution)/shard_map/dot_general | solution.py:202
  237.5 8.8 %convolution_convert_fusion = bf16[1024,2048]{1,0:T(8,128)(2,1)} fusion(bf16[1024,2048]{1,0:T(8,128)(2,1)} %reshape.277, bf16[1,256,2048]{2,1,0:T(8,128)(2,1)S(1)} %copy-done, bf16[1,2048,256]{2,1,0:T(8,128)(2,1)S(1)} %copy-done.21, f32[1024,256]{1,0:T(8,128)} %fusion.8), kind=kOutput, calls=%fused_computation | convolution fusion | flops 2151153664 | bytes 11534336 | tf_op jit(solution)/shard_map/dot_general | solution.py:205
  246.3 4.8 %all-to-all-start.3 = ((bf16[32,32,2048]{2,1,0:T(8,128)(2,1)}), bf16[32,32,2048]{2,1,0:T(8,128)(2,1)}, u32[]{:S(2)}, u32[]{:S(2)}) async-start(bf16[32,32,2048]{2,1,0:T(8,128)(2,1)} %bitcast.121), calls=%async_computation.3 | async-start | bytes 8388608 | tf_op jit(solution)/shard_map/all_to_all | solution.py:206
  251.2 91.3 %all-to-all-done.3 = bf16[32,32,2048]{2,1,0:T(8,128)(2,1)} async-done(((bf16[32,32,2048]{2,1,0:T(8,128)(2,1)}), bf16[32,32,2048]{2,1,0:T(8,128)(2,1)}, u32[]{:S(2)}, u32[]{:S(2)}) %all-to-all-start.3) | async-done | bytes 4194336 | tf_op jit(solution)/shard_map/all_to_all | solution.py:206
  342.6 3.0 reduce_sum.108
  346.3 9.3 %all-to-all-start.4 = ((bf16[16,2,2048]{2,1,0:T(2,128)(2,1)}), bf16[16,2,2048]{2,1,0:T(2,128)(2,1)S(1)}, u32[]{:S(2)}, u32[]{:S(2)}) async-start(bf16[16,2,2048]{2,1,0:T(2,128)(2,1)} %reshape.279), calls=%async_computation.4 | async-start | bytes 262144 | tf_op jit(solution)/shard_map/all_to_all | solution.py:210
  356.0 8.8 %all-to-all-done.4 = bf16[16,2,2048]{2,1,0:T(2,128)(2,1)S(1)} async-done(((bf16[16,2,2048]{2,1,0:T(2,128)(2,1)}), bf16[16,2,2048]{2,1,0:T(2,128)(2,1)S(1)}, u32[]{:S(2)}, u32[]{:S(2)}) %all-to-all-start.4) | async-done | bytes 131104 | tf_op jit(solution)/shard_map/all_to_all | solution.py:210
  (144 shorter events, 36.8 us)
Async XLA Ops:
  0.0 237.5 %copy-start = (bf16[1,256,2048]{2,1,0:T(8,128)(2,1)S(1)}, bf16[1,256,2048]{2,1,0:T(8,128)(2,1)}, u32[]{:S(2)}) copy-start(bf16[1,256,2048]{2,1,0:T(8,128)(2,1)} %param.31) | copy-start | bytes 3145732
  0.0 12.6 %copy-start.14 = (f32[256,2]{0,1:T(2,128)S(1)}, f32[256,2]{0,1:T(2,128)}, u32[]{:S(2)}) copy-start(f32[256,2]{0,1:T(2,128)} %param.18) | copy-start | bytes 6148
  0.0 12.6 %copy-start.19 = (f32[2]{0:T(128)S(1)}, f32[2]{0:T(128)}, u32[]{:S(2)}) copy-start(f32[2]{0:T(128)} %param.19) | copy-start | bytes 28
  0.0 14.1 %copy-start.11 = (bf16[256,128]{1,0:T(8,128)(2,1)S(1)}, bf16[256,128]{1,0:T(8,128)(2,1)}, u32[]{:S(2)}) copy-start(bf16[256,128]{1,0:T(8,128)(2,1)} %param.16) | copy-start | bytes 196612
  0.0 14.2 %copy-start.7 = (bf16[256,128]{1,0:T(8,128)(2,1)S(1)}, bf16[256,128]{1,0:T(8,128)(2,1)}, u32[]{:S(2)}) copy-start(bf16[256,128]{1,0:T(8,128)(2,1)} %param.20) | copy-start | bytes 196612
  2.1 41.9 %all-to-all-start = ((bf16[32,128,64]{1,2,0:T(8,128)(2,1)}), bf16[32,128,64]{1,2,0:T(8,128)(2,1)S(1)}, u32[]{:S(2)}, u32[]{:S(2)}) async-start(bf16[32,128,64]{1,2,0:T(8,128)(2,1)} %copy_bitcast_fusion), calls=%async_computation | async-start | bytes 1048576 | tf_op jit(solution)/shard_map/all_to_all | solution.py:167
  12.6 29.6 %copy-start.8 = (bf16[256,128]{1,0:T(8,128)(2,1)S(1)}, bf16[256,128]{1,0:T(8,128)(2,1)}, u32[]{:S(2)}) copy-start(bf16[256,128]{1,0:T(8,128)(2,1)} %param.21) | copy-start | bytes 196612
  14.4 28.2 %copy-start.23 = (f32[2]{0:T(128)S(1)}, f32[2]{0:T(128)}, u32[]{:S(2)}) copy-start(f32[2]{0:T(128)} %param.22) | copy-start | bytes 28
  41.2 2.8 copy-start.16
  52.5 12.6 %copy-start.15 = (s32[8,2]{0,1:T(2,128)S(1)}, s32[8,2]{0,1:T(2,128)}, u32[]{:S(2)}) copy-start(s32[8,2]{0,1:T(2,128)} %param.28) | copy-start | bytes 196
  55.5 35.8 %all-to-all-start.1 = ((bf16[32,8,2176]{2,1,0:T(8,128)(2,1)}), bf16[32,8,2176]{2,1,0:T(8,128)(2,1)S(1)}, u32[]{:S(2)}, u32[]{:S(2)}) async-start(bf16[32,8,2176]{2,1,0:T(8,128)(2,1)} %concatenate.16), calls=%async_computation.1 | async-start | bytes 2228224 | tf_op jit(solution)/shard_map/all_to_all | solution.py:177
  65.8 26.1 %copy-start.12 = (bf16[8,2048]{1,0:T(8,128)(2,1)S(1)}, bf16[8,2048]{1,0:T(8,128)(2,1)}, u32[]{:S(2)}) copy-start(bf16[8,2048]{1,0:T(8,128)(2,1)} %param.25) | copy-start | bytes 98308
  109.3 8.5 %collective-permute-start = (bf16[16,2,2048]{2,1,0:T(2,128)(2,1)S(1)}, bf16[16,2,2048]{2,1,0:T(2,128)(2,1)S(1)}, u32[]{:S(2)}, u32[]{:S(2)}) collective-permute-start(bf16[16,2,2048]{2,1,0:T(2,128)(2,1)S(1)} %all_to_all.25), channel_id=1, source_target_pairs={{0,1},{1,2},{2,3},{3,4},{4,5},{5,6},{6,7},{7,0},{8,9},{9,10},{10,1... | collective-permute-start | bytes 393224 | tf_op jit(solution)/shard_map/ppermute | solution.py:59
  117.8 7.6 %collective-permute-start.1 = (bf16[16,2,2048]{2,1,0:T(2,128)(2,1)S(1)}, bf16[16,2,2048]{2,1,0:T(2,128)(2,1)S(1)}, u32[]{:S(2)}, u32[]{:S(2)}) collective-permute-start(bf16[16,2,2048]{2,1,0:T(2,128)(2,1)S(1)} %collective-permute-done), channel_id=1, source_target_pairs={{0,1},{1,2},{2,3},{3,4},{4,5},{5,6},{6,7},{7,0},{8,9},{9,10},{10,1... | collective-permute-start | bytes 393224 | tf_op jit(solution)/shard_map/ppermute | solution.py:59
  119.7 7.6 %collective-permute-start.4 = (bf16[16,2,2048]{2,1,0:T(2,128)(2,1)S(1)}, bf16[16,2,2048]{2,1,0:T(2,128)(2,1)S(1)}, u32[]{:S(2)}, u32[]{:S(2)}) collective-permute-start(bf16[16,2,2048]{2,1,0:T(2,128)(2,1)S(1)} %all_to_all.25), channel_id=1, source_target_pairs={{0,7},{1,0},{2,1},{3,2},{4,3},{5,4},{6,5},{7,6},{8,15},{9,8},{10,9... | collective-permute-start | bytes 393224 | tf_op jit(solution)/shard_map/ppermute | solution.py:62
  125.4 6.9 %collective-permute-start.2 = (bf16[16,2,2048]{2,1,0:T(2,128)(2,1)S(1)}, bf16[16,2,2048]{2,1,0:T(2,128)(2,1)S(1)}, u32[]{:S(2)}, u32[]{:S(2)}) collective-permute-start(bf16[16,2,2048]{2,1,0:T(2,128)(2,1)S(1)} %collective-permute-done.1), channel_id=1, source_target_pairs={{0,1},{1,2},{2,3},{3,4},{4,5},{5,6},{6,7},{7,0},{8,9},{9,10},{10,1... | collective-permute-start | bytes 393224 | tf_op jit(solution)/shard_map/ppermute | solution.py:59
  127.4 6.9 %collective-permute-start.5 = (bf16[16,2,2048]{2,1,0:T(2,128)(2,1)S(1)}, bf16[16,2,2048]{2,1,0:T(2,128)(2,1)}, u32[]{:S(2)}, u32[]{:S(2)}) collective-permute-start(bf16[16,2,2048]{2,1,0:T(2,128)(2,1)S(1)} %collective-permute-done.4), channel_id=1, source_target_pairs={{0,7},{1,0},{2,1},{3,2},{4,3},{5,4},{6,5},{7,6},{8,15},{9,8},{10,9... | collective-permute-start | bytes 393224 | tf_op jit(solution)/shard_map/ppermute | solution.py:62
  132.4 6.8 %copy-start.4 = (bf16[16,2,2048]{2,1,0:T(2,128)(2,1)}, bf16[16,2,2048]{2,1,0:T(2,128)(2,1)S(1)}, u32[]{:S(2)}) copy-start(bf16[16,2,2048]{2,1,0:T(2,128)(2,1)S(1)} %collective-permute-done.2) | copy-start | bytes 393220
  132.4 7.0 %collective-permute-start.3 = (bf16[16,2,2048]{2,1,0:T(2,128)(2,1)S(1)}, bf16[16,2,2048]{2,1,0:T(2,128)(2,1)}, u32[]{:S(2)}, u32[]{:S(2)}) collective-permute-start(bf16[16,2,2048]{2,1,0:T(2,128)(2,1)S(1)} %collective-permute-done.2), channel_id=1, source_target_pairs={{0,1},{1,2},{2,3},{3,4},{4,5},{5,6},{6,7},{7,0},{8,9},{9,10},{10,1... | collective-permute-start | bytes 393224 | tf_op jit(solution)/shard_map/ppermute | solution.py:59
  134.3 10.7 %copy-start.3 = (bf16[16,2,2048]{2,1,0:T(2,128)(2,1)S(1)}, bf16[16,2,2048]{2,1,0:T(2,128)(2,1)}, u32[]{:S(2)}) copy-start(bf16[16,2,2048]{2,1,0:T(2,128)(2,1)} %copy-done.2) | copy-start | bytes 393220
  134.3 9.4 %collective-permute-start.6 = (bf16[16,2,2048]{2,1,0:T(2,128)(2,1)}, bf16[16,2,2048]{2,1,0:T(2,128)(2,1)S(1)}, u32[]{:S(2)}, u32[]{:S(2)}) collective-permute-start(bf16[16,2,2048]{2,1,0:T(2,128)(2,1)} %collective-permute-done.5), channel_id=1, source_target_pairs={{0,7},{1,0},{2,1},{3,2},{4,3},{5,4},{6,5},{7,6},{8,15},{9,8},{10,9... | collective-permute-start | bytes 393224 | tf_op jit(solution)/shard_map/ppermute | solution.py:62
  139.4 5.5 %copy-start.5 = (bf16[16,2,2048]{2,1,0:T(2,128)(2,1)S(1)}, bf16[16,2,2048]{2,1,0:T(2,128)(2,1)}, u32[]{:S(2)}) copy-start(bf16[16,2,2048]{2,1,0:T(2,128)(2,1)} %copy-done.4) | copy-start | bytes 393220
  148.6 24.2 %collective-permute-start.7 = (bf16[8,16,2,2048]{3,2,1,0:T(2,128)(2,1)S(1)}, bf16[8,16,2,2048]{3,2,1,0:T(2,128)(2,1)}, u32[]{:S(2)}, u32[]{:S(2)}) collective-permute-start(bf16[8,16,2,2048]{3,2,1,0:T(2,128)(2,1)S(1)} %constant_dynamic-slice_fusion), channel_id=1, source_target_pairs={{0,8},{8,16},{16,24},{24,0},{1,9},{9,17},{17,25},{25,1},{2,10},{10... | collective-permute-start | bytes 3145736 | tf_op jit(solution)/shard_map/ppermute | solution.py:59
  172.7 23.5 %collective-permute-start.8 = (bf16[8,16,2,2048]{3,2,1,0:T(2,128)(2,1)}, bf16[8,16,2,2048]{3,2,1,0:T(2,128)(2,1)}, u32[]{:S(2)}, u32[]{:S(2)}) collective-permute-start(bf16[8,16,2,2048]{3,2,1,0:T(2,128)(2,1)} %collective-permute-done.7), channel_id=1, source_target_pairs={{0,8},{8,16},{16,24},{24,0},{1,9},{9,17},{17,25},{25,1},{2,10},{10... | collective-permute-start | bytes 3145736 | tf_op jit(solution)/shard_map/ppermute | solution.py:59
  174.7 29.7 %collective-permute-start.9 = (bf16[8,16,2,2048]{3,2,1,0:T(2,128)(2,1)}, bf16[8,16,2,2048]{3,2,1,0:T(2,128)(2,1)S(1)}, u32[]{:S(2)}, u32[]{:S(2)}) collective-permute-start(bf16[8,16,2,2048]{3,2,1,0:T(2,128)(2,1)} %copy-done.1), channel_id=1, source_target_pairs={{0,24},{8,0},{16,8},{24,16},{1,25},{9,1},{17,9},{25,17},{2,26},{10... | collective-permute-start | bytes 3145736 | tf_op jit(solution)/shard_map/ppermute | solution.py:62
  225.6 7.3 %copy-start.20 = (bf16[1,2048,256]{2,1,0:T(8,128)(2,1)S(1)}, bf16[1,2048,256]{2,1,0:T(8,128)(2,1)}, u32[]{:S(2)}) copy-start(bf16[1,2048,256]{2,1,0:T(8,128)(2,1)} %param.29) | copy-start | bytes 3145732
  232.9 4.6 %copy-start.21 = (bf16[1,2048,256]{2,1,0:T(8,128)(2,1)S(1)}, bf16[1,2048,256]{2,1,0:T(8,128)(2,1)}, u32[]{:S(2)}) copy-start(bf16[1,2048,256]{2,1,0:T(8,128)(2,1)} %param.30) | copy-start | bytes 3145732
  246.3 96.3 %all-to-all-start.3 = ((bf16[32,32,2048]{2,1,0:T(8,128)(2,1)}), bf16[32,32,2048]{2,1,0:T(8,128)(2,1)}, u32[]{:S(2)}, u32[]{:S(2)}) async-start(bf16[32,32,2048]{2,1,0:T(8,128)(2,1)} %bitcast.121), calls=%async_computation.3 | async-start | bytes 8388608 | tf_op jit(solution)/shard_map/all_to_all | solution.py:206
  251.2 104.3 %copy-start.10 = (bf16[8,2048]{1,0:T(8,128)(2,1)S(1)}, bf16[8,2048]{1,0:T(8,128)(2,1)}, u32[]{:S(2)}) copy-start(bf16[8,2048]{1,0:T(8,128)(2,1)} %copy-done.9) | copy-start | bytes 98308
  251.2 104.3 %copy-start.18 = (f32[8]{0:T(128)S(1)}, f32[8]{0:T(128)}, u32[]{:S(2)}) copy-start(f32[8]{0:T(128)} %copy-done.17) | copy-start | bytes 100
  251.2 104.4 %copy-start.22 = (f32[2048,16]{0,1:T(8,128)S(1)}, f32[2048,16]{0,1:T(8,128)}, u32[]{:S(2)}) copy-start(f32[2048,16]{0,1:T(8,128)} %param.27) | copy-start | bytes 393220
  346.3 18.5 %all-to-all-start.4 = ((bf16[16,2,2048]{2,1,0:T(2,128)(2,1)}), bf16[16,2,2048]{2,1,0:T(2,128)(2,1)S(1)}, u32[]{:S(2)}, u32[]{:S(2)}) async-start(bf16[16,2,2048]{2,1,0:T(2,128)(2,1)} %reshape.279), calls=%async_computation.4 | async-start | bytes 262144 | tf_op jit(solution)/shard_map/all_to_all | solution.py:210
  (6 other events, 8.0 us)

commit v3 on v2

--- a/solution.py
+++ b/solution.py
@@ -161,24 +161,31 @@
         gate_input.astype(jnp.float32)
     )
     gated_gain = gated_out * norm_gain[None, :]
-    squares = jnp.sum(gated_out * gated_out, axis=1)
-    squares_hi = squares.astype(jnp.bfloat16)
-    squares_lo = (squares - squares_hi.astype(jnp.float32)).astype(jnp.bfloat16)
+    squares = gated_out * gated_out
     proj_rows = lax.all_to_all(
         out_proj.reshape(dev_count, -1, out_proj.shape[1]), DEV, 0, 0, tiled=True
     )
-    partial = jnp.einsum(
-        "tc,scf->tsf", gated_gain, proj_rows.astype(jnp.float32), precision=HIGHEST_PREC
-    ).reshape(tok_rows, model_dim)
-    lane_pad = jnp.zeros((tok_rows, 126), jnp.bfloat16)
-    payload = jnp.concatenate(
-        [partial.astype(jnp.bfloat16), squares_hi[:, None], squares_lo[:, None], lane_pad], axis=1
-    )
+    chan = proj_rows.shape[1]
+    proj_rows = jnp.transpose(proj_rows, (1, 0, 2)).reshape(chan, model_dim)
+    lane_pad = 128
+    square_cols = (jnp.arange(lane_pad) == 0).astype(jnp.bfloat16)
+    rhs = jnp.concatenate(
+        [
+            jnp.concatenate([proj_rows, jnp.zeros((chan, lane_pad), jnp.bfloat16)], axis=1),
+            jnp.concatenate(
+                [jnp.zeros((chan, model_dim), jnp.bfloat16), jnp.broadcast_to(square_cols, (chan, lane_pad))],
+                axis=1,
+            ),
+        ],
+        axis=0,
+    )
+    lhs = jnp.concatenate([gated_gain, squares], axis=1).astype(jnp.bfloat16)
+    payload = jnp.dot(lhs, rhs, preferred_element_type=jnp.float32).astype(jnp.bfloat16)
     landed = lax.all_to_all(
         payload.reshape(dev_count, block_rows, payload.shape[1]), DEV, 0, 0, tiled=True
     ).astype(jnp.float32)
     summed_proj = jnp.sum(landed[:, :, :model_dim], axis=0)
-    token_squares = jnp.sum(landed[:, :, model_dim] + landed[:, :, model_dim + 1], axis=0)
+    token_squares = jnp.sum(landed[:, :, model_dim], axis=0)
     mamba_out = (
         summed_proj * lax.rsqrt(token_squares / inner_dim + EPSILON)[:, None]
     ).astype(jnp.bfloat16)
@@ -198,15 +205,17 @@
     ).astype(jnp.bfloat16)
     outgoing = outgoing.reshape(experts, slot_cap, model_dim)
     arrived = lax.all_to_all(outgoing, "grp", split_axis=0, concat_axis=0, tiled=True)
-    all_rows = ring_gather(ring_gather(arrived, "dev_1"), "dev_0").reshape(-1, model_dim)
+    all_rows = arrived.reshape(-1, model_dim)
+    all_rows = lax.all_gather(all_rows, "dev_0", axis=0, tiled=True)
+    all_rows = lax.all_gather(all_rows, "dev_1", axis=0, tiled=True)
     gate_act = jnp.dot(all_rows, gate_weight[0], preferred_element_type=jnp.float32)
     up_act = jnp.dot(all_rows, up_weight[0], preferred_element_type=jnp.float32)
     hidden = (jax.nn.silu(gate_act) * up_act).astype(jnp.bfloat16)
     partial_down = jnp.dot(hidden, down_weight[0], preferred_element_type=jnp.float32)
-    spread_down = lax.all_to_all(
-        partial_down.astype(jnp.bfloat16).reshape(dev_count, -1, model_dim), DEV, 0, 0, tiled=True
-    )
-    summed = jnp.sum(spread_down.astype(jnp.float32), axis=0)
+    summed = lax.psum_scatter(
+        partial_down.astype(jnp.bfloat16), "dev_1", scatter_dimension=0, tiled=True
+    )
+    summed = lax.psum_scatter(summed, "dev_0", scatter_dimension=0, tiled=True)
     returned = lax.all_to_all(
         summed.astype(jnp.bfloat16).reshape(experts, slot_cap, model_dim),
         "grp",

time: 367 us -> 295 us (0.80)
  local copies, waits for them, and re-layouts: 61.6 us -> 7.49 us
  starting transfers between devices: 65.2 us -> 30 us
  between operations: 0.68 us -> 13.4 us
  blocking collectives: 41.7 us -> 53.6 us
    all_to_all x1 -> x0, waiting for transfers between devices: 91.3 us -> none  [shards(): lax.all_to_all(partial_down.astype(jnp.bfloat16).reshape(dev_count, -1, m...]
    reduce_scatter x0 -> x2, waiting for transfers between devices: none -> 83.7 us  [the longest x1 56.8 us: shards(): lax.psum_scatter(partial_down.astype(jnp.bfloat16), 'dev_1', scatter_dime...]
    all_gather x0 -> x1, waiting for transfers between devices: none -> 51 us  [shards(): all_rows = lax.all_gather(all_rows, 'dev_1', axis=0, tiled=True)]
    ppermute x10 -> x0, waiting for transfers between devices: 46.4 us -> none  [the longest x6 46.4 us: ring_gather(): lax.ppermute(forward, axis, [(i, (i + 1) % size) for i in range(size)])]
    ppermute x10 -> x0, starting transfers between devices: 31.1 us -> none  [the longest x4 18.6 us: ring_gather(): lax.ppermute(backward, axis, [(i, (i - 1) % size) for i in range(size)])]
    unnamed x74 -> x30, local copies, waits for them, and re-layouts: 27.2 us -> 1.2 us
    all_gather x0 -> x1, blocking collectives: none -> 11.8 us  [shards(): all_rows = lax.all_gather(all_rows, 'dev_0', axis=0, tiled=True)]
    dynamic_slice x2 -> x0, local copies, waits for them, and re-layouts: 10.1 us -> none  [ring_gather(): return lax.dynamic_slice_in_dim(doubled, start, size, 0)]
  transfers between devices with their start and end apart: 14 -> 6, of which waited for: 9 -> 5; matrix products, arithmetic and copies ran while one was open for 5% -> 3% of each run, Pallas kernels for 0% -> 0%
where the time goes in v3:
time: 295 us
  waiting for transfers between devices  169 us (57%)
  blocking collectives  53.6 us (18%)
  starting transfers between devices  30 us (10%)
  matrix products  18.1 us (6%)
  between operations  13.4 us (5%)
  local copies, waits for them, and re-layouts  7.49 us (3%)
  other arithmetic  3.2 us (1%)
    reduce_scatter x1, waiting for transfers between devices, shards(): lax.psum_scatter(partial_down.astype(jnp.bfloat16), 'dev_1', scatter_dime...  56.8 us
    all_gather x1, waiting for transfers between devices, shards(): all_rows = lax.all_gather(all_rows, 'dev_1', axis=0, tiled=True)  51 us
    reduce_scatter x1, waiting for transfers between devices, shards(): summed = lax.psum_scatter(summed, 'dev_0', scatter_dimension=0, tiled=True)  26.9 us
    all_to_all x1, waiting for transfers between devices, shards(): lax.all_to_all(payload.reshape(dev_count, block_rows, payload.shape[1]),...  25.5 us
    all_gather x1, blocking collectives, side_by_side(): lax.all_gather(both, axis, axis=dim, tiled=True)  25.4 us
    all_to_all x1, blocking collectives, shards(): lax.all_to_all(outgoing, 'grp', split_axis=0, concat_axis=0, tiled=True)  16.3 us
    all_gather x1, blocking collectives, shards(): all_rows = lax.all_gather(all_rows, 'dev_0', axis=0, tiled=True)  11.8 us
    all_to_all x1, starting transfers between devices, shards(): lax.all_to_all(out_proj.reshape(dev_count, -1, out_proj.shape[1]), DEV, 0...  10.6 us
  transfers between devices with their start and end apart: 6, of which 5 were waited for; matrix products, arithmetic and copies ran while one was open for 3% of the time, Pallas kernels for 0%

profile of v3, /device:TPU:1, one launch (start us, length us, event | category | flops | bytes accessed | tf_op | source)
XLA Modules:
  0.0 294.7 jit_solution(4130537382517096242)
XLA Ops:
  6.5 2.1 copy_bitcast_fusion
  8.6 10.6 %all-to-all-start = ((bf16[32,128,64]{1,2,0:T(8,128)(2,1)}), bf16[32,128,64]{1,2,0:T(8,128)(2,1)S(1)}, u32[]{:S(2)}, u32[]{:S(2)}) async-start(bf16[32,128,64]{1,2,0:T(8,128)(2,1)} %copy_bitcast_fusion), calls=%async_computation | async-start | bytes 1048576 | tf_op jit(solution)/shard_map/all_to_all | solution.py:165
  19.2 0.8 negate_bitcast_fusion
  20.0 0.6 reduce-window.6
  21.0 0.2 slice_reduce_fusion.3
  21.3 0.9 copy.61
  22.4 0.2 convolution_convert_fusion.3
  22.7 25.4 %all_gather.9 = bf16[16,2,8193]{2,1,0:T(2,128)(2,1)S(1)} all-gather(bf16[1,2,8193]{2,1,0:T(2,128)(2,1)S(1)} %pad_maximum_fusion), channel_id=1, replica_groups=mesh['grp'=16,'dev_0'=4,'dev_1'=8] {'grp'}, dimensions={0}, use_global_device_ids=true | all-gather | bytes 557124 | tf_op jit(solution)/shard_map/all_gather | solution.py:18
  48.1 0.7 slice.48
  49.3 0.4 reshape.236
  49.7 0.6 fusion.23
  50.3 0.2 fusion.6
  50.8 0.6 fusion.5
  51.6 0.3 concatenate.25
  52.0 1.5 fusion
  53.5 9.5 %all-to-all-start.1 = ((bf16[32,8,2176]{2,1,0:T(8,128)(2,1)}), bf16[32,8,2176]{2,1,0:T(8,128)(2,1)S(1)}, u32[]{:S(2)}, u32[]{:S(2)}) async-start(bf16[32,8,2176]{2,1,0:T(8,128)(2,1)} %fusion), calls=%async_computation.1 | async-start | bytes 2228224 | tf_op jit(solution)/shard_map/all_to_all | solution.py:184
  63.3 0.2 select_reduce_fusion
  63.8 25.5 %all-to-all-done.1 = bf16[32,8,2176]{2,1,0:T(8,128)(2,1)S(1)} async-done(((bf16[32,8,2176]{2,1,0:T(8,128)(2,1)}), bf16[32,8,2176]{2,1,0:T(8,128)(2,1)S(1)}, u32[]{:S(2)}, u32[]{:S(2)}) %all-to-all-start.1) | async-done | bytes 1114144 | tf_op jit(solution)/shard_map/all_to_all | solution.py:184
  89.7 0.2 fusion.45
  89.9 0.2 convolution_convert_fusion.2
  90.3 16.3 %all_to_all.20 = bf16[16,2,2048]{2,1,0:T(2,128)(2,1)S(1)} all-to-all(bf16[16,2,2048]{2,1,0:T(2,128)(2,1)S(1)} %reshape.241), channel_id=1, replica_groups=mesh['grp'=16,'dev_0'=4,'dev_1'=8] {'grp'}, dimensions={0} | all-to-all | bytes 262144 | tf_op jit(solution)/shard_map/all_to_all | solution.py:207
  106.7 11.8 %all_gather.10 = bf16[128,2048]{1,0:T(8,128)(2,1)} all-gather(bf16[32,2048]{1,0:T(8,128)(2,1)S(1)} %reshape.242), channel_id=1, replica_groups=mesh['grp'=16,'dev_0'=4,'dev_1'=8] {'dev_0'}, dimensions={0}, use_global_device_ids=true | all-gather | bytes 655360 | tf_op jit(solution)/shard_map/all_gather | solution.py:209
  118.6 51.0 %all-gather.2.cloned.1.call-done = bf16[1024,2048]{1,0:T(8,128)(2,1)} async-done(((bf16[128,2048]{1,0:T(8,128)(2,1)}), bf16[1024,2048]{1,0:T(8,128)(2,1)}) %all-gather.2.cloned.1.call-update) | async-done | bytes 4194320 | tf_op jit(solution)/shard_map/all_gather | solution.py:210
  169.5 4.5 %fusion.15 = f32[1024,256]{1,0:T(8,128)} fusion(bf16[1024,2048]{1,0:T(8,128)(2,1)} %all-gather.2.cloned.1.call-done, bf16[1,2048,256]{2,1,0:T(8,128)(2,1)S(1)} %copy-done.9), kind=kOutput, calls=%fused_computation.23 | convolution fusion | flops 1073741824 | bytes 6291456 | tf_op jit(solution)/shard_map/dot_general | solution.py:211
  174.0 8.8 %convolution_convert_fusion.1 = bf16[1024,2048]{1,0:T(8,128)(2,1)} fusion(bf16[1024,2048]{1,0:T(8,128)(2,1)} %all-gather.2.cloned.1.call-done, bf16[1,256,2048]{2,1,0:T(8,128)(2,1)S(1)} %copy-done, bf16[1,2048,256]{2,1,0:T(8,128)(2,1)S(1)} %copy-done.10, f32[1024,256]{1,0:T(8,128)} %fusion.15), kind=kOutput, calls=%fused_computation.1 | convolution fusion | flops 2151153664 | bytes 11534336 | tf_op jit(solution)/shard_map/dot_general | solution.py:214
  182.9 56.8 %reduce-scatter.3.cloned.1.call-done = bf16[128,2048]{1,0:T(8,128)(2,1)} async-done(((bf16[1024,2048]{1,0:T(8,128)(2,1)}), bf16[128,2048]{1,0:T(8,128)(2,1)}) %reduce-scatter.3.cloned.1.call-update) | async-done | bytes 524304 | tf_op jit(solution)/shard_map/reduce_scatter | solution.py:215
  239.8 26.9 %reduce-scatter.5.cloned.1.call-done = bf16[32,2048]{1,0:T(8,128)(2,1)} async-done(((bf16[128,2048]{1,0:T(8,128)(2,1)}), bf16[32,2048]{1,0:T(8,128)(2,1)}) %reduce-scatter.5.cloned.1.call-update) | async-done | bytes 131088 | tf_op jit(solution)/shard_map/reduce_scatter | solution.py:218
  266.7 1.6 reshape.243
  268.4 9.7 %all-to-all-start.3 = ((bf16[16,2,2048]{2,1,0:T(2,128)(2,1)}), bf16[16,2,2048]{2,1,0:T(2,128)(2,1)S(1)}, u32[]{:S(2)}, u32[]{:S(2)}) async-start(bf16[16,2,2048]{2,1,0:T(2,128)(2,1)} %reshape.243), calls=%async_computation.5 | async-start | bytes 262144 | tf_op jit(solution)/shard_map/all_to_all | solution.py:219
  278.1 0.3 select_reduce_fusion.2
  278.5 8.8 %all-to-all-done.3 = bf16[16,2,2048]{2,1,0:T(2,128)(2,1)S(1)} async-done(((bf16[16,2,2048]{2,1,0:T(2,128)(2,1)}), bf16[16,2,2048]{2,1,0:T(2,128)(2,1)S(1)}, u32[]{:S(2)}, u32[]{:S(2)}) %all-to-all-start.3) | async-done | bytes 131104 | tf_op jit(solution)/shard_map/all_to_all | solution.py:219
  287.3 0.9 fusion.2
  (76 shorter events, 3.1 us)
Async XLA Ops:
  6.5 167.5 %copy-start = (bf16[1,256,2048]{2,1,0:T(8,128)(2,1)S(1)}, bf16[1,256,2048]{2,1,0:T(8,128)(2,1)}, u32[]{:S(2)}) copy-start(bf16[1,256,2048]{2,1,0:T(8,128)(2,1)} %param.31) | copy-start | bytes 3145732
  6.5 15.7 %copy-start.6 = (f32[256,2]{0,1:T(2,128)S(1)}, f32[256,2]{0,1:T(2,128)}, u32[]{:S(2)}) copy-start(f32[256,2]{0,1:T(2,128)} %param.18) | copy-start | bytes 6148
  6.5 15.8 %copy-start.1 = (bf16[256,128]{1,0:T(8,128)(2,1)S(1)}, bf16[256,128]{1,0:T(8,128)(2,1)}, u32[]{:S(2)}) copy-start(bf16[256,128]{1,0:T(8,128)(2,1)} %param.20) | copy-start | bytes 196612
  8.6 41.7 %copy-start.2 = (bf16[256,128]{1,0:T(8,128)(2,1)S(1)}, bf16[256,128]{1,0:T(8,128)(2,1)}, u32[]{:S(2)}) copy-start(bf16[256,128]{1,0:T(8,128)(2,1)} %param.21) | copy-start | bytes 196612
  8.6 43.0 %all-to-all-start = ((bf16[32,128,64]{1,2,0:T(8,128)(2,1)}), bf16[32,128,64]{1,2,0:T(8,128)(2,1)S(1)}, u32[]{:S(2)}, u32[]{:S(2)}) async-start(bf16[32,128,64]{1,2,0:T(8,128)(2,1)} %copy_bitcast_fusion), calls=%async_computation | async-start | bytes 1048576 | tf_op jit(solution)/shard_map/all_to_all | solution.py:165
  22.3 28.5 %copy-start.12 = (f32[2]{0:T(128)S(1)}, f32[2]{0:T(128)}, u32[]{:S(2)}) copy-start(f32[2]{0:T(128)} %param.22) | copy-start | bytes 28
  48.8 2.7 copy-start.3
  48.8 2.7 copy-start.8
  52.0 11.1 %copy-start.7 = (s32[8,2]{0,1:T(2,128)S(1)}, s32[8,2]{0,1:T(2,128)}, u32[]{:S(2)}) copy-start(s32[8,2]{0,1:T(2,128)} %param.28) | copy-start | bytes 196
  53.5 35.8 %all-to-all-start.1 = ((bf16[32,8,2176]{2,1,0:T(8,128)(2,1)}), bf16[32,8,2176]{2,1,0:T(8,128)(2,1)S(1)}, u32[]{:S(2)}, u32[]{:S(2)}) async-start(bf16[32,8,2176]{2,1,0:T(8,128)(2,1)} %fusion), calls=%async_computation.1 | async-start | bytes 2228224 | tf_op jit(solution)/shard_map/all_to_all | solution.py:184
  63.0 106.5 %all-gather.2.cloned.1.call-start = ((), (), s32[]{:S(2)}) async-start(), calls=%async_computation.6 | async-start | bytes 4718592 | tf_op jit(solution)/shard_map/all_gather | solution.py:210
  63.8 25.9 %copy-start.4 = (bf16[8,2048]{1,0:T(8,128)(2,1)S(1)}, bf16[8,2048]{1,0:T(8,128)(2,1)}, u32[]{:S(2)}) copy-start(bf16[8,2048]{1,0:T(8,128)(2,1)} %param.25) | copy-start | bytes 98308
  63.8 26.1 %copy-start.5 = (f32[2048]{0:T(1024)S(1)}, f32[2048]{0:T(1024)}, u32[]{:S(2)}) copy-start(f32[2048]{0:T(1024)} %param.26) | copy-start | bytes 24580
  89.4 80.1 %copy-start.9 = (bf16[1,2048,256]{2,1,0:T(8,128)(2,1)S(1)}, bf16[1,2048,256]{2,1,0:T(8,128)(2,1)}, u32[]{:S(2)}) copy-start(bf16[1,2048,256]{2,1,0:T(8,128)(2,1)} %param.29) | copy-start | bytes 3145732
  118.5 55.5 %copy-start.10 = (bf16[1,2048,256]{2,1,0:T(8,128)(2,1)S(1)}, bf16[1,2048,256]{2,1,0:T(8,128)(2,1)}, u32[]{:S(2)}) copy-start(bf16[1,2048,256]{2,1,0:T(8,128)(2,1)} %param.30) | copy-start | bytes 3145732
  118.5 121.2 %reduce-scatter.3.cloned.1.call-start = ((), (), s32[]{:S(2)}) async-start(), calls=%async_computation.7 | async-start | bytes 4718592 | tf_op jit(solution)/shard_map/reduce_scatter | solution.py:215
  182.9 95.2 %copy-start.11 = (f32[2048,16]{0,1:T(8,128)S(1)}, f32[2048,16]{0,1:T(8,128)}, u32[]{:S(2)}) copy-start(f32[2048,16]{0,1:T(8,128)} %param.27) | copy-start | bytes 393220
  182.9 83.8 %reduce-scatter.5.cloned.1.call-start = ((), (), s32[]{:S(2)}) async-start(), calls=%async_computation.8 | async-start | bytes 655360 | tf_op jit(solution)/shard_map/reduce_scatter | solution.py:218
  268.4 18.9 %all-to-all-start.3 = ((bf16[16,2,2048]{2,1,0:T(2,128)(2,1)}), bf16[16,2,2048]{2,1,0:T(2,128)(2,1)S(1)}, u32[]{:S(2)}, u32[]{:S(2)}) async-start(bf16[16,2,2048]{2,1,0:T(2,128)(2,1)} %reshape.243), calls=%async_computation.5 | async-start | bytes 262144 | tf_op jit(solution)/shard_map/all_to_all | solution.py:219
Sparse Core Ops, SparseCore 0:
  118.6 50.8 all-gather.1
  183.0 56.6 reduce-scatter.2
  242.6 24.1 reduce-scatter.4

commit v4 on v3

--- a/solution.py
+++ b/solution.py
@@ -215,18 +215,18 @@
     summed = lax.psum_scatter(
         partial_down.astype(jnp.bfloat16), "dev_1", scatter_dimension=0, tiled=True
     )
-    summed = lax.psum_scatter(summed, "dev_0", scatter_dimension=0, tiled=True)
-    returned = lax.all_to_all(
-        summed.astype(jnp.bfloat16).reshape(experts, slot_cap, model_dim),
-        "grp",
-        split_axis=0,
-        concat_axis=0,
-        tiled=True,
+    x_count = lax.axis_size("dev_0")
+    summed = jnp.swapaxes(summed.reshape(x_count, experts, slot_cap, model_dim), 0, 1)
+    landed_back = lax.all_to_all(
+        summed.reshape(experts * x_count, slot_cap, model_dim), ("grp", "dev_0"), 0, 0, tiled=True
+    )
+    returned = jnp.sum(
+        landed_back.reshape(experts, x_count, slot_cap, model_dim).astype(jnp.float32), axis=1
     )
     weights = first_prob[:, None] * placed[:, 0, :] + second_prob[:, None] * placed[:, 1, :]
     contrib = jnp.dot(
         weights,
-        returned.reshape(group_slots, model_dim).astype(jnp.float32),
+        returned.reshape(group_slots, model_dim),
         precision=HIGHEST_PREC,
     )
     return (hidden_float + contrib).astype(jnp.bfloat16)

time: 295 us -> 280 us (0.949)
  waiting for transfers between devices: 169 us -> 150 us
    reduce_scatter x1 -> x0, waiting for transfers between devices: 26.9 us -> none  [shards(): summed = lax.psum_scatter(summed, 'dev_0', scatter_dimension=0, tiled=True)]
    all_to_all x1, waiting for transfers between devices: 8.79 us -> 16.8 us  [shards(): lax.all_to_all(summed.reshape(experts * x_count, slot_cap, model_dim), ('...]
  transfers between devices with their start and end apart: 6 -> 5, of which waited for: 5 -> 4; matrix products, arithmetic and copies ran while one was open for 3% -> 3% of each run, Pallas kernels for 0% -> 0%
where the time goes in v4:
time: 280 us; the launch traced here: 279 us
  waiting for transfers between devices  150 us (54%)
  blocking collectives  53.6 us (19%)
  starting transfers between devices  31.2 us (11%)
  matrix products  18.1 us (6%)
  between operations  13.8 us (5%)
  local copies, waits for them, and re-layouts  8.66 us (3%)
  other arithmetic  3.69 us (1%)
    reduce_scatter x1, waiting for transfers between devices, shards(): lax.psum_scatter(partial_down.astype(jnp.bfloat16), 'dev_1', scatter_dime...  56.8 us
    all_gather x1, waiting for transfers between devices, shards(): all_rows = lax.all_gather(all_rows, 'dev_1', axis=0, tiled=True)  51 us
    all_to_all x1, waiting for transfers between devices, shards(): lax.all_to_all(payload.reshape(dev_count, block_rows, payload.shape[1]),...  25.5 us
    all_gather x1, blocking collectives, side_by_side(): lax.all_gather(both, axis, axis=dim, tiled=True)  25.4 us
    all_to_all x1, waiting for transfers between devices, shards(): lax.all_to_all(summed.reshape(experts * x_count, slot_cap, model_dim), ('...  16.8 us
    all_to_all x1, blocking collectives, shards(): lax.all_to_all(outgoing, 'grp', split_axis=0, concat_axis=0, tiled=True)  16.3 us
    all_gather x1, blocking collectives, shards(): all_rows = lax.all_gather(all_rows, 'dev_0', axis=0, tiled=True)  11.8 us
    all_to_all x1, starting transfers between devices, shards(): lax.all_to_all(summed.reshape(experts * x_count, slot_cap, model_dim), ('...  11 us
  transfers between devices with their start and end apart: 5, of which 4 were waited for; matrix products, arithmetic and copies ran while one was open for 3% of the time, Pallas kernels for 0%

profile of v4, /device:TPU:1, one launch (start us, length us, event | category | flops | bytes accessed | tf_op | source)
XLA Modules:
  0.0 279.1 jit_solution(2786931629578190042)
XLA Ops:
  6.5 2.1 copy_bitcast_fusion
  8.6 10.6 %all-to-all-start = ((bf16[32,128,64]{1,2,0:T(8,128)(2,1)}), bf16[32,128,64]{1,2,0:T(8,128)(2,1)S(1)}, u32[]{:S(2)}, u32[]{:S(2)}) async-start(bf16[32,128,64]{1,2,0:T(8,128)(2,1)} %copy_bitcast_fusion), calls=%async_computation | async-start | bytes 1048576 | tf_op jit(solution)/shard_map/all_to_all | solution.py:165
  19.2 0.8 negate_bitcast_fusion
  20.0 0.6 reduce-window.6
  21.0 0.2 slice_reduce_fusion.3
  21.3 0.9 copy.65
  22.4 0.2 convolution_convert_fusion.3
  22.7 25.4 %all_gather.9 = bf16[16,2,8193]{2,1,0:T(2,128)(2,1)S(1)} all-gather(bf16[1,2,8193]{2,1,0:T(2,128)(2,1)S(1)} %pad_maximum_fusion), channel_id=1, replica_groups=mesh['grp'=16,'dev_0'=4,'dev_1'=8] {'grp'}, dimensions={0}, use_global_device_ids=true | all-gather | bytes 557124 | tf_op jit(solution)/shard_map/all_gather | solution.py:18
  48.1 0.7 slice.48
  49.3 0.4 reshape.242
  49.7 0.6 fusion.23
  50.3 0.2 fusion.6
  50.8 0.6 fusion.5
  51.6 0.3 concatenate.25
  52.0 1.5 fusion
  53.5 9.5 %all-to-all-start.1 = ((bf16[32,8,2176]{2,1,0:T(8,128)(2,1)}), bf16[32,8,2176]{2,1,0:T(8,128)(2,1)S(1)}, u32[]{:S(2)}, u32[]{:S(2)}) async-start(bf16[32,8,2176]{2,1,0:T(8,128)(2,1)} %fusion), calls=%async_computation.1 | async-start | bytes 2228224 | tf_op jit(solution)/shard_map/all_to_all | solution.py:184
  63.8 25.5 %all-to-all-done.1 = bf16[32,8,2176]{2,1,0:T(8,128)(2,1)S(1)} async-done(((bf16[32,8,2176]{2,1,0:T(8,128)(2,1)}), bf16[32,8,2176]{2,1,0:T(8,128)(2,1)S(1)}, u32[]{:S(2)}, u32[]{:S(2)}) %all-to-all-start.1) | async-done | bytes 1114144 | tf_op jit(solution)/shard_map/all_to_all | solution.py:184
  89.7 0.2 fusion.45
  89.9 0.2 convolution_convert_fusion.2
  90.3 16.3 %all_to_all.20 = bf16[16,2,2048]{2,1,0:T(2,128)(2,1)S(1)} all-to-all(bf16[16,2,2048]{2,1,0:T(2,128)(2,1)S(1)} %reshape.247), channel_id=1, replica_groups=mesh['grp'=16,'dev_0'=4,'dev_1'=8] {'grp'}, dimensions={0} | all-to-all | bytes 262144 | tf_op jit(solution)/shard_map/all_to_all | solution.py:207
  106.7 11.8 %all_gather.10 = bf16[128,2048]{1,0:T(8,128)(2,1)} all-gather(bf16[32,2048]{1,0:T(8,128)(2,1)S(1)} %reshape.248), channel_id=1, replica_groups=mesh['grp'=16,'dev_0'=4,'dev_1'=8] {'dev_0'}, dimensions={0}, use_global_device_ids=true | all-gather | bytes 655360 | tf_op jit(solution)/shard_map/all_gather | solution.py:209
  118.6 51.0 %all-gather.2.cloned.1.call-done = bf16[1024,2048]{1,0:T(8,128)(2,1)} async-done(((bf16[128,2048]{1,0:T(8,128)(2,1)}), bf16[1024,2048]{1,0:T(8,128)(2,1)}) %all-gather.2.cloned.1.call-update) | async-done | bytes 4194320 | tf_op jit(solution)/shard_map/all_gather | solution.py:210
  169.5 4.5 %fusion.15 = f32[1024,256]{1,0:T(8,128)} fusion(bf16[1024,2048]{1,0:T(8,128)(2,1)} %all-gather.2.cloned.1.call-done, bf16[1,2048,256]{2,1,0:T(8,128)(2,1)S(1)} %copy-done.9), kind=kOutput, calls=%fused_computation.24 | convolution fusion | flops 1073741824 | bytes 6291456 | tf_op jit(solution)/shard_map/dot_general | solution.py:211
  174.0 8.8 %convolution_convert_fusion.1 = bf16[1024,2048]{1,0:T(8,128)(2,1)} fusion(bf16[1024,2048]{1,0:T(8,128)(2,1)} %all-gather.2.cloned.1.call-done, bf16[1,256,2048]{2,1,0:T(8,128)(2,1)S(1)} %copy-done, bf16[1,2048,256]{2,1,0:T(8,128)(2,1)S(1)} %copy-done.10, f32[1024,256]{1,0:T(8,128)} %fusion.15), kind=kOutput, calls=%fused_computation.1 | convolution fusion | flops 2151153664 | bytes 11534336 | tf_op jit(solution)/shard_map/dot_general | solution.py:214
  182.9 56.8 %reduce-scatter.2.cloned.1.call-done = bf16[128,2048]{1,0:T(8,128)(2,1)} async-done(((bf16[1024,2048]{1,0:T(8,128)(2,1)}), bf16[128,2048]{1,0:T(8,128)(2,1)}) %reduce-scatter.2.cloned.1.call-update) | async-done | bytes 524304 | tf_op jit(solution)/shard_map/reduce_scatter | solution.py:215
  239.7 1.4 reshape.249
  241.1 1.3 copy.75
  242.4 11.0 %all-to-all-start.3 = ((bf16[64,2,2048]{2,1,0:T(2,128)(2,1)}), bf16[64,2,2048]{2,1,0:T(2,128)(2,1)S(1)}, u32[]{:S(2)}, u32[]{:S(2)}) async-start(bf16[64,2,2048]{2,1,0:T(2,128)(2,1)} %bitcast.24), calls=%async_computation.4 | async-start | bytes 1048576 | tf_op jit(solution)/shard_map/all_to_all | solution.py:220
  253.5 0.3 select_reduce_fusion.2
  253.8 16.8 %all-to-all-done.3 = bf16[64,2,2048]{2,1,0:T(2,128)(2,1)S(1)} async-done(((bf16[64,2,2048]{2,1,0:T(2,128)(2,1)}), bf16[64,2,2048]{2,1,0:T(2,128)(2,1)S(1)}, u32[]{:S(2)}, u32[]{:S(2)}) %all-to-all-start.3) | async-done | bytes 524320 | tf_op jit(solution)/shard_map/all_to_all | solution.py:220
  270.6 0.5 convert_reduce_fusion
  271.3 0.9 fusion.2
  (75 shorter events, 3.3 us)
Async XLA Ops:
  6.5 167.5 %copy-start = (bf16[1,256,2048]{2,1,0:T(8,128)(2,1)S(1)}, bf16[1,256,2048]{2,1,0:T(8,128)(2,1)}, u32[]{:S(2)}) copy-start(bf16[1,256,2048]{2,1,0:T(8,128)(2,1)} %param.31) | copy-start | bytes 3145732
  6.5 15.7 %copy-start.6 = (f32[256,2]{0,1:T(2,128)S(1)}, f32[256,2]{0,1:T(2,128)}, u32[]{:S(2)}) copy-start(f32[256,2]{0,1:T(2,128)} %param.18) | copy-start | bytes 6148
  6.5 15.8 %copy-start.1 = (bf16[256,128]{1,0:T(8,128)(2,1)S(1)}, bf16[256,128]{1,0:T(8,128)(2,1)}, u32[]{:S(2)}) copy-start(bf16[256,128]{1,0:T(8,128)(2,1)} %param.20) | copy-start | bytes 196612
  8.6 41.7 %copy-start.2 = (bf16[256,128]{1,0:T(8,128)(2,1)S(1)}, bf16[256,128]{1,0:T(8,128)(2,1)}, u32[]{:S(2)}) copy-start(bf16[256,128]{1,0:T(8,128)(2,1)} %param.21) | copy-start | bytes 196612
  8.6 43.0 %all-to-all-start = ((bf16[32,128,64]{1,2,0:T(8,128)(2,1)}), bf16[32,128,64]{1,2,0:T(8,128)(2,1)S(1)}, u32[]{:S(2)}, u32[]{:S(2)}) async-start(bf16[32,128,64]{1,2,0:T(8,128)(2,1)} %copy_bitcast_fusion), calls=%async_computation | async-start | bytes 1048576 | tf_op jit(solution)/shard_map/all_to_all | solution.py:165
  22.3 28.5 %copy-start.12 = (f32[2]{0:T(128)S(1)}, f32[2]{0:T(128)}, u32[]{:S(2)}) copy-start(f32[2]{0:T(128)} %param.22) | copy-start | bytes 28
  48.8 2.7 copy-start.3
  48.8 2.7 copy-start.8
  52.0 11.1 %copy-start.7 = (s32[8,2]{0,1:T(2,128)S(1)}, s32[8,2]{0,1:T(2,128)}, u32[]{:S(2)}) copy-start(s32[8,2]{0,1:T(2,128)} %param.28) | copy-start | bytes 196
  53.5 35.8 %all-to-all-start.1 = ((bf16[32,8,2176]{2,1,0:T(8,128)(2,1)}), bf16[32,8,2176]{2,1,0:T(8,128)(2,1)S(1)}, u32[]{:S(2)}, u32[]{:S(2)}) async-start(bf16[32,8,2176]{2,1,0:T(8,128)(2,1)} %fusion), calls=%async_computation.1 | async-start | bytes 2228224 | tf_op jit(solution)/shard_map/all_to_all | solution.py:184
  63.0 106.5 %all-gather.2.cloned.1.call-start = ((), (), s32[]{:S(2)}) async-start(), calls=%async_computation.5 | async-start | bytes 4718592 | tf_op jit(solution)/shard_map/all_gather | solution.py:210
  63.8 25.9 %copy-start.4 = (bf16[8,2048]{1,0:T(8,128)(2,1)S(1)}, bf16[8,2048]{1,0:T(8,128)(2,1)}, u32[]{:S(2)}) copy-start(bf16[8,2048]{1,0:T(8,128)(2,1)} %param.25) | copy-start | bytes 98308
  63.8 26.1 %copy-start.5 = (f32[2048]{0:T(1024)S(1)}, f32[2048]{0:T(1024)}, u32[]{:S(2)}) copy-start(f32[2048]{0:T(1024)} %param.26) | copy-start | bytes 24580
  89.4 80.1 %copy-start.9 = (bf16[1,2048,256]{2,1,0:T(8,128)(2,1)S(1)}, bf16[1,2048,256]{2,1,0:T(8,128)(2,1)}, u32[]{:S(2)}) copy-start(bf16[1,2048,256]{2,1,0:T(8,128)(2,1)} %param.29) | copy-start | bytes 3145732
  118.5 55.5 %copy-start.10 = (bf16[1,2048,256]{2,1,0:T(8,128)(2,1)S(1)}, bf16[1,2048,256]{2,1,0:T(8,128)(2,1)}, u32[]{:S(2)}) copy-start(bf16[1,2048,256]{2,1,0:T(8,128)(2,1)} %param.30) | copy-start | bytes 3145732
  118.5 121.2 %reduce-scatter.2.cloned.1.call-start = ((), (), s32[]{:S(2)}) async-start(), calls=%async_computation.6 | async-start | bytes 4718592 | tf_op jit(solution)/shard_map/reduce_scatter | solution.py:215
  182.9 70.6 %copy-start.11 = (f32[2048,16]{0,1:T(8,128)S(1)}, f32[2048,16]{0,1:T(8,128)}, u32[]{:S(2)}) copy-start(f32[2048,16]{0,1:T(8,128)} %param.27) | copy-start | bytes 393220
  242.4 28.2 %all-to-all-start.3 = ((bf16[64,2,2048]{2,1,0:T(2,128)(2,1)}), bf16[64,2,2048]{2,1,0:T(2,128)(2,1)S(1)}, u32[]{:S(2)}, u32[]{:S(2)}) async-start(bf16[64,2,2048]{2,1,0:T(2,128)(2,1)} %bitcast.24), calls=%async_computation.4 | async-start | bytes 1048576 | tf_op jit(solution)/shard_map/all_to_all | solution.py:220
Sparse Core Ops, SparseCore 0:
  118.6 50.8 all-gather.1
  183.0 56.6 reduce-scatter.1

commit v5 on v4

--- a/solution.py
+++ b/solution.py
@@ -205,24 +205,26 @@
     ).astype(jnp.bfloat16)
     outgoing = outgoing.reshape(experts, slot_cap, model_dim)
     arrived = lax.all_to_all(outgoing, "grp", split_axis=0, concat_axis=0, tiled=True)
-    all_rows = arrived.reshape(-1, model_dim)
-    all_rows = lax.all_gather(all_rows, "dev_0", axis=0, tiled=True)
-    all_rows = lax.all_gather(all_rows, "dev_1", axis=0, tiled=True)
-    gate_act = jnp.dot(all_rows, gate_weight[0], preferred_element_type=jnp.float32)
-    up_act = jnp.dot(all_rows, up_weight[0], preferred_element_type=jnp.float32)
-    hidden = (jax.nn.silu(gate_act) * up_act).astype(jnp.bfloat16)
-    partial_down = jnp.dot(hidden, down_weight[0], preferred_element_type=jnp.float32)
-    summed = lax.psum_scatter(
-        partial_down.astype(jnp.bfloat16), "dev_1", scatter_dimension=0, tiled=True
-    )
     x_count = lax.axis_size("dev_0")
-    summed = jnp.swapaxes(summed.reshape(x_count, experts, slot_cap, model_dim), 0, 1)
-    landed_back = lax.all_to_all(
-        summed.reshape(experts * x_count, slot_cap, model_dim), ("grp", "dev_0"), 0, 0, tiled=True
-    )
-    returned = jnp.sum(
-        landed_back.reshape(experts, x_count, slot_cap, model_dim).astype(jnp.float32), axis=1
-    )
+    halves = []
+    for slot in range(slot_cap):
+        rows = lax.all_gather(arrived[:, slot, :], "dev_0", axis=0, tiled=True)
+        rows = lax.all_gather(rows, "dev_1", axis=0, tiled=True)
+        gate_act = jnp.dot(rows, gate_weight[0], preferred_element_type=jnp.float32)
+        up_act = jnp.dot(rows, up_weight[0], preferred_element_type=jnp.float32)
+        hidden = (jax.nn.silu(gate_act) * up_act).astype(jnp.bfloat16)
+        partial_down = jnp.dot(hidden, down_weight[0], preferred_element_type=jnp.float32)
+        summed = lax.psum_scatter(
+            partial_down.astype(jnp.bfloat16), "dev_1", scatter_dimension=0, tiled=True
+        )
+        summed = jnp.swapaxes(summed.reshape(x_count, experts, model_dim), 0, 1)
+        landed_back = lax.all_to_all(
+            summed.reshape(experts * x_count, model_dim), ("grp", "dev_0"), 0, 0, tiled=True
+        )
+        halves.append(
+            jnp.sum(landed_back.reshape(experts, x_count, model_dim).astype(jnp.float32), axis=1)
+        )
+    returned = jnp.stack(halves, axis=1)
     weights = first_prob[:, None] * placed[:, 0, :] + second_prob[:, None] * placed[:, 1, :]
     contrib = jnp.dot(
         weights,

time: 280 us -> 330 us (1.18)
  starting transfers between devices: 31.2 us -> 50.3 us
  blocking collectives: 53.6 us -> 63 us
  waiting for transfers between devices: 150 us -> 158 us
  other arithmetic: 3.69 us -> 10.9 us
  matrix products: 18.1 us -> 21.8 us
    all_to_all x1 -> x2, starting transfers between devices: 11 us -> 29.9 us  [shards(): lax.all_to_all(summed.reshape(experts * x_count, model_dim), ('grp', 'dev...]
    all_gather x1 -> x2, blocking collectives: 11.8 us -> 21.3 us  [shards(): rows = lax.all_gather(arrived[:, slot, :], 'dev_0', axis=0, tiled=True)]
    all_gather x1 -> x2, waiting for transfers between devices: 51 us -> 59.3 us  [shards(): rows = lax.all_gather(rows, 'dev_1', axis=0, tiled=True)]
    all_to_all x1 -> x2, waiting for transfers between devices: 16.8 us -> 9.59 us  [shards(): lax.all_to_all(summed.reshape(experts * x_count, model_dim), ('grp', 'dev...]
    reduce_scatter x1 -> x2, waiting for transfers between devices: 56.8 us -> 63.7 us  [shards(): lax.psum_scatter(partial_down.astype(jnp.bfloat16), 'dev_1', scatter_dime...]
    all_to_all x0 -> x2, other arithmetic: none -> 4.56 us  [shards(): lax.all_to_all(summed.reshape(experts * x_count, model_dim), ('grp', 'dev...]
    dot_general x1 -> x2, matrix products: 4.52 us -> 7.02 us  [shards(): gate_act = jnp.dot(rows, gate_weight[0], preferred_element_type=jnp.float32)]
    dot_general x1 -> x2, matrix products: 8.8 us -> 9.97 us  [shards(): jnp.dot(hidden, down_weight[0], preferred_element_type=jnp.float32)]
  transfers between devices with their start and end apart: 5 -> 8, of which waited for: 4 -> 6; matrix products, arithmetic and copies ran while one was open for 3% -> 11% of each run, Pallas kernels for 0% -> 0%
where the time goes in v5:
time: 330 us
  waiting for transfers between devices  158 us (48%)
  blocking collectives  63 us (19%)
  starting transfers between devices  50.3 us (15%)
  matrix products  21.8 us (7%)
  between operations  13.6 us (4%)
  local copies, waits for them, and re-layouts  11.7 us (4%)
  other arithmetic  10.9 us (3%)
    reduce_scatter x2, waiting for transfers between devices, shards(): lax.psum_scatter(partial_down.astype(jnp.bfloat16), 'dev_1', scatter_dime...  63.7 us
    all_gather x2, waiting for transfers between devices, shards(): rows = lax.all_gather(rows, 'dev_1', axis=0, tiled=True)  59.3 us
    all_to_all x2, starting transfers between devices, shards(): lax.all_to_all(summed.reshape(experts * x_count, model_dim), ('grp', 'dev...  29.9 us
    all_to_all x1, waiting for transfers between devices, shards(): lax.all_to_all(payload.reshape(dev_count, block_rows, payload.shape[1]),...  25.5 us
    all_gather x1, blocking collectives, side_by_side(): lax.all_gather(both, axis, axis=dim, tiled=True)  25.4 us
    all_gather x2, blocking collectives, shards(): rows = lax.all_gather(arrived[:, slot, :], 'dev_0', axis=0, tiled=True)  21.3 us
    all_to_all x1, blocking collectives, shards(): lax.all_to_all(outgoing, 'grp', split_axis=0, concat_axis=0, tiled=True)  16.3 us
    all_to_all x1, starting transfers between devices, shards(): lax.all_to_all(out_proj.reshape(dev_count, -1, out_proj.shape[1]), DEV, 0...  10.5 us
  transfers between devices with their start and end apart: 8, of which 6 were waited for; matrix products, arithmetic and copies ran while one was open for 11% of the time, Pallas kernels for 0%

profile of v5, /device:TPU:1, one launch (start us, length us, event | category | flops | bytes accessed | tf_op | source)
XLA Modules:
  0.0 329.5 jit_solution(5488313034065792741)
XLA Ops:
  6.5 2.1 copy_bitcast_fusion
  8.6 10.5 %all-to-all-start = ((bf16[32,128,64]{1,2,0:T(8,128)(2,1)}), bf16[32,128,64]{1,2,0:T(8,128)(2,1)S(1)}, u32[]{:S(2)}, u32[]{:S(2)}) async-start(bf16[32,128,64]{1,2,0:T(8,128)(2,1)} %copy_bitcast_fusion), calls=%async_computation | async-start | bytes 1048576 | tf_op jit(solution)/shard_map/all_to_all | solution.py:165
  19.2 0.6 reduce-window.6
  21.1 25.4 %all_gather.15 = bf16[16,2,8193]{2,1,0:T(2,128)(2,1)S(1)} all-gather(bf16[1,2,8193]{2,1,0:T(2,128)(2,1)S(1)} %pad_maximum_fusion.1), channel_id=1, replica_groups=mesh['grp'=16,'dev_0'=4,'dev_1'=8] {'grp'}, dimensions={0}, use_global_device_ids=true | all-gather | bytes 557124 | tf_op jit(solution)/shard_map/all_gather | solution.py:18
  46.5 0.7 slice.56
  49.2 0.6 fusion.28
  50.4 1.5 fusion
  51.9 9.5 %all-to-all-start.1 = ((bf16[32,8,2176]{2,1,0:T(8,128)(2,1)}), bf16[32,8,2176]{2,1,0:T(8,128)(2,1)S(1)}, u32[]{:S(2)}, u32[]{:S(2)}) async-start(bf16[32,8,2176]{2,1,0:T(8,128)(2,1)} %fusion), calls=%async_computation.1 | async-start | bytes 2228224 | tf_op jit(solution)/shard_map/all_to_all | solution.py:184
  62.2 25.5 %all-to-all-done.1 = bf16[32,8,2176]{2,1,0:T(8,128)(2,1)S(1)} async-done(((bf16[32,8,2176]{2,1,0:T(8,128)(2,1)}), bf16[32,8,2176]{2,1,0:T(8,128)(2,1)S(1)}, u32[]{:S(2)}, u32[]{:S(2)}) %all-to-all-start.1) | async-done | bytes 1114144 | tf_op jit(solution)/shard_map/all_to_all | solution.py:184
  88.6 16.3 %all_to_all.35 = bf16[16,2,2048]{2,1,0:T(2,128)(2,1)S(1)} all-to-all(bf16[16,2,2048]{2,1,0:T(2,128)(2,1)S(1)} %reshape.257), channel_id=1, replica_groups=mesh['grp'=16,'dev_0'=4,'dev_1'=8] {'grp'}, dimensions={0} | all-to-all | bytes 262144 | tf_op jit(solution)/shard_map/all_to_all | solution.py:207
  105.2 10.6 %all-gather.2 = bf16[64,1,2048]{2,0,1:T(8,128)(2,1)} all-gather(bf16[16,1,2048]{2,0,1:T(8,128)(2,1)S(1)} %copy.102), channel_id=4, replica_groups=mesh['grp'=16,'dev_0'=4,'dev_1'=8] {'dev_0'}, dimensions={0}, use_global_device_ids=true | all-gather | bytes 327680 | tf_op jit(solution)/shard_map/all_gather | solution.py:211
  116.0 10.7 %all-gather = bf16[64,1,2048]{2,0,1:T(8,128)(2,1)} all-gather(bf16[16,1,2048]{2,0,1:T(8,128)(2,1)S(1)} %copy.101), channel_id=2, replica_groups=mesh['grp'=16,'dev_0'=4,'dev_1'=8] {'dev_0'}, dimensions={0}, use_global_device_ids=true | all-gather | bytes 327680 | tf_op jit(solution)/shard_map/all_gather | solution.py:211
  126.7 23.2 %all-gather.9.cloned.1.call-done = bf16[512,1,2048]{2,0,1:T(8,128)(2,1)} async-done(((bf16[64,1,2048]{2,0,1:T(8,128)(2,1)}), bf16[512,1,2048]{2,0,1:T(8,128)(2,1)}) %all-gather.9.cloned.1.call-update) | async-done | bytes 2097168 | tf_op jit(solution)/shard_map/all_gather | solution.py:212
  149.9 3.5 %fusion.5 = f32[512,256]{1,0:T(8,128)} fusion(bf16[512,1,2048]{2,0,1:T(8,128)(2,1)} %all-gather.9.cloned.1.call-done, bf16[1,2048,256]{2,1,0:T(8,128)(2,1)} %param.29), kind=kOutput, calls=%fused_computation.12 | convolution fusion | flops 536870912 | bytes 3670016 | tf_op jit(solution)/shard_map/dot_general | solution.py:213
  153.4 5.0 %convolution_convert_fusion.1 = bf16[512,2048]{1,0:T(8,128)(2,1)} fusion(bf16[512,1,2048]{2,0,1:T(8,128)(2,1)S(1)} %copy-done.12, bf16[1,256,2048]{2,1,0:T(8,128)(2,1)S(1)} %copy-done, bf16[1,2048,256]{2,1,0:T(8,128)(2,1)} %param.30, f32[512,256]{1,0:T(8,128)} %fusion.5), kind=kOutput, calls=%fused_computation.2 | convolution fusion | flops 1075576832 | bytes 6815744 | tf_op jit(solution)/shard_map/dot_general | solution.py:216
  158.7 36.1 %all-gather.7.cloned.1.call-done = bf16[512,1,2048]{2,0,1:T(8,128)(2,1)} async-done(((bf16[64,1,2048]{2,0,1:T(8,128)(2,1)}), bf16[512,1,2048]{2,0,1:T(8,128)(2,1)}) %all-gather.7.cloned.1.call-update) | async-done | bytes 2097168 | tf_op jit(solution)/shard_map/all_gather | solution.py:212
  194.8 3.5 %fusion.9 = f32[512,256]{1,0:T(8,128)} fusion(bf16[512,1,2048]{2,0,1:T(8,128)(2,1)} %all-gather.7.cloned.1.call-done, bf16[1,2048,256]{2,1,0:T(8,128)(2,1)} %param.29), kind=kOutput, calls=%fused_computation.16 | convolution fusion | flops 536870912 | bytes 3670016 | tf_op jit(solution)/shard_map/dot_general | solution.py:213
  198.3 5.0 %convolution_convert_fusion.2 = bf16[512,2048]{1,0:T(8,128)(2,1)} fusion(bf16[512,1,2048]{2,0,1:T(8,128)(2,1)S(1)} %copy-done.11, bf16[1,256,2048]{2,1,0:T(8,128)(2,1)S(1)} %copy-done, bf16[1,2048,256]{2,1,0:T(8,128)(2,1)} %param.30, f32[512,256]{1,0:T(8,128)} %fusion.9), kind=kOutput, calls=%fused_computation.3 | convolution fusion | flops 1075576832 | bytes 6815744 | tf_op jit(solution)/shard_map/dot_general | solution.py:216
  203.3 37.6 %reduce-scatter.5.cloned.1.call-done = bf16[64,2048]{1,0:T(8,128)(2,1)} async-done(((bf16[512,2048]{1,0:T(8,128)(2,1)}), bf16[64,2048]{1,0:T(8,128)(2,1)}) %reduce-scatter.5.cloned.1.call-update) | async-done | bytes 262160 | tf_op jit(solution)/shard_map/reduce_scatter | solution.py:217
  240.9 1.2 copy.115
  243.0 2.3 reduce.10
  245.3 0.9 reshape.276
  246.2 15.0 %all-to-all-start.4 = ((bf16[64,2,1024]{2,1,0:T(2,128)(2,1)}), bf16[64,2,1024]{2,1,0:T(2,128)(2,1)S(1)}, u32[]{:S(2)}, u32[]{:S(2)}) async-start(bf16[64,2,1024]{2,1,0:T(2,128)(2,1)} %reshape.276), calls=%async_computation.6 | async-start | bytes 524288 | tf_op jit(solution)/shard_map/all_to_all | solution.py:221
  261.3 26.1 %reduce-scatter.3.cloned.1.call-done = bf16[64,2048]{1,0:T(8,128)(2,1)} async-done(((bf16[512,2048]{1,0:T(8,128)(2,1)}), bf16[64,2048]{1,0:T(8,128)(2,1)}) %reduce-scatter.3.cloned.1.call-update) | async-done | bytes 262160 | tf_op jit(solution)/shard_map/reduce_scatter | solution.py:217
  287.4 1.2 copy.116
  289.0 2.3 reduce.11
  291.3 0.9 reshape.278
  292.1 14.9 %all-to-all-start.3 = ((bf16[64,2,1024]{2,1,0:T(2,128)(2,1)}), bf16[64,2,1024]{2,1,0:T(2,128)(2,1)S(1)}, u32[]{:S(2)}, u32[]{:S(2)}) async-start(bf16[64,2,1024]{2,1,0:T(2,128)(2,1)} %reshape.278), calls=%async_computation.4 | async-start | bytes 524288 | tf_op jit(solution)/shard_map/all_to_all | solution.py:221
  307.7 1.5 convert_reduce_fusion
  309.8 9.6 %all-to-all-done.3 = bf16[64,2,1024]{2,1,0:T(2,128)(2,1)S(1)} async-done(((bf16[64,2,1024]{2,1,0:T(2,128)(2,1)}), bf16[64,2,1024]{2,1,0:T(2,128)(2,1)S(1)}, u32[]{:S(2)}, u32[]{:S(2)}) %all-to-all-start.3) | async-done | bytes 262176 | tf_op jit(solution)/shard_map/all_to_all | solution.py:221
  319.6 1.5 convert_reduce_fusion.1
  322.1 0.9 fusion.2
  (109 shorter events, 9.9 us)
Async XLA Ops:
  6.5 146.9 %copy-start = (bf16[1,256,2048]{2,1,0:T(8,128)(2,1)S(1)}, bf16[1,256,2048]{2,1,0:T(8,128)(2,1)}, u32[]{:S(2)}) copy-start(bf16[1,256,2048]{2,1,0:T(8,128)(2,1)} %param.31) | copy-start | bytes 3145732
  6.5 12.6 %copy-start.7 = (f32[256,2]{0,1:T(2,128)S(1)}, f32[256,2]{0,1:T(2,128)}, u32[]{:S(2)}) copy-start(f32[256,2]{0,1:T(2,128)} %param.18) | copy-start | bytes 6148
  6.5 12.6 %copy-start.10 = (f32[2]{0:T(128)S(1)}, f32[2]{0:T(128)}, u32[]{:S(2)}) copy-start(f32[2]{0:T(128)} %param.19) | copy-start | bytes 28
  6.5 14.0 %copy-start.4 = (bf16[256,128]{1,0:T(8,128)(2,1)S(1)}, bf16[256,128]{1,0:T(8,128)(2,1)}, u32[]{:S(2)}) copy-start(bf16[256,128]{1,0:T(8,128)(2,1)} %param.16) | copy-start | bytes 196612
  6.5 14.2 %copy-start.1 = (bf16[256,128]{1,0:T(8,128)(2,1)S(1)}, bf16[256,128]{1,0:T(8,128)(2,1)}, u32[]{:S(2)}) copy-start(bf16[256,128]{1,0:T(8,128)(2,1)} %param.20) | copy-start | bytes 196612
  8.6 41.4 %all-to-all-start = ((bf16[32,128,64]{1,2,0:T(8,128)(2,1)}), bf16[32,128,64]{1,2,0:T(8,128)(2,1)S(1)}, u32[]{:S(2)}, u32[]{:S(2)}) async-start(bf16[32,128,64]{1,2,0:T(8,128)(2,1)} %copy_bitcast_fusion), calls=%async_computation | async-start | bytes 1048576 | tf_op jit(solution)/shard_map/all_to_all | solution.py:165
  19.1 29.5 %copy-start.2 = (bf16[256,128]{1,0:T(8,128)(2,1)S(1)}, bf16[256,128]{1,0:T(8,128)(2,1)}, u32[]{:S(2)}) copy-start(bf16[256,128]{1,0:T(8,128)(2,1)} %param.21) | copy-start | bytes 196612
  20.9 28.2 %copy-start.14 = (f32[2]{0:T(128)S(1)}, f32[2]{0:T(128)}, u32[]{:S(2)}) copy-start(f32[2]{0:T(128)} %param.22) | copy-start | bytes 28
  47.2 2.7 copy-start.3
  47.2 2.7 copy-start.9
  50.3 11.1 %copy-start.8 = (s32[8,2]{0,1:T(2,128)S(1)}, s32[8,2]{0,1:T(2,128)}, u32[]{:S(2)}) copy-start(s32[8,2]{0,1:T(2,128)} %param.28) | copy-start | bytes 196
  51.9 35.8 %all-to-all-start.1 = ((bf16[32,8,2176]{2,1,0:T(8,128)(2,1)}), bf16[32,8,2176]{2,1,0:T(8,128)(2,1)S(1)}, u32[]{:S(2)}, u32[]{:S(2)}) async-start(bf16[32,8,2176]{2,1,0:T(8,128)(2,1)} %fusion), calls=%async_computation.1 | async-start | bytes 2228224 | tf_op jit(solution)/shard_map/all_to_all | solution.py:184
  61.4 88.6 %all-gather.9.cloned.1.call-start = ((), (), s32[]{:S(2)}) async-start(), calls=%async_computation.10 | async-start | bytes 2359296 | tf_op jit(solution)/shard_map/all_gather | solution.py:212
  62.1 25.9 %copy-start.5 = (bf16[8,2048]{1,0:T(8,128)(2,1)S(1)}, bf16[8,2048]{1,0:T(8,128)(2,1)}, u32[]{:S(2)}) copy-start(bf16[8,2048]{1,0:T(8,128)(2,1)} %param.25) | copy-start | bytes 98308
  62.1 26.1 %copy-start.6 = (f32[2048]{0:T(1024)S(1)}, f32[2048]{0:T(1024)}, u32[]{:S(2)}) copy-start(f32[2048]{0:T(1024)} %param.26) | copy-start | bytes 24580
  115.9 78.9 %all-gather.7.cloned.1.call-start = ((), (), s32[]{:S(2)}) async-start(), calls=%async_computation.9 | async-start | bytes 2359296 | tf_op jit(solution)/shard_map/all_gather | solution.py:212
  126.7 114.3 %reduce-scatter.5.cloned.1.call-start = ((), (), s32[]{:S(2)}) async-start(), calls=%async_computation.8 | async-start | bytes 2359296 | tf_op jit(solution)/shard_map/reduce_scatter | solution.py:217
  149.9 3.5 %copy-start.12 = (bf16[512,1,2048]{2,0,1:T(8,128)(2,1)S(1)}, bf16[512,1,2048]{2,0,1:T(8,128)(2,1)}, u32[]{:S(2)}) copy-start(bf16[512,1,2048]{2,0,1:T(8,128)(2,1)} %all-gather.9.cloned.1.call-done) | copy-start | bytes 6291460
  158.4 129.0 %reduce-scatter.3.cloned.1.call-start = ((), (), s32[]{:S(2)}) async-start(), calls=%async_computation.7 | async-start | bytes 2359296 | tf_op jit(solution)/shard_map/reduce_scatter | solution.py:217
  194.8 3.5 %copy-start.11 = (bf16[512,1,2048]{2,0,1:T(8,128)(2,1)S(1)}, bf16[512,1,2048]{2,0,1:T(8,128)(2,1)}, u32[]{:S(2)}) copy-start(bf16[512,1,2048]{2,0,1:T(8,128)(2,1)} %all-gather.7.cloned.1.call-done) | copy-start | bytes 6291460
  245.3 61.8 %copy-start.13 = (f32[2048,16]{0,1:T(8,128)S(1)}, f32[2048,16]{0,1:T(8,128)}, u32[]{:S(2)}) copy-start(f32[2048,16]{0,1:T(8,128)} %param.27) | copy-start | bytes 393220
  246.2 45.9 %all-to-all-start.4 = ((bf16[64,2,1024]{2,1,0:T(2,128)(2,1)}), bf16[64,2,1024]{2,1,0:T(2,128)(2,1)S(1)}, u32[]{:S(2)}, u32[]{:S(2)}) async-start(bf16[64,2,1024]{2,1,0:T(2,128)(2,1)} %reshape.276), calls=%async_computation.6 | async-start | bytes 524288 | tf_op jit(solution)/shard_map/all_to_all | solution.py:221
  292.1 27.2 %all-to-all-start.3 = ((bf16[64,2,1024]{2,1,0:T(2,128)(2,1)}), bf16[64,2,1024]{2,1,0:T(2,128)(2,1)S(1)}, u32[]{:S(2)}, u32[]{:S(2)}) async-start(bf16[64,2,1024]{2,1,0:T(2,128)(2,1)} %reshape.278), calls=%async_computation.4 | async-start | bytes 524288 | tf_op jit(solution)/shard_map/all_to_all | solution.py:221
Sparse Core Ops, SparseCore 0:
  116.0 33.8 all-gather.8
  152.0 42.7 all-gather.6
  197.6 43.2 reduce-scatter.4
  243.6 43.7 reduce-scatter.2

commit v6 on v5

--- a/solution.py
+++ b/solution.py
@@ -66,6 +66,18 @@
     doubled = jnp.concatenate([stacked, stacked])
     start = (-offsets[0] - lax.axis_index(axis)) % size
     return lax.dynamic_slice_in_dim(doubled, start, size, 0)
+
+
+def ring_pieces(shard, axis):
+    size = lax.axis_size(axis)
+    forward, backward, pieces = shard, shard, [shard]
+    for step in range(1, size // 2 + 1):
+        forward = lax.ppermute(forward, axis, [(i, (i + 1) % size) for i in range(size)])
+        pieces.append(forward)
+        if step < size - step:
+            backward = lax.ppermute(backward, axis, [(i, (i - 1) % size) for i in range(size)])
+            pieces.append(backward)
+    return pieces
 
 
 def rms_scale(values, gain_vec):
@@ -118,6 +130,9 @@
     experts = lax.axis_size("grp")
     slot_cap = max(2, 4 * block_rows // experts)
     group_slots = experts * slot_cap
+    x_count = lax.axis_size("dev_0")
+    own_w = jnp.stack([gate_weight[0], up_weight[0], down_weight[0].T])
+    expert_w = ring_pieces(own_w, "dev_0")
     inputs_f = ssm_input.astype(jnp.float32).reshape(tok_rows, head_count, head_width)
     in_float = in_coeff.astype(jnp.float32)
     out_float = out_coeff.astype(jnp.float32)
@@ -183,7 +198,9 @@
     payload = jnp.dot(lhs, rhs, preferred_element_type=jnp.float32).astype(jnp.bfloat16)
     landed = lax.all_to_all(
         payload.reshape(dev_count, block_rows, payload.shape[1]), DEV, 0, 0, tiled=True
-    ).astype(jnp.float32)
+    )
+    landed, expert_w = lax.optimization_barrier((landed, expert_w))
+    landed = landed.astype(jnp.float32)
     summed_proj = jnp.sum(landed[:, :, :model_dim], axis=0)
     token_squares = jnp.sum(landed[:, :, model_dim], axis=0)
     mamba_out = (
@@ -205,26 +222,21 @@
     ).astype(jnp.bfloat16)
     outgoing = outgoing.reshape(experts, slot_cap, model_dim)
     arrived = lax.all_to_all(outgoing, "grp", split_axis=0, concat_axis=0, tiled=True)
-    x_count = lax.axis_size("dev_0")
-    halves = []
-    for slot in range(slot_cap):
-        rows = lax.all_gather(arrived[:, slot, :], "dev_0", axis=0, tiled=True)
-        rows = lax.all_gather(rows, "dev_1", axis=0, tiled=True)
-        gate_act = jnp.dot(rows, gate_weight[0], preferred_element_type=jnp.float32)
-        up_act = jnp.dot(rows, up_weight[0], preferred_element_type=jnp.float32)
+    rows = lax.all_gather(arrived.reshape(-1, model_dim), "dev_1", axis=0, tiled=True)
+    partial_down = 0.0
+    for piece in expert_w:
+        gate_act = jnp.dot(rows, piece[0], preferred_element_type=jnp.float32)
+        up_act = jnp.dot(rows, piece[1], preferred_element_type=jnp.float32)
         hidden = (jax.nn.silu(gate_act) * up_act).astype(jnp.bfloat16)
-        partial_down = jnp.dot(hidden, down_weight[0], preferred_element_type=jnp.float32)
-        summed = lax.psum_scatter(
-            partial_down.astype(jnp.bfloat16), "dev_1", scatter_dimension=0, tiled=True
-        )
-        summed = jnp.swapaxes(summed.reshape(x_count, experts, model_dim), 0, 1)
-        landed_back = lax.all_to_all(
-            summed.reshape(experts * x_count, model_dim), ("grp", "dev_0"), 0, 0, tiled=True
-        )
-        halves.append(
-            jnp.sum(landed_back.reshape(experts, x_count, model_dim).astype(jnp.float32), axis=1)
-        )
-    returned = jnp.stack(halves, axis=1)
+        block_out = lax.dot_general(
+            hidden, piece[2], (((1,), (1,)), ((), ())), preferred_element_type=jnp.float32
+        ).astype(jnp.bfloat16)
+        partial_down = partial_down + block_out.astype(jnp.float32)
+    partial_down = partial_down.astype(jnp.bfloat16)
+    summed = lax.psum_scatter(partial_down, "dev_1", scatter_dimension=0, tiled=True)
+    returned = lax.all_to_all(
+        summed.reshape(experts, slot_cap, model_dim), "grp", 0, 0, tiled=True
+    ).astype(jnp.float32)
     weights = first_prob[:, None] * placed[:, 0, :] + second_prob[:, None] * placed[:, 1, :]
     contrib = jnp.dot(
         weights,

time: 330 us -> 326 us (0.988)
  blocking collectives: 63 us -> 48.6 us
  waiting for transfers between devices: 158 us -> 171 us
  matrix products: 21.8 us -> 30.5 us
  other arithmetic: 10.9 us -> 5.78 us
  starting transfers between devices: 50.3 us -> 45.9 us
    all_to_all x1, waiting for transfers between devices: 25.5 us -> 67.1 us  [shards(): lax.all_to_all(payload.reshape(dev_count, block_rows, payload.shape[1]),...]
    all_gather x2 -> x1, waiting for transfers between devices: 59.3 us -> 30.8 us  [shards(): lax.all_gather(arrived.reshape(-1, model_dim), 'dev_1', axis=0, tiled=True)]
    ppermute x0 -> x3, waiting for transfers between devices: none -> 25.1 us  [the longest x2 25.1 us: ring_pieces(): lax.ppermute(forward, axis, [(i, (i + 1) % size) for i in range(size)])]
    reduce_scatter x2 -> x1, waiting for transfers between devices: 63.7 us -> 39.6 us  [shards(): lax.psum_scatter(partial_down, 'dev_1', scatter_dimension=0, tiled=True)]
    all_gather x2 -> x0, blocking collectives: 21.3 us -> none  [shards(): rows = lax.all_gather(arrived[:, slot, :], 'dev_0', axis=0, tiled=True)]
    all_to_all x2 -> x1, starting transfers between devices: 29.9 us -> 12.3 us  [shards(): lax.all_to_all(summed.reshape(experts, slot_cap, model_dim), 'grp', 0, 0,...]
    ppermute x0 -> x3, starting transfers between devices: none -> 14.1 us  [the longest x2 11 us: ring_pieces(): lax.ppermute(forward, axis, [(i, (i + 1) % size) for i in range(size)])]
    dot_general x4 -> x8, matrix products: 17 us -> 25.7 us  [the longest x4 18.5 us: shards(): lax.dot_general(hidden, piece[2], (((1,), (1,)), ((), ())), preferred_ele...]
  transfers between devices with their start and end apart: 8 -> 8, of which waited for: 6 -> 5; matrix products, arithmetic and copies ran while one was open for 11% -> 3% of each run, Pallas kernels for 0% -> 0%
where the time goes in v6:
time: 326 us; the launch traced here: 325 us
  waiting for transfers between devices  171 us (52%)
  blocking collectives  48.6 us (15%)
  starting transfers between devices  45.9 us (14%)
  matrix products  30.5 us (9%)
  between operations  13.9 us (4%)
  local copies, waits for them, and re-layouts  9.27 us (3%)
  other arithmetic  5.78 us (2%)
    all_to_all x1, waiting for transfers between devices, shards(): lax.all_to_all(payload.reshape(dev_count, block_rows, payload.shape[1]),...  67.1 us
    reduce_scatter x1, waiting for transfers between devices, shards(): lax.psum_scatter(partial_down, 'dev_1', scatter_dimension=0, tiled=True)  39.6 us
    all_gather x1, waiting for transfers between devices, shards(): lax.all_gather(arrived.reshape(-1, model_dim), 'dev_1', axis=0, tiled=True)  30.8 us
    all_gather x1, blocking collectives, side_by_side(): lax.all_gather(both, axis, axis=dim, tiled=True)  26 us
    ppermute x2, waiting for transfers between devices, ring_pieces(): lax.ppermute(forward, axis, [(i, (i + 1) % size) for i in range(size)])  25.1 us
    all_to_all x1, blocking collectives, shards(): lax.all_to_all(outgoing, 'grp', split_axis=0, concat_axis=0, tiled=True)  22.6 us
    dot_general x4, matrix products, shards(): lax.dot_general(hidden, piece[2], (((1,), (1,)), ((), ())), preferred_ele...  18.5 us
    all_to_all x1, starting transfers between devices, shards(): lax.all_to_all(summed.reshape(experts, slot_cap, model_dim), 'grp', 0, 0,...  12.3 us
  transfers between devices with their start and end apart: 8, of which 5 were waited for; matrix products, arithmetic and copies ran while one was open for 3% of the time, Pallas kernels for 0%

profile of v6, /device:TPU:1, one launch (start us, length us, event | category | flops | bytes accessed | tf_op | source)
XLA Modules:
  0.0 325.3 jit_solution(568918409340139053)
XLA Ops:
  6.5 1.5 copy.79
  8.1 1.5 copy.78
  9.6 3.3 %pad_maximum_fusion = bf16[3,2048,256]{1,2,0:T(8,128)(2,1)} fusion(bf16[1,2048,256]{1,2,0:T(8,128)(2,1)} %bitcast.124, bf16[1,2048,256]{1,2,0:T(8,128)(2,1)S(1)} %copy.79, bf16[1,2048,256]{1,2,0:T(8,128)(2,1)S(1)} %copy.78), kind=kLoop, calls=%fused_computation.2 | loop fusion | flops 3145728 | bytes 6291456 | tf_op jit(solution)/shard_map/stack | solution.py:134
  12.9 4.1 %collective-permute-start = (bf16[3,2048,256]{1,2,0:T(8,128)(2,1)}, bf16[3,2048,256]{1,2,0:T(8,128)(2,1)}, u32[]{:S(2)}, u32[]{:S(2)}) collective-permute-start(bf16[3,2048,256]{1,2,0:T(8,128)(2,1)} %pad_maximum_fusion), channel_id=1, source_target_pairs={{0,8},{8,16},{16,24},{24,0},{1,9},{9,17},{17,25},{25,1},{2,10},{10... | collective-permute-start | bytes 9437192 | tf_op jit(solution)/shard_map/ppermute | solution.py:75
  16.9 3.2 collective-permute-start.1
  20.1 1.0 copy_bitcast_fusion
  21.1 8.8 %all-to-all-start = ((bf16[32,128,64]{1,2,0:T(8,128)(2,1)}), bf16[32,128,64]{1,2,0:T(8,128)(2,1)S(1)}, u32[]{:S(2)}, u32[]{:S(2)}) async-start(bf16[32,128,64]{1,2,0:T(8,128)(2,1)} %copy_bitcast_fusion), calls=%async_computation | async-start | bytes 1048576 | tf_op jit(solution)/shard_map/all_to_all | solution.py:180
  30.2 0.6 reduce-window.6
  31.9 26.0 %all_gather.6 = bf16[16,2,8193]{2,1,0:T(2,128)(2,1)S(1)} all-gather(bf16[1,2,8193]{2,1,0:T(2,128)(2,1)S(1)} %pad_maximum_fusion.1), channel_id=1, replica_groups=mesh['grp'=16,'dev_0'=4,'dev_1'=8] {'grp'}, dimensions={0}, use_global_device_ids=true | all-gather | bytes 557124 | tf_op jit(solution)/shard_map/all_gather | solution.py:18
  57.8 0.7 slice.96
  60.2 25.1 %collective-permute-done = bf16[3,2048,256]{1,2,0:T(8,128)(2,1)} collective-permute-done((bf16[3,2048,256]{1,2,0:T(8,128)(2,1)}, bf16[3,2048,256]{1,2,0:T(8,128)(2,1)}, u32[]{:S(2)}, u32[]{:S(2)}) %collective-permute-start) | collective-permute-done | bytes 3145760 | tf_op jit(solution)/shard_map/ppermute | solution.py:75
  85.3 6.9 %collective-permute-start.2 = (bf16[3,2048,256]{1,2,0:T(8,128)(2,1)}, bf16[3,2048,256]{1,2,0:T(8,128)(2,1)}, u32[]{:S(2)}, u32[]{:S(2)}) collective-permute-start(bf16[3,2048,256]{1,2,0:T(8,128)(2,1)} %collective-permute-done), channel_id=1, source_target_pairs={{0,8},{8,16},{16,24},{24,0},{1,9},{9,17},{17,25},{25,1},{2,10},{10... | collective-permute-start | bytes 9437192 | tf_op jit(solution)/shard_map/ppermute | solution.py:75
  92.5 0.6 fusion.16
  93.7 1.6 fusion
  95.3 10.4 %all-to-all-start.1 = ((bf16[32,8,2176]{2,1,0:T(8,128)(2,1)}), bf16[32,8,2176]{2,1,0:T(8,128)(2,1)S(1)}, u32[]{:S(2)}, u32[]{:S(2)}) async-start(bf16[32,8,2176]{2,1,0:T(8,128)(2,1)} %fusion), calls=%async_computation.1 | async-start | bytes 2228224 | tf_op jit(solution)/shard_map/all_to_all | solution.py:199
  106.5 67.1 %all-to-all-done.1 = bf16[32,8,2176]{2,1,0:T(8,128)(2,1)S(1)} async-done(((bf16[32,8,2176]{2,1,0:T(8,128)(2,1)}), bf16[32,8,2176]{2,1,0:T(8,128)(2,1)S(1)}, u32[]{:S(2)}, u32[]{:S(2)}) %all-to-all-start.1) | async-done | bytes 1114144 | tf_op jit(solution)/shard_map/all_to_all | solution.py:199
  174.5 22.6 %all_to_all.20 = bf16[16,2,2048]{2,1,0:T(2,128)(2,1)S(1)} all-to-all(bf16[16,2,2048]{2,1,0:T(2,128)(2,1)S(1)} %reshape.241), channel_id=1, replica_groups=mesh['grp'=16,'dev_0'=4,'dev_1'=8] {'grp'}, dimensions={0} | all-to-all | bytes 262144 | tf_op jit(solution)/shard_map/all_to_all | solution.py:224
  197.2 0.7 reshape.242
  198.1 30.8 %all-gather.2.cloned.1.call-done = bf16[256,2048]{1,0:T(8,128)(2,1)} async-done(((bf16[32,2048]{1,0:T(8,128)(2,1)}), bf16[256,2048]{1,0:T(8,128)(2,1)}) %all-gather.2.cloned.1.call-update) | async-done | bytes 1048592 | tf_op jit(solution)/shard_map/all_gather | solution.py:225
  228.9 2.1 fusion.26
  231.0 4.2 %fusion.8 = f32[256,2048]{1,0:T(8,128)} fusion(bf16[256,2048]{1,0:T(8,128)(2,1)S(1)} %copy-done.1, bf16[3,2048,256]{1,2,0:T(8,128)(2,1)} %collective-permute-done.2, f32[256,256]{1,0:T(8,128)S(1)} %fusion.26), kind=kOutput, calls=%fused_computation.14 | convolution fusion | flops 538312704 | bytes 5505024 | tf_op jit(solution)/shard_map/dot_general | solution.py:231
  235.2 1.7 fusion.31
  236.9 4.2 %fusion.7 = f32[256,2048]{1,0:T(8,128)} fusion(bf16[256,2048]{1,0:T(8,128)(2,1)S(1)} %copy-done.1, bf16[3,2048,256]{1,2,0:T(8,128)(2,1)} %collective-permute-done.1, f32[256,256]{1,0:T(8,128)S(1)} %fusion.31), kind=kOutput, calls=%fused_computation.13 | convolution fusion | flops 538312704 | bytes 5505024 | tf_op jit(solution)/shard_map/dot_general | solution.py:231
  241.1 1.7 fusion.36
  242.8 4.2 %fusion.6 = f32[256,2048]{1,0:T(8,128)} fusion(bf16[256,2048]{1,0:T(8,128)(2,1)S(1)} %copy-done.1, bf16[3,2048,256]{1,2,0:T(8,128)(2,1)} %collective-permute-done, f32[256,256]{1,0:T(8,128)S(1)} %fusion.36), kind=kOutput, calls=%fused_computation.12 | convolution fusion | flops 538312704 | bytes 5505024 | tf_op jit(solution)/shard_map/dot_general | solution.py:231
  247.0 1.7 fusion.41
  248.7 5.9 %fusion.5 = bf16[256,2048]{1,0:T(8,128)(2,1)} fusion(f32[256,2048]{1,0:T(8,128)} %fusion.8, f32[256,2048]{1,0:T(8,128)} %fusion.7, f32[256,2048]{1,0:T(8,128)} %fusion.6, bf16[256,2048]{1,0:T(8,128)(2,1)S(1)} %copy-done.1, bf16[3,2048,256]{1,2,0:T(8,128)(2,1)} %pad_maximum_fusion, f32[256,256]{1,0:T(8,128)S(1)} %fusion.41), kind=kOutput, calls=%fused_computation.11 | convolution fusion | flops 540409856 | bytes 10747904 | tf_op jit(solution)/shard_map/dot_general | solution.py:231
  254.7 39.6 %reduce-scatter.2.cloned.1.call-done = bf16[32,2048]{1,0:T(8,128)(2,1)} async-done(((bf16[256,2048]{1,0:T(8,128)(2,1)}), bf16[32,2048]{1,0:T(8,128)(2,1)}) %reduce-scatter.2.cloned.1.call-update) | async-done | bytes 131088 | tf_op jit(solution)/shard_map/reduce_scatter | solution.py:236
  294.4 1.7 reshape.243
  296.0 12.3 %all-to-all-start.3 = ((bf16[16,2,2048]{2,1,0:T(2,128)(2,1)}), bf16[16,2,2048]{2,1,0:T(2,128)(2,1)S(1)}, u32[]{:S(2)}, u32[]{:S(2)}) async-start(bf16[16,2,2048]{2,1,0:T(2,128)(2,1)} %reshape.243), calls=%async_computation.4 | async-start | bytes 262144 | tf_op jit(solution)/shard_map/all_to_all | solution.py:237
  308.7 8.8 %all-to-all-done.3 = bf16[16,2,2048]{2,1,0:T(2,128)(2,1)S(1)} async-done(((bf16[16,2,2048]{2,1,0:T(2,128)(2,1)}), bf16[16,2,2048]{2,1,0:T(2,128)(2,1)S(1)}, u32[]{:S(2)}, u32[]{:S(2)}) %all-to-all-start.3) | async-done | bytes 131104 | tf_op jit(solution)/shard_map/all_to_all | solution.py:237
  317.6 0.9 fusion.10
  (89 shorter events, 6.2 us)
Async XLA Ops:
  6.5 13.6 %copy-start = (bf16[4096,64]{0,1:T(8,128)(2,1)S(1)}, bf16[4096,64]{0,1:T(8,128)(2,1)}, u32[]{:S(2)}) copy-start(bf16[4096,64]{0,1:T(8,128)(2,1)} %param.24) | copy-start | bytes 1572868
  9.6 20.3 %copy-start.5 = (bf16[256,128]{1,0:T(8,128)(2,1)S(1)}, bf16[256,128]{1,0:T(8,128)(2,1)}, u32[]{:S(2)}) copy-start(bf16[256,128]{1,0:T(8,128)(2,1)} %param.16) | copy-start | bytes 196612
  12.9 17.2 %copy-start.8 = (f32[256,2]{0,1:T(2,128)S(1)}, f32[256,2]{0,1:T(2,128)}, u32[]{:S(2)}) copy-start(f32[256,2]{0,1:T(2,128)} %param.18) | copy-start | bytes 6148
  12.9 17.2 %copy-start.11 = (f32[2]{0:T(128)S(1)}, f32[2]{0:T(128)}, u32[]{:S(2)}) copy-start(f32[2]{0:T(128)} %param.19) | copy-start | bytes 28
  12.9 18.6 %copy-start.2 = (bf16[256,128]{1,0:T(8,128)(2,1)S(1)}, bf16[256,128]{1,0:T(8,128)(2,1)}, u32[]{:S(2)}) copy-start(bf16[256,128]{1,0:T(8,128)(2,1)} %param.20) | copy-start | bytes 196612
  12.9 72.5 %collective-permute-start = (bf16[3,2048,256]{1,2,0:T(8,128)(2,1)}, bf16[3,2048,256]{1,2,0:T(8,128)(2,1)}, u32[]{:S(2)}, u32[]{:S(2)}) collective-permute-start(bf16[3,2048,256]{1,2,0:T(8,128)(2,1)} %pad_maximum_fusion), channel_id=1, source_target_pairs={{0,8},{8,16},{16,24},{24,0},{1,9},{9,17},{17,25},{25,1},{2,10},{10... | collective-permute-start | bytes 9437192 | tf_op jit(solution)/shard_map/ppermute | solution.py:75
  16.9 89.5 %collective-permute-start.1 = (bf16[3,2048,256]{1,2,0:T(8,128)(2,1)}, bf16[3,2048,256]{1,2,0:T(8,128)(2,1)}, u32[]{:S(2)}, u32[]{:S(2)}) collective-permute-start(bf16[3,2048,256]{1,2,0:T(8,128)(2,1)} %pad_maximum_fusion), channel_id=1, source_target_pairs={{0,24},{8,0},{16,8},{24,16},{1,25},{9,1},{17,9},{25,17},{2,26},{10... | collective-permute-start | bytes 9437192 | tf_op jit(solution)/shard_map/ppermute | solution.py:78
  21.1 38.3 %copy-start.3 = (bf16[256,128]{1,0:T(8,128)(2,1)S(1)}, bf16[256,128]{1,0:T(8,128)(2,1)}, u32[]{:S(2)}) copy-start(bf16[256,128]{1,0:T(8,128)(2,1)} %param.21) | copy-start | bytes 196612
  21.1 72.2 %all-to-all-start = ((bf16[32,128,64]{1,2,0:T(8,128)(2,1)}), bf16[32,128,64]{1,2,0:T(8,128)(2,1)S(1)}, u32[]{:S(2)}, u32[]{:S(2)}) async-start(bf16[32,128,64]{1,2,0:T(8,128)(2,1)} %copy_bitcast_fusion), calls=%async_computation | async-start | bytes 1048576 | tf_op jit(solution)/shard_map/all_to_all | solution.py:180
  30.1 62.4 %copy-start.13 = (f32[2]{0:T(128)S(1)}, f32[2]{0:T(128)}, u32[]{:S(2)}) copy-start(f32[2]{0:T(128)} %param.22) | copy-start | bytes 28
  58.5 34.7 %copy-start.4 = (bf16[256,128]{1,0:T(8,128)(2,1)S(1)}, bf16[256,128]{1,0:T(8,128)(2,1)}, u32[]{:S(2)}) copy-start(bf16[256,128]{1,0:T(8,128)(2,1)} %param.17) | copy-start | bytes 196612
  58.5 34.7 %copy-start.10 = (f32[128]{0:T(128)S(1)}, f32[128]{0:T(128)}, u32[]{:S(2)}) copy-start(f32[128]{0:T(128)} %param.23) | copy-start | bytes 1540
  85.3 88.2 %collective-permute-start.2 = (bf16[3,2048,256]{1,2,0:T(8,128)(2,1)}, bf16[3,2048,256]{1,2,0:T(8,128)(2,1)}, u32[]{:S(2)}, u32[]{:S(2)}) collective-permute-start(bf16[3,2048,256]{1,2,0:T(8,128)(2,1)} %collective-permute-done), channel_id=1, source_target_pairs={{0,8},{8,16},{16,24},{24,0},{1,9},{9,17},{17,25},{25,1},{2,10},{10... | collective-permute-start | bytes 9437192 | tf_op jit(solution)/shard_map/ppermute | solution.py:75
  93.7 12.1 %copy-start.9 = (s32[8,2]{0,1:T(2,128)S(1)}, s32[8,2]{0,1:T(2,128)}, u32[]{:S(2)}) copy-start(s32[8,2]{0,1:T(2,128)} %param.28) | copy-start | bytes 196
  95.3 78.3 %all-to-all-start.1 = ((bf16[32,8,2176]{2,1,0:T(8,128)(2,1)}), bf16[32,8,2176]{2,1,0:T(8,128)(2,1)S(1)}, u32[]{:S(2)}, u32[]{:S(2)}) async-start(bf16[32,8,2176]{2,1,0:T(8,128)(2,1)} %fusion), calls=%async_computation.1 | async-start | bytes 2228224 | tf_op jit(solution)/shard_map/all_to_all | solution.py:199
  105.7 123.2 %all-gather.2.cloned.1.call-start = ((), (), s32[]{:S(2)}) async-start(), calls=%async_computation.5 | async-start | bytes 1179648 | tf_op jit(solution)/shard_map/all_gather | solution.py:225
  106.5 67.5 %copy-start.6 = (bf16[8,2048]{1,0:T(8,128)(2,1)S(1)}, bf16[8,2048]{1,0:T(8,128)(2,1)}, u32[]{:S(2)}) copy-start(bf16[8,2048]{1,0:T(8,128)(2,1)} %param.25) | copy-start | bytes 98308
  106.5 67.7 %copy-start.7 = (f32[2048]{0:T(1024)S(1)}, f32[2048]{0:T(1024)}, u32[]{:S(2)}) copy-start(f32[2048]{0:T(1024)} %param.26) | copy-start | bytes 24580
  197.9 96.5 %reduce-scatter.2.cloned.1.call-start = ((), (), s32[]{:S(2)}) async-start(), calls=%async_computation.6 | async-start | bytes 1179648 | tf_op jit(solution)/shard_map/reduce_scatter | solution.py:236
  228.9 2.1 copy-start.1
  248.7 59.6 %copy-start.12 = (f32[2048,16]{0,1:T(8,128)S(1)}, f32[2048,16]{0,1:T(8,128)}, u32[]{:S(2)}) copy-start(f32[2048,16]{0,1:T(8,128)} %param.27) | copy-start | bytes 393220
  296.0 21.5 %all-to-all-start.3 = ((bf16[16,2,2048]{2,1,0:T(2,128)(2,1)}), bf16[16,2,2048]{2,1,0:T(2,128)(2,1)S(1)}, u32[]{:S(2)}, u32[]{:S(2)}) async-start(bf16[16,2,2048]{2,1,0:T(2,128)(2,1)} %reshape.243), calls=%async_computation.4 | async-start | bytes 262144 | tf_op jit(solution)/shard_map/all_to_all | solution.py:237
Sparse Core Ops, SparseCore 0:
  198.0 30.8 all-gather.1
  254.8 39.5 reduce-scatter.1

commit v7 on v4

--- a/solution.py
+++ b/solution.py
@@ -208,9 +208,14 @@
     all_rows = arrived.reshape(-1, model_dim)
     all_rows = lax.all_gather(all_rows, "dev_0", axis=0, tiled=True)
     all_rows = lax.all_gather(all_rows, "dev_1", axis=0, tiled=True)
-    gate_act = jnp.dot(all_rows, gate_weight[0], preferred_element_type=jnp.float32)
-    up_act = jnp.dot(all_rows, up_weight[0], preferred_element_type=jnp.float32)
-    hidden = (jax.nn.silu(gate_act) * up_act).astype(jnp.bfloat16)
+    hid_units = gate_weight.shape[2]
+    both_act = jnp.dot(
+        all_rows,
+        jnp.concatenate([gate_weight[0], up_weight[0]], axis=1),
+        preferred_element_type=jnp.float32,
+    )
+    hidden = (jax.nn.silu(both_act[:, :hid_units]) * both_act[:, hid_units:]).astype(jnp.bfloat16)
+    hidden = lax.optimization_barrier(hidden)
     partial_down = jnp.dot(hidden, down_weight[0], preferred_element_type=jnp.float32)
     summed = lax.psum_scatter(
         partial_down.astype(jnp.bfloat16), "dev_1", scatter_dimension=0, tiled=True

time: 280 us -> 275 us (0.982)
  matrix products: 18.1 us -> 12.8 us
    dot_general x1, matrix products: 8.8 us -> 3.19 us  [shards(): jnp.dot(hidden, down_weight[0], preferred_element_type=jnp.float32)]
where the time goes in v7:
time: 275 us; the launch traced here: 274 us
  waiting for transfers between devices  150 us (55%)
  blocking collectives  53.6 us (19%)
  starting transfers between devices  31.2 us (11%)
  between operations  13.8 us (5%)
  matrix products  12.8 us (5%)
  local copies, waits for them, and re-layouts  8.66 us (3%)
  other arithmetic  4.02 us (1%)
    reduce_scatter x1, waiting for transfers between devices, shards(): lax.psum_scatter(partial_down.astype(jnp.bfloat16), 'dev_1', scatter_dime...  56.8 us
    all_gather x1, waiting for transfers between devices, shards(): all_rows = lax.all_gather(all_rows, 'dev_1', axis=0, tiled=True)  51 us
    all_to_all x1, waiting for transfers between devices, shards(): lax.all_to_all(payload.reshape(dev_count, block_rows, payload.shape[1]),...  25.5 us
    all_gather x1, blocking collectives, side_by_side(): lax.all_gather(both, axis, axis=dim, tiled=True)  25.4 us
    all_to_all x1, waiting for transfers between devices, shards(): lax.all_to_all(summed.reshape(experts * x_count, slot_cap, model_dim), ('...  16.8 us
    all_to_all x1, blocking collectives, shards(): lax.all_to_all(outgoing, 'grp', split_axis=0, concat_axis=0, tiled=True)  16.3 us
    all_gather x1, blocking collectives, shards(): all_rows = lax.all_gather(all_rows, 'dev_0', axis=0, tiled=True)  11.8 us
    all_to_all x1, starting transfers between devices, shards(): lax.all_to_all(summed.reshape(experts * x_count, slot_cap, model_dim), ('...  11 us
  transfers between devices with their start and end apart: 5, of which 4 were waited for; matrix products, arithmetic and copies ran while one was open for 3% of the time, Pallas kernels for 0%

profile of v7, /device:TPU:1, one launch (start us, length us, event | category | flops | bytes accessed | tf_op | source)
XLA Modules:
  0.0 274.1 jit_solution(155404555594883410)
XLA Ops:
  6.5 2.1 copy_bitcast_fusion
  8.6 10.6 %all-to-all-start = ((bf16[32,128,64]{1,2,0:T(8,128)(2,1)}), bf16[32,128,64]{1,2,0:T(8,128)(2,1)S(1)}, u32[]{:S(2)}, u32[]{:S(2)}) async-start(bf16[32,128,64]{1,2,0:T(8,128)(2,1)} %copy_bitcast_fusion), calls=%async_computation | async-start | bytes 1048576 | tf_op jit(solution)/shard_map/all_to_all | solution.py:165
  19.2 0.8 negate_bitcast_fusion
  20.0 0.6 reduce-window.6
  21.3 0.9 copy.65
  22.4 0.2 convolution_convert_fusion.3
  22.7 25.4 %all_gather.9 = bf16[16,2,8193]{2,1,0:T(2,128)(2,1)S(1)} all-gather(bf16[1,2,8193]{2,1,0:T(2,128)(2,1)S(1)} %pad_maximum_fusion), channel_id=1, replica_groups=mesh['grp'=16,'dev_0'=4,'dev_1'=8] {'grp'}, dimensions={0}, use_global_device_ids=true | all-gather | bytes 557124 | tf_op jit(solution)/shard_map/all_gather | solution.py:18
  48.1 0.7 slice.56
  49.3 0.4 reshape.242
  49.7 0.6 fusion.18
  50.3 0.2 fusion.9
  50.8 0.6 fusion.8
  51.6 0.3 concatenate.28
  52.0 1.5 fusion
  53.5 9.5 %all-to-all-start.1 = ((bf16[32,8,2176]{2,1,0:T(8,128)(2,1)}), bf16[32,8,2176]{2,1,0:T(8,128)(2,1)S(1)}, u32[]{:S(2)}, u32[]{:S(2)}) async-start(bf16[32,8,2176]{2,1,0:T(8,128)(2,1)} %fusion), calls=%async_computation.1 | async-start | bytes 2228224 | tf_op jit(solution)/shard_map/all_to_all | solution.py:184
  63.8 25.5 %all-to-all-done.1 = bf16[32,8,2176]{2,1,0:T(8,128)(2,1)S(1)} async-done(((bf16[32,8,2176]{2,1,0:T(8,128)(2,1)}), bf16[32,8,2176]{2,1,0:T(8,128)(2,1)S(1)}, u32[]{:S(2)}, u32[]{:S(2)}) %all-to-all-start.1) | async-done | bytes 1114144 | tf_op jit(solution)/shard_map/all_to_all | solution.py:184
  89.7 0.2 fusion.39
  89.9 0.2 convolution_convert_fusion.2
  90.3 16.3 %all_to_all.20 = bf16[16,2,2048]{2,1,0:T(2,128)(2,1)S(1)} all-to-all(bf16[16,2,2048]{2,1,0:T(2,128)(2,1)S(1)} %reshape.247), channel_id=1, replica_groups=mesh['grp'=16,'dev_0'=4,'dev_1'=8] {'grp'}, dimensions={0} | all-to-all | bytes 262144 | tf_op jit(solution)/shard_map/all_to_all | solution.py:207
  106.7 11.8 %all_gather.10 = bf16[128,2048]{1,0:T(8,128)(2,1)} all-gather(bf16[32,2048]{1,0:T(8,128)(2,1)S(1)} %reshape.248), channel_id=1, replica_groups=mesh['grp'=16,'dev_0'=4,'dev_1'=8] {'dev_0'}, dimensions={0}, use_global_device_ids=true | all-gather | bytes 655360 | tf_op jit(solution)/shard_map/all_gather | solution.py:209
  118.6 51.0 %all-gather.2.cloned.1.call-done = bf16[1024,2048]{1,0:T(8,128)(2,1)} async-done(((bf16[128,2048]{1,0:T(8,128)(2,1)}), bf16[1024,2048]{1,0:T(8,128)(2,1)}) %all-gather.2.cloned.1.call-update) | async-done | bytes 4194320 | tf_op jit(solution)/shard_map/all_gather | solution.py:210
  169.5 4.8 %fusion.3 = f32[1024,512]{1,0:T(8,128)S(1)} fusion(bf16[1024,2048]{1,0:T(8,128)(2,1)} %all-gather.2.cloned.1.call-done, bf16[2048,256]{1,0:T(8,128)(2,1)S(1)} %bitcast.93, bf16[2048,256]{1,0:T(8,128)(2,1)} %bitcast.94), kind=kOutput, calls=%fused_computation.9 | convolution fusion | flops 2151677952 | bytes 8388608 | tf_op jit(solution)/shard_map/dot_general | solution.py:212
  174.4 0.3 fusion.15
  174.7 3.2 %convolution_convert_fusion.1 = bf16[1024,2048]{1,0:T(8,128)(2,1)} fusion(bf16[1024,256]{1,0:T(8,128)(2,1)S(1)} %fusion.15, bf16[1,256,2048]{2,1,0:T(8,128)(2,1)S(1)} %copy-done), kind=kOutput, calls=%fused_computation.1 | convolution fusion | flops 1075838976 | bytes 5767168 | tf_op jit(solution)/shard_map/dot_general | solution.py:219
  177.9 56.8 %reduce-scatter.2.cloned.1.call-done = bf16[128,2048]{1,0:T(8,128)(2,1)} async-done(((bf16[1024,2048]{1,0:T(8,128)(2,1)}), bf16[128,2048]{1,0:T(8,128)(2,1)}) %reduce-scatter.2.cloned.1.call-update) | async-done | bytes 524304 | tf_op jit(solution)/shard_map/reduce_scatter | solution.py:220
  234.8 1.4 reshape.249
  236.2 1.3 copy.75
  237.4 11.0 %all-to-all-start.3 = ((bf16[64,2,2048]{2,1,0:T(2,128)(2,1)}), bf16[64,2,2048]{2,1,0:T(2,128)(2,1)S(1)}, u32[]{:S(2)}, u32[]{:S(2)}) async-start(bf16[64,2,2048]{2,1,0:T(2,128)(2,1)} %bitcast.24), calls=%async_computation.4 | async-start | bytes 1048576 | tf_op jit(solution)/shard_map/all_to_all | solution.py:225
  248.5 0.3 select_reduce_fusion.2
  248.9 16.8 %all-to-all-done.3 = bf16[64,2,2048]{2,1,0:T(2,128)(2,1)S(1)} async-done(((bf16[64,2,2048]{2,1,0:T(2,128)(2,1)}), bf16[64,2,2048]{2,1,0:T(2,128)(2,1)S(1)}, u32[]{:S(2)}, u32[]{:S(2)}) %all-to-all-start.3) | async-done | bytes 524320 | tf_op jit(solution)/shard_map/all_to_all | solution.py:225
  265.7 0.5 convert_reduce_fusion
  266.4 0.9 fusion.2
  (74 shorter events, 3.5 us)
Async XLA Ops:
  6.5 168.2 %copy-start = (bf16[1,256,2048]{2,1,0:T(8,128)(2,1)S(1)}, bf16[1,256,2048]{2,1,0:T(8,128)(2,1)}, u32[]{:S(2)}) copy-start(bf16[1,256,2048]{2,1,0:T(8,128)(2,1)} %param.31) | copy-start | bytes 3145732
  6.5 15.7 %copy-start.6 = (f32[256,2]{0,1:T(2,128)S(1)}, f32[256,2]{0,1:T(2,128)}, u32[]{:S(2)}) copy-start(f32[256,2]{0,1:T(2,128)} %param.18) | copy-start | bytes 6148
  6.5 15.8 %copy-start.1 = (bf16[256,128]{1,0:T(8,128)(2,1)S(1)}, bf16[256,128]{1,0:T(8,128)(2,1)}, u32[]{:S(2)}) copy-start(bf16[256,128]{1,0:T(8,128)(2,1)} %param.20) | copy-start | bytes 196612
  8.6 41.7 %copy-start.2 = (bf16[256,128]{1,0:T(8,128)(2,1)S(1)}, bf16[256,128]{1,0:T(8,128)(2,1)}, u32[]{:S(2)}) copy-start(bf16[256,128]{1,0:T(8,128)(2,1)} %param.21) | copy-start | bytes 196612
  8.6 43.0 %all-to-all-start = ((bf16[32,128,64]{1,2,0:T(8,128)(2,1)}), bf16[32,128,64]{1,2,0:T(8,128)(2,1)S(1)}, u32[]{:S(2)}, u32[]{:S(2)}) async-start(bf16[32,128,64]{1,2,0:T(8,128)(2,1)} %copy_bitcast_fusion), calls=%async_computation | async-start | bytes 1048576 | tf_op jit(solution)/shard_map/all_to_all | solution.py:165
  22.3 28.5 %copy-start.11 = (f32[2]{0:T(128)S(1)}, f32[2]{0:T(128)}, u32[]{:S(2)}) copy-start(f32[2]{0:T(128)} %param.22) | copy-start | bytes 28
  48.8 2.7 copy-start.3
  48.8 2.7 copy-start.8
  52.0 11.1 %copy-start.7 = (s32[8,2]{0,1:T(2,128)S(1)}, s32[8,2]{0,1:T(2,128)}, u32[]{:S(2)}) copy-start(s32[8,2]{0,1:T(2,128)} %param.28) | copy-start | bytes 196
  53.5 35.8 %all-to-all-start.1 = ((bf16[32,8,2176]{2,1,0:T(8,128)(2,1)}), bf16[32,8,2176]{2,1,0:T(8,128)(2,1)S(1)}, u32[]{:S(2)}, u32[]{:S(2)}) async-start(bf16[32,8,2176]{2,1,0:T(8,128)(2,1)} %fusion), calls=%async_computation.1 | async-start | bytes 2228224 | tf_op jit(solution)/shard_map/all_to_all | solution.py:184
  63.0 106.5 %all-gather.2.cloned.1.call-start = ((), (), s32[]{:S(2)}) async-start(), calls=%async_computation.5 | async-start | bytes 4718592 | tf_op jit(solution)/shard_map/all_gather | solution.py:210
  63.8 25.9 %copy-start.4 = (bf16[8,2048]{1,0:T(8,128)(2,1)S(1)}, bf16[8,2048]{1,0:T(8,128)(2,1)}, u32[]{:S(2)}) copy-start(bf16[8,2048]{1,0:T(8,128)(2,1)} %param.25) | copy-start | bytes 98308
  63.8 26.1 %copy-start.5 = (f32[2048]{0:T(1024)S(1)}, f32[2048]{0:T(1024)}, u32[]{:S(2)}) copy-start(f32[2048]{0:T(1024)} %param.26) | copy-start | bytes 24580
  89.4 80.1 %copy-start.9 = (bf16[1,2048,256]{2,1,0:T(8,128)(2,1)S(1)}, bf16[1,2048,256]{2,1,0:T(8,128)(2,1)}, u32[]{:S(2)}) copy-start(bf16[1,2048,256]{2,1,0:T(8,128)(2,1)} %param.30) | copy-start | bytes 3145732
  118.5 116.3 %reduce-scatter.2.cloned.1.call-start = ((), (), s32[]{:S(2)}) async-start(), calls=%async_computation.6 | async-start | bytes 4718592 | tf_op jit(solution)/shard_map/reduce_scatter | solution.py:220
  177.9 70.6 %copy-start.10 = (f32[2048,16]{0,1:T(8,128)S(1)}, f32[2048,16]{0,1:T(8,128)}, u32[]{:S(2)}) copy-start(f32[2048,16]{0,1:T(8,128)} %param.27) | copy-start | bytes 393220
  237.4 28.2 %all-to-all-start.3 = ((bf16[64,2,2048]{2,1,0:T(2,128)(2,1)}), bf16[64,2,2048]{2,1,0:T(2,128)(2,1)S(1)}, u32[]{:S(2)}, u32[]{:S(2)}) async-start(bf16[64,2,2048]{2,1,0:T(2,128)(2,1)} %bitcast.24), calls=%async_computation.4 | async-start | bytes 1048576 | tf_op jit(solution)/shard_map/all_to_all | solution.py:225
Sparse Core Ops, SparseCore 0:
  118.6 50.8 all-gather.1
  178.0 56.6 reduce-scatter.1

commit v8 on v7

--- a/solution.py
+++ b/solution.py
@@ -204,10 +204,12 @@
         filled.T.astype(jnp.bfloat16), normed, preferred_element_type=jnp.float32
     ).astype(jnp.bfloat16)
     outgoing = outgoing.reshape(experts, slot_cap, model_dim)
-    arrived = lax.all_to_all(outgoing, "grp", split_axis=0, concat_axis=0, tiled=True)
-    all_rows = arrived.reshape(-1, model_dim)
-    all_rows = lax.all_gather(all_rows, "dev_0", axis=0, tiled=True)
-    all_rows = lax.all_gather(all_rows, "dev_1", axis=0, tiled=True)
+    x_count = lax.axis_size("dev_0")
+    outgoing = jnp.broadcast_to(outgoing[:, None], (experts, x_count, slot_cap, model_dim))
+    arrived = lax.all_to_all(
+        outgoing.reshape(experts * x_count, slot_cap, model_dim), ("grp", "dev_0"), 0, 0, tiled=True
+    )
+    all_rows = lax.all_gather(arrived.reshape(-1, model_dim), "dev_1", axis=0, tiled=True)
     hid_units = gate_weight.shape[2]
     both_act = jnp.dot(
         all_rows,
@@ -220,8 +222,6 @@
     summed = lax.psum_scatter(
         partial_down.astype(jnp.bfloat16), "dev_1", scatter_dimension=0, tiled=True
     )
-    x_count = lax.axis_size("dev_0")
-    summed = jnp.swapaxes(summed.reshape(x_count, experts, slot_cap, model_dim), 0, 1)
     landed_back = lax.all_to_all(
         summed.reshape(experts * x_count, slot_cap, model_dim), ("grp", "dev_0"), 0, 0, tiled=True
     )

time: 275 us -> 273 us (level)
  blocking collectives: 53.6 us -> 50.6 us
    all_gather x1 -> x0, blocking collectives: 11.8 us -> none  [shards(): all_rows = lax.all_gather(all_rows, 'dev_0', axis=0, tiled=True)]
    all_to_all x1, blocking collectives: 16.3 us -> 25.2 us  [shards(): lax.all_to_all(outgoing.reshape(experts * x_count, slot_cap, model_dim),...]
where the time goes in v8:
time: 273 us; the launch traced here: 272 us
  waiting for transfers between devices  151 us (55%)
  blocking collectives  50.6 us (19%)
  starting transfers between devices  31.2 us (11%)
  between operations  13.8 us (5%)
  matrix products  12.8 us (5%)
  local copies, waits for them, and re-layouts  9.4 us (3%)
  other arithmetic  4.02 us (1%)
    reduce_scatter x1, waiting for transfers between devices, shards(): lax.psum_scatter(partial_down.astype(jnp.bfloat16), 'dev_1', scatter_dime...  56.9 us
    all_gather x1, waiting for transfers between devices, shards(): lax.all_gather(arrived.reshape(-1, model_dim), 'dev_1', axis=0, tiled=True)  51.4 us
    all_to_all x1, waiting for transfers between devices, shards(): lax.all_to_all(payload.reshape(dev_count, block_rows, payload.shape[1]),...  25.5 us
    all_gather x1, blocking collectives, side_by_side(): lax.all_gather(both, axis, axis=dim, tiled=True)  25.4 us
    all_to_all x1, blocking collectives, shards(): lax.all_to_all(outgoing.reshape(experts * x_count, slot_cap, model_dim),...  25.2 us
    all_to_all x1, waiting for transfers between devices, shards(): lax.all_to_all(summed.reshape(experts * x_count, slot_cap, model_dim), ('...  16.8 us
    all_to_all x1, starting transfers between devices, shards(): lax.all_to_all(summed.reshape(experts * x_count, slot_cap, model_dim), ('...  11 us
    all_to_all x1, starting transfers between devices, shards(): lax.all_to_all(out_proj.reshape(dev_count, -1, out_proj.shape[1]), DEV, 0...  10.6 us
  transfers between devices with their start and end apart: 5, of which 4 were waited for; matrix products, arithmetic and copies ran while one was open for 3% of the time, Pallas kernels for 0%

profile of v8, /device:TPU:1, one launch (start us, length us, event | category | flops | bytes accessed | tf_op | source)
XLA Modules:
  0.0 272.3 jit_solution(17784014850709647600)
XLA Ops:
  6.5 2.1 copy_bitcast_fusion
  8.6 10.6 %all-to-all-start = ((bf16[32,128,64]{1,2,0:T(8,128)(2,1)}), bf16[32,128,64]{1,2,0:T(8,128)(2,1)S(1)}, u32[]{:S(2)}, u32[]{:S(2)}) async-start(bf16[32,128,64]{1,2,0:T(8,128)(2,1)} %copy_bitcast_fusion), calls=%async_computation | async-start | bytes 1048576 | tf_op jit(solution)/shard_map/all_to_all | solution.py:165
  19.2 0.8 negate_bitcast_fusion
  20.0 0.6 reduce-window.6
  21.3 0.9 copy.61
  22.4 0.2 convolution_convert_fusion.3
  22.7 25.4 %all_gather.6 = bf16[16,2,8193]{2,1,0:T(2,128)(2,1)S(1)} all-gather(bf16[1,2,8193]{2,1,0:T(2,128)(2,1)S(1)} %pad_maximum_fusion), channel_id=1, replica_groups=mesh['grp'=16,'dev_0'=4,'dev_1'=8] {'grp'}, dimensions={0}, use_global_device_ids=true | all-gather | bytes 557124 | tf_op jit(solution)/shard_map/all_gather | solution.py:18
  48.1 0.7 slice.56
  49.3 0.4 reshape.240
  49.7 0.6 fusion.18
  50.3 0.2 fusion.9
  50.8 0.6 fusion.8
  51.6 0.3 concatenate.28
  52.0 1.5 fusion
  53.5 9.5 %all-to-all-start.1 = ((bf16[32,8,2176]{2,1,0:T(8,128)(2,1)}), bf16[32,8,2176]{2,1,0:T(8,128)(2,1)S(1)}, u32[]{:S(2)}, u32[]{:S(2)}) async-start(bf16[32,8,2176]{2,1,0:T(8,128)(2,1)} %fusion), calls=%async_computation.1 | async-start | bytes 2228224 | tf_op jit(solution)/shard_map/all_to_all | solution.py:184
  63.8 25.5 %all-to-all-done.1 = bf16[32,8,2176]{2,1,0:T(8,128)(2,1)S(1)} async-done(((bf16[32,8,2176]{2,1,0:T(8,128)(2,1)}), bf16[32,8,2176]{2,1,0:T(8,128)(2,1)S(1)}, u32[]{:S(2)}, u32[]{:S(2)}) %all-to-all-start.1) | async-done | bytes 1114144 | tf_op jit(solution)/shard_map/all_to_all | solution.py:184
  89.7 0.2 fusion.39
  89.9 0.2 convolution_convert_fusion.2
  90.3 0.3 broadcast_in_dim.79
  90.6 25.2 %all_to_all.20 = bf16[64,2,2048]{2,1,0:T(2,128)(2,1)S(1)} all-to-all(bf16[64,2,2048]{2,1,0:T(2,128)(2,1)S(1)} %bitcast.82), channel_id=1, replica_groups=mesh['grp'=16,'dev_0'=4,'dev_1'=8] {'grp','dev_0'}, dimensions={0} | all-to-all | bytes 1048576 | tf_op jit(solution)/shard_map/all_to_all | solution.py:209
  115.8 1.0 reshape.246
  116.9 51.4 %all-gather.2.cloned.1.call-done = bf16[1024,2048]{1,0:T(8,128)(2,1)} async-done(((bf16[128,2048]{1,0:T(8,128)(2,1)}), bf16[1024,2048]{1,0:T(8,128)(2,1)}) %all-gather.2.cloned.1.call-update) | async-done | bytes 4194320 | tf_op jit(solution)/shard_map/all_gather | solution.py:212
  168.3 4.8 %fusion.3 = f32[1024,512]{1,0:T(8,128)S(1)} fusion(bf16[1024,2048]{1,0:T(8,128)(2,1)} %all-gather.2.cloned.1.call-done, bf16[2048,256]{1,0:T(8,128)(2,1)S(1)} %bitcast.92, bf16[2048,256]{1,0:T(8,128)(2,1)} %bitcast.93), kind=kOutput, calls=%fused_computation.9 | convolution fusion | flops 2151677952 | bytes 8388608 | tf_op jit(solution)/shard_map/dot_general | solution.py:214
  173.1 0.3 fusion.15
  173.4 3.2 %convolution_convert_fusion.1 = bf16[1024,2048]{1,0:T(8,128)(2,1)} fusion(bf16[1024,256]{1,0:T(8,128)(2,1)S(1)} %fusion.15, bf16[1,256,2048]{2,1,0:T(8,128)(2,1)S(1)} %copy-done), kind=kOutput, calls=%fused_computation.1 | convolution fusion | flops 1075838976 | bytes 5767168 | tf_op jit(solution)/shard_map/dot_general | solution.py:221
  176.6 56.9 %reduce-scatter.2.cloned.1.call-done = bf16[128,2048]{1,0:T(8,128)(2,1)} async-done(((bf16[1024,2048]{1,0:T(8,128)(2,1)}), bf16[128,2048]{1,0:T(8,128)(2,1)}) %reduce-scatter.2.cloned.1.call-update) | async-done | bytes 524304 | tf_op jit(solution)/shard_map/reduce_scatter | solution.py:222
  233.5 2.2 reshape.247
  235.7 11.0 %all-to-all-start.3 = ((bf16[64,2,2048]{2,1,0:T(2,128)(2,1)}), bf16[64,2,2048]{2,1,0:T(2,128)(2,1)S(1)}, u32[]{:S(2)}, u32[]{:S(2)}) async-start(bf16[64,2,2048]{2,1,0:T(2,128)(2,1)} %reshape.247), calls=%async_computation.4 | async-start | bytes 1048576 | tf_op jit(solution)/shard_map/all_to_all | solution.py:225
  246.7 0.3 select_reduce_fusion.2
  247.1 16.8 %all-to-all-done.3 = bf16[64,2,2048]{2,1,0:T(2,128)(2,1)S(1)} async-done(((bf16[64,2,2048]{2,1,0:T(2,128)(2,1)}), bf16[64,2,2048]{2,1,0:T(2,128)(2,1)S(1)}, u32[]{:S(2)}, u32[]{:S(2)}) %all-to-all-start.3) | async-done | bytes 524320 | tf_op jit(solution)/shard_map/all_to_all | solution.py:225
  263.9 0.5 convert_reduce_fusion
  264.6 0.9 fusion.2
  (73 shorter events, 3.4 us)
Async XLA Ops:
  6.5 166.9 %copy-start = (bf16[1,256,2048]{2,1,0:T(8,128)(2,1)S(1)}, bf16[1,256,2048]{2,1,0:T(8,128)(2,1)}, u32[]{:S(2)}) copy-start(bf16[1,256,2048]{2,1,0:T(8,128)(2,1)} %param.31) | copy-start | bytes 3145732
  6.5 15.7 %copy-start.6 = (f32[256,2]{0,1:T(2,128)S(1)}, f32[256,2]{0,1:T(2,128)}, u32[]{:S(2)}) copy-start(f32[256,2]{0,1:T(2,128)} %param.18) | copy-start | bytes 6148
  6.5 15.8 %copy-start.1 = (bf16[256,128]{1,0:T(8,128)(2,1)S(1)}, bf16[256,128]{1,0:T(8,128)(2,1)}, u32[]{:S(2)}) copy-start(bf16[256,128]{1,0:T(8,128)(2,1)} %param.20) | copy-start | bytes 196612
  8.6 41.7 %copy-start.2 = (bf16[256,128]{1,0:T(8,128)(2,1)S(1)}, bf16[256,128]{1,0:T(8,128)(2,1)}, u32[]{:S(2)}) copy-start(bf16[256,128]{1,0:T(8,128)(2,1)} %param.21) | copy-start | bytes 196612
  8.6 43.0 %all-to-all-start = ((bf16[32,128,64]{1,2,0:T(8,128)(2,1)}), bf16[32,128,64]{1,2,0:T(8,128)(2,1)S(1)}, u32[]{:S(2)}, u32[]{:S(2)}) async-start(bf16[32,128,64]{1,2,0:T(8,128)(2,1)} %copy_bitcast_fusion), calls=%async_computation | async-start | bytes 1048576 | tf_op jit(solution)/shard_map/all_to_all | solution.py:165
  22.3 28.5 %copy-start.11 = (f32[2]{0:T(128)S(1)}, f32[2]{0:T(128)}, u32[]{:S(2)}) copy-start(f32[2]{0:T(128)} %param.22) | copy-start | bytes 28
  48.8 2.7 copy-start.3
  48.8 2.7 copy-start.8
  52.0 11.1 %copy-start.7 = (s32[8,2]{0,1:T(2,128)S(1)}, s32[8,2]{0,1:T(2,128)}, u32[]{:S(2)}) copy-start(s32[8,2]{0,1:T(2,128)} %param.28) | copy-start | bytes 196
  53.5 35.8 %all-to-all-start.1 = ((bf16[32,8,2176]{2,1,0:T(8,128)(2,1)}), bf16[32,8,2176]{2,1,0:T(8,128)(2,1)S(1)}, u32[]{:S(2)}, u32[]{:S(2)}) async-start(bf16[32,8,2176]{2,1,0:T(8,128)(2,1)} %fusion), calls=%async_computation.1 | async-start | bytes 2228224 | tf_op jit(solution)/shard_map/all_to_all | solution.py:184
  63.0 105.3 %all-gather.2.cloned.1.call-start = ((), (), s32[]{:S(2)}) async-start(), calls=%async_computation.5 | async-start | bytes 4718592 | tf_op jit(solution)/shard_map/all_gather | solution.py:212
  63.8 25.9 %copy-start.4 = (bf16[8,2048]{1,0:T(8,128)(2,1)S(1)}, bf16[8,2048]{1,0:T(8,128)(2,1)}, u32[]{:S(2)}) copy-start(bf16[8,2048]{1,0:T(8,128)(2,1)} %param.25) | copy-start | bytes 98308
  63.8 26.1 %copy-start.5 = (f32[2048]{0:T(1024)S(1)}, f32[2048]{0:T(1024)}, u32[]{:S(2)}) copy-start(f32[2048]{0:T(1024)} %param.26) | copy-start | bytes 24580
  89.5 78.7 %copy-start.9 = (bf16[1,2048,256]{2,1,0:T(8,128)(2,1)S(1)}, bf16[1,2048,256]{2,1,0:T(8,128)(2,1)}, u32[]{:S(2)}) copy-start(bf16[1,2048,256]{2,1,0:T(8,128)(2,1)} %param.30) | copy-start | bytes 3145732
  116.8 116.7 %reduce-scatter.2.cloned.1.call-start = ((), (), s32[]{:S(2)}) async-start(), calls=%async_computation.6 | async-start | bytes 4718592 | tf_op jit(solution)/shard_map/reduce_scatter | solution.py:222
  176.6 70.1 %copy-start.10 = (f32[2048,16]{0,1:T(8,128)S(1)}, f32[2048,16]{0,1:T(8,128)}, u32[]{:S(2)}) copy-start(f32[2048,16]{0,1:T(8,128)} %param.27) | copy-start | bytes 393220
  235.7 28.2 %all-to-all-start.3 = ((bf16[64,2,2048]{2,1,0:T(2,128)(2,1)}), bf16[64,2,2048]{2,1,0:T(2,128)(2,1)S(1)}, u32[]{:S(2)}, u32[]{:S(2)}) async-start(bf16[64,2,2048]{2,1,0:T(2,128)(2,1)} %reshape.247), calls=%async_computation.4 | async-start | bytes 1048576 | tf_op jit(solution)/shard_map/all_to_all | solution.py:225
Sparse Core Ops, SparseCore 0:
  116.9 51.2 all-gather.1
  176.8 56.6 reduce-scatter.1

commit v9 on v8

--- a/solution.py
+++ b/solution.py
@@ -181,11 +181,16 @@
     )
     lhs = jnp.concatenate([gated_gain, squares], axis=1).astype(jnp.bfloat16)
     payload = jnp.dot(lhs, rhs, preferred_element_type=jnp.float32).astype(jnp.bfloat16)
-    landed = lax.all_to_all(
-        payload.reshape(dev_count, block_rows, payload.shape[1]), DEV, 0, 0, tiled=True
-    ).astype(jnp.float32)
-    summed_proj = jnp.sum(landed[:, :, :model_dim], axis=0)
-    token_squares = jnp.sum(landed[:, :, model_dim], axis=0)
+    x_count = lax.axis_size("dev_0")
+    y_count = lax.axis_size("dev_1")
+    by_x = lax.all_to_all(
+        payload.reshape(x_count, y_count, block_rows, payload.shape[1]), "dev_0", 0, 0, tiled=True
+    )
+    by_x = jnp.sum(by_x.astype(jnp.float32), axis=0).astype(jnp.bfloat16)
+    landed = lax.all_to_all(by_x, "dev_1", 0, 0, tiled=True)
+    landed = jnp.sum(landed.astype(jnp.float32), axis=0)
+    summed_proj = landed[:, :model_dim]
+    token_squares = landed[:, model_dim]
     mamba_out = (
         summed_proj * lax.rsqrt(token_squares / inner_dim + EPSILON)[:, None]
     ).astype(jnp.bfloat16)
@@ -204,7 +209,6 @@
         filled.T.astype(jnp.bfloat16), normed, preferred_element_type=jnp.float32
     ).astype(jnp.bfloat16)
     outgoing = outgoing.reshape(experts, slot_cap, model_dim)
-    x_count = lax.axis_size("dev_0")
     outgoing = jnp.broadcast_to(outgoing[:, None], (experts, x_count, slot_cap, model_dim))
     arrived = lax.all_to_all(
         outgoing.reshape(experts * x_count, slot_cap, model_dim), ("grp", "dev_0"), 0, 0, tiled=True

time: 273 us -> 270 us (0.989)
  waiting for transfers between devices: 151 us -> 148 us
    all_to_all x1 -> x2, starting transfers between devices: 9.5 us -> 10.8 us  [the longest x1 6.38 us: shards(): landed = lax.all_to_all(by_x, 'dev_1', 0, 0, tiled=True)]
    all_to_all x1 -> x2, waiting for transfers between devices: 25.5 us -> 25.1 us  [the longest x1 15.3 us: shards(): lax.all_to_all(payload.reshape(x_count, y_count, block_rows, payload.shap...]
  transfers between devices with their start and end apart: 5 -> 6, of which waited for: 4 -> 5; matrix products, arithmetic and copies ran while one was open for 3% -> 3% of each run, Pallas kernels for 0% -> 0%
where the time goes in v9:
time: 270 us
  waiting for transfers between devices  148 us (55%)
  blocking collectives  49.1 us (18%)
  starting transfers between devices  32.5 us (12%)
  between operations  13.7 us (5%)
  matrix products  12.8 us (5%)
  local copies, waits for them, and re-layouts  9.39 us (3%)
  other arithmetic  4.69 us (2%)
    reduce_scatter x1, waiting for transfers between devices, shards(): lax.psum_scatter(partial_down.astype(jnp.bfloat16), 'dev_1', scatter_dime...  56.9 us
    all_gather x1, waiting for transfers between devices, shards(): lax.all_gather(arrived.reshape(-1, model_dim), 'dev_1', axis=0, tiled=True)  48.7 us
    all_gather x1, blocking collectives, side_by_side(): lax.all_gather(both, axis, axis=dim, tiled=True)  25.4 us
    all_to_all x1, blocking collectives, shards(): lax.all_to_all(outgoing.reshape(experts * x_count, slot_cap, model_dim),...  23.7 us
    all_to_all x1, waiting for transfers between devices, shards(): lax.all_to_all(summed.reshape(experts * x_count, slot_cap, model_dim), ('...  16.8 us
    all_to_all x1, waiting for transfers between devices, shards(): lax.all_to_all(payload.reshape(x_count, y_count, block_rows, payload.shap...  15.3 us
    all_to_all x1, starting transfers between devices, shards(): lax.all_to_all(summed.reshape(experts * x_count, slot_cap, model_dim), ('...  11 us
    all_to_all x1, starting transfers between devices, shards(): lax.all_to_all(out_proj.reshape(dev_count, -1, out_proj.shape[1]), DEV, 0...  10.6 us
  transfers between devices with their start and end apart: 6, of which 5 were waited for; matrix products, arithmetic and copies ran while one was open for 3% of the time, Pallas kernels for 0%

profile of v9, /device:TPU:1, one launch (start us, length us, event | category | flops | bytes accessed | tf_op | source)
XLA Modules:
  0.0 269.7 jit_solution(6882521227025079430)
XLA Ops:
  6.5 2.1 copy_bitcast_fusion
  8.6 10.6 %all-to-all-start = ((bf16[32,128,64]{1,2,0:T(8,128)(2,1)}), bf16[32,128,64]{1,2,0:T(8,128)(2,1)S(1)}, u32[]{:S(2)}, u32[]{:S(2)}) async-start(bf16[32,128,64]{1,2,0:T(8,128)(2,1)} %copy_bitcast_fusion), calls=%async_computation | async-start | bytes 1048576 | tf_op jit(solution)/shard_map/all_to_all | solution.py:165
  19.2 0.8 negate_bitcast_fusion
  20.0 0.6 reduce-window.6
  21.3 0.9 copy.61
  22.7 25.4 %all_gather.6 = bf16[16,2,8193]{2,1,0:T(2,128)(2,1)S(1)} all-gather(bf16[1,2,8193]{2,1,0:T(2,128)(2,1)S(1)} %pad_maximum_fusion), channel_id=1, replica_groups=mesh['grp'=16,'dev_0'=4,'dev_1'=8] {'grp'}, dimensions={0}, use_global_device_ids=true | all-gather | bytes 557124 | tf_op jit(solution)/shard_map/all_gather | solution.py:18
  48.1 0.7 slice.56
  49.3 0.4 reshape.235
  49.7 0.6 fusion.17
  50.8 0.6 fusion.7
  51.6 0.3 concatenate.28
  52.0 1.5 convolution_convert_fusion
  53.5 4.4 %all-to-all-start.1 = ((bf16[4,8,8,2176]{3,2,1,0:T(8,128)(2,1)}), bf16[4,8,8,2176]{3,2,1,0:T(8,128)(2,1)S(1)}, u32[]{:S(2)}, u32[]{:S(2)}) async-start(bf16[4,8,8,2176]{3,2,1,0:T(8,128)(2,1)} %bitcast.16), calls=%async_computation.1 | async-start | bytes 2228224 | tf_op jit(solution)/shard_map/all_to_all | solution.py:186
  58.1 15.3 %all-to-all-done.1 = bf16[4,8,8,2176]{3,2,1,0:T(8,128)(2,1)S(1)} async-done(((bf16[4,8,8,2176]{3,2,1,0:T(8,128)(2,1)}), bf16[4,8,8,2176]{3,2,1,0:T(8,128)(2,1)S(1)}, u32[]{:S(2)}, u32[]{:S(2)}) %all-to-all-start.1) | async-done | bytes 1114144 | tf_op jit(solution)/shard_map/all_to_all | solution.py:186
  73.4 0.9 reduce_sum.87
  74.3 6.4 %all-to-all-start.2 = ((bf16[8,8,2176]{2,1,0:T(8,128)(2,1)}), bf16[8,8,2176]{2,1,0:T(8,128)(2,1)S(1)}, u32[]{:S(2)}, u32[]{:S(2)}) async-start(bf16[8,8,2176]{2,1,0:T(8,128)(2,1)} %reduce_sum.87), calls=%async_computation.2 | async-start | bytes 557056 | tf_op jit(solution)/shard_map/all_to_all | solution.py:190
  81.3 9.8 %all-to-all-done.2 = bf16[8,8,2176]{2,1,0:T(8,128)(2,1)S(1)} async-done(((bf16[8,8,2176]{2,1,0:T(8,128)(2,1)}), bf16[8,8,2176]{2,1,0:T(8,128)(2,1)S(1)}, u32[]{:S(2)}, u32[]{:S(2)}) %all-to-all-start.2) | async-done | bytes 278560 | tf_op jit(solution)/shard_map/all_to_all | solution.py:190
  91.4 0.2 convolution_convert_fusion.2
  91.8 0.3 broadcast_in_dim.79
  92.1 23.7 %all_to_all.25 = bf16[64,2,2048]{2,1,0:T(2,128)(2,1)S(1)} all-to-all(bf16[64,2,2048]{2,1,0:T(2,128)(2,1)S(1)} %bitcast.81), channel_id=1, replica_groups=mesh['grp'=16,'dev_0'=4,'dev_1'=8] {'grp','dev_0'}, dimensions={0} | all-to-all | bytes 1048576 | tf_op jit(solution)/shard_map/all_to_all | solution.py:213
  115.9 1.0 reshape.241
  116.9 48.7 %all-gather.2.cloned.1.call-done = bf16[1024,2048]{1,0:T(8,128)(2,1)} async-done(((bf16[128,2048]{1,0:T(8,128)(2,1)}), bf16[1024,2048]{1,0:T(8,128)(2,1)}) %all-gather.2.cloned.1.call-update) | async-done | bytes 4194320 | tf_op jit(solution)/shard_map/all_gather | solution.py:216
  165.6 4.8 %fusion.2 = f32[1024,512]{1,0:T(8,128)S(1)} fusion(bf16[1024,2048]{1,0:T(8,128)(2,1)} %all-gather.2.cloned.1.call-done, bf16[2048,256]{1,0:T(8,128)(2,1)S(1)} %bitcast.91, bf16[2048,256]{1,0:T(8,128)(2,1)} %bitcast.92), kind=kOutput, calls=%fused_computation.7 | convolution fusion | flops 2151677952 | bytes 8388608 | tf_op jit(solution)/shard_map/dot_general | solution.py:218
  170.5 0.3 fusion.14
  170.8 3.2 %convolution_convert_fusion.1 = bf16[1024,2048]{1,0:T(8,128)(2,1)} fusion(bf16[1024,256]{1,0:T(8,128)(2,1)S(1)} %fusion.14, bf16[1,256,2048]{2,1,0:T(8,128)(2,1)S(1)} %copy-done), kind=kOutput, calls=%fused_computation.1 | convolution fusion | flops 1075838976 | bytes 5767168 | tf_op jit(solution)/shard_map/dot_general | solution.py:225
  174.0 56.9 %reduce-scatter.2.cloned.1.call-done = bf16[128,2048]{1,0:T(8,128)(2,1)} async-done(((bf16[1024,2048]{1,0:T(8,128)(2,1)}), bf16[128,2048]{1,0:T(8,128)(2,1)}) %reduce-scatter.2.cloned.1.call-update) | async-done | bytes 524304 | tf_op jit(solution)/shard_map/reduce_scatter | solution.py:226
  230.9 2.2 reshape.242
  233.0 11.0 %all-to-all-start.4 = ((bf16[64,2,2048]{2,1,0:T(2,128)(2,1)}), bf16[64,2,2048]{2,1,0:T(2,128)(2,1)S(1)}, u32[]{:S(2)}, u32[]{:S(2)}) async-start(bf16[64,2,2048]{2,1,0:T(2,128)(2,1)} %reshape.242), calls=%async_computation.5 | async-start | bytes 1048576 | tf_op jit(solution)/shard_map/all_to_all | solution.py:229
  244.1 0.3 select_reduce_fusion.2
  244.5 16.8 %all-to-all-done.4 = bf16[64,2,2048]{2,1,0:T(2,128)(2,1)S(1)} async-done(((bf16[64,2,2048]{2,1,0:T(2,128)(2,1)}), bf16[64,2,2048]{2,1,0:T(2,128)(2,1)S(1)}, u32[]{:S(2)}, u32[]{:S(2)}) %all-to-all-start.4) | async-done | bytes 524320 | tf_op jit(solution)/shard_map/all_to_all | solution.py:229
  261.3 0.5 convert_reduce_fusion
  262.0 0.9 fusion.1
  (74 shorter events, 3.8 us)
Async XLA Ops:
  6.5 164.3 %copy-start = (bf16[1,256,2048]{2,1,0:T(8,128)(2,1)S(1)}, bf16[1,256,2048]{2,1,0:T(8,128)(2,1)}, u32[]{:S(2)}) copy-start(bf16[1,256,2048]{2,1,0:T(8,128)(2,1)} %param.31) | copy-start | bytes 3145732
  6.5 15.7 %copy-start.6 = (f32[256,2]{0,1:T(2,128)S(1)}, f32[256,2]{0,1:T(2,128)}, u32[]{:S(2)}) copy-start(f32[256,2]{0,1:T(2,128)} %param.18) | copy-start | bytes 6148
  6.5 15.8 %copy-start.1 = (bf16[256,128]{1,0:T(8,128)(2,1)S(1)}, bf16[256,128]{1,0:T(8,128)(2,1)}, u32[]{:S(2)}) copy-start(bf16[256,128]{1,0:T(8,128)(2,1)} %param.20) | copy-start | bytes 196612
  8.6 41.7 %copy-start.2 = (bf16[256,128]{1,0:T(8,128)(2,1)S(1)}, bf16[256,128]{1,0:T(8,128)(2,1)}, u32[]{:S(2)}) copy-start(bf16[256,128]{1,0:T(8,128)(2,1)} %param.21) | copy-start | bytes 196612
  8.6 43.0 %all-to-all-start = ((bf16[32,128,64]{1,2,0:T(8,128)(2,1)}), bf16[32,128,64]{1,2,0:T(8,128)(2,1)S(1)}, u32[]{:S(2)}, u32[]{:S(2)}) async-start(bf16[32,128,64]{1,2,0:T(8,128)(2,1)} %copy_bitcast_fusion), calls=%async_computation | async-start | bytes 1048576 | tf_op jit(solution)/shard_map/all_to_all | solution.py:165
  22.3 28.5 %copy-start.11 = (f32[2]{0:T(128)S(1)}, f32[2]{0:T(128)}, u32[]{:S(2)}) copy-start(f32[2]{0:T(128)} %param.22) | copy-start | bytes 28
  48.8 2.7 copy-start.3
  48.8 2.7 copy-start.8
  52.0 5.9 %copy-start.7 = (s32[8,2]{0,1:T(2,128)S(1)}, s32[8,2]{0,1:T(2,128)}, u32[]{:S(2)}) copy-start(s32[8,2]{0,1:T(2,128)} %param.28) | copy-start | bytes 196
  53.5 37.8 %copy-start.4 = (bf16[8,2048]{1,0:T(8,128)(2,1)S(1)}, bf16[8,2048]{1,0:T(8,128)(2,1)}, u32[]{:S(2)}) copy-start(bf16[8,2048]{1,0:T(8,128)(2,1)} %param.25) | copy-start | bytes 98308
  53.5 38.0 %copy-start.5 = (f32[2048]{0:T(1024)S(1)}, f32[2048]{0:T(1024)}, u32[]{:S(2)}) copy-start(f32[2048]{0:T(1024)} %param.26) | copy-start | bytes 24580
  53.5 19.9 %all-to-all-start.1 = ((bf16[4,8,8,2176]{3,2,1,0:T(8,128)(2,1)}), bf16[4,8,8,2176]{3,2,1,0:T(8,128)(2,1)S(1)}, u32[]{:S(2)}, u32[]{:S(2)}) async-start(bf16[4,8,8,2176]{3,2,1,0:T(8,128)(2,1)} %bitcast.16), calls=%async_computation.1 | async-start | bytes 2228224 | tf_op jit(solution)/shard_map/all_to_all | solution.py:186
  74.3 16.8 %all-to-all-start.2 = ((bf16[8,8,2176]{2,1,0:T(8,128)(2,1)}), bf16[8,8,2176]{2,1,0:T(8,128)(2,1)S(1)}, u32[]{:S(2)}, u32[]{:S(2)}) async-start(bf16[8,8,2176]{2,1,0:T(8,128)(2,1)} %reduce_sum.87), calls=%async_computation.2 | async-start | bytes 557056 | tf_op jit(solution)/shard_map/all_to_all | solution.py:190
  80.7 85.0 %copy-start.9 = (bf16[1,2048,256]{2,1,0:T(8,128)(2,1)S(1)}, bf16[1,2048,256]{2,1,0:T(8,128)(2,1)}, u32[]{:S(2)}) copy-start(bf16[1,2048,256]{2,1,0:T(8,128)(2,1)} %param.30) | copy-start | bytes 3145732
  80.7 85.0 %all-gather.2.cloned.1.call-start = ((), (), s32[]{:S(2)}) async-start(), calls=%async_computation.6 | async-start | bytes 4718592 | tf_op jit(solution)/shard_map/all_gather | solution.py:216
  116.9 114.0 %reduce-scatter.2.cloned.1.call-start = ((), (), s32[]{:S(2)}) async-start(), calls=%async_computation.7 | async-start | bytes 4718592 | tf_op jit(solution)/shard_map/reduce_scatter | solution.py:226
  174.0 70.1 %copy-start.10 = (f32[2048,16]{0,1:T(8,128)S(1)}, f32[2048,16]{0,1:T(8,128)}, u32[]{:S(2)}) copy-start(f32[2048,16]{0,1:T(8,128)} %param.27) | copy-start | bytes 393220
  233.0 28.2 %all-to-all-start.4 = ((bf16[64,2,2048]{2,1,0:T(2,128)(2,1)}), bf16[64,2,2048]{2,1,0:T(2,128)(2,1)S(1)}, u32[]{:S(2)}, u32[]{:S(2)}) async-start(bf16[64,2,2048]{2,1,0:T(2,128)(2,1)} %reshape.242), calls=%async_computation.5 | async-start | bytes 1048576 | tf_op jit(solution)/shard_map/all_to_all | solution.py:229
Sparse Core Ops, SparseCore 0:
  117.0 48.5 all-gather.1
  174.1 56.6 reduce-scatter.1

commit v10 on v9

--- a/solution.py
+++ b/solution.py
@@ -183,11 +183,15 @@
     payload = jnp.dot(lhs, rhs, preferred_element_type=jnp.float32).astype(jnp.bfloat16)
     x_count = lax.axis_size("dev_0")
     y_count = lax.axis_size("dev_1")
-    by_x = lax.all_to_all(
-        payload.reshape(x_count, y_count, block_rows, payload.shape[1]), "dev_0", 0, 0, tiled=True
-    )
-    by_x = jnp.sum(by_x.astype(jnp.float32), axis=0).astype(jnp.bfloat16)
-    landed = lax.all_to_all(by_x, "dev_1", 0, 0, tiled=True)
+    by_y = lax.all_to_all(
+        jnp.swapaxes(payload.reshape(x_count, y_count, block_rows, payload.shape[1]), 0, 1),
+        "dev_1",
+        0,
+        0,
+        tiled=True,
+    )
+    by_y = jnp.sum(by_y.astype(jnp.float32), axis=0).astype(jnp.bfloat16)
+    landed = lax.all_to_all(by_y, "dev_0", 0, 0, tiled=True)
     landed = jnp.sum(landed.astype(jnp.float32), axis=0)
     summed_proj = landed[:, :model_dim]
     token_squares = landed[:, model_dim]

time: 270 us -> 277 us (1.026)
  waiting for transfers between devices: 148 us -> 157 us
    all_to_all x2, waiting for transfers between devices: 25.1 us -> 34.8 us  [the longest x1 30 us: shards(): lax.all_to_all(jnp.swapaxes(payload.reshape(x_count, y_count, block_rows,...]
  transfers between devices with their start and end apart: 6 -> 6, of which waited for: 5 -> 5; matrix products, arithmetic and copies ran while one was open for 3% -> 2% of each run, Pallas kernels for 0% -> 0%
where the time goes in v10:
time: 277 us
  waiting for transfers between devices  157 us (57%)
  blocking collectives  48.2 us (17%)
  starting transfers between devices  32.4 us (12%)
  between operations  13.8 us (5%)
  matrix products  11.8 us (4%)
  local copies, waits for them, and re-layouts  9.65 us (3%)
  other arithmetic  3.87 us (1%)
    reduce_scatter x1, waiting for transfers between devices, shards(): lax.psum_scatter(partial_down.astype(jnp.bfloat16), 'dev_1', scatter_dime...  56.8 us
    all_gather x1, waiting for transfers between devices, shards(): lax.all_gather(arrived.reshape(-1, model_dim), 'dev_1', axis=0, tiled=True)  48.7 us
    all_to_all x1, waiting for transfers between devices, shards(): lax.all_to_all(jnp.swapaxes(payload.reshape(x_count, y_count, block_rows,...  30 us
    all_gather x1, blocking collectives, side_by_side(): lax.all_gather(both, axis, axis=dim, tiled=True)  25.4 us
    all_to_all x1, blocking collectives, shards(): lax.all_to_all(outgoing.reshape(experts * x_count, slot_cap, model_dim),...  22.8 us
    all_to_all x1, waiting for transfers between devices, shards(): lax.all_to_all(summed.reshape(experts * x_count, slot_cap, model_dim), ('...  16.8 us
    all_to_all x1, starting transfers between devices, shards(): lax.all_to_all(summed.reshape(experts * x_count, slot_cap, model_dim), ('...  11 us
    all_to_all x1, starting transfers between devices, shards(): lax.all_to_all(out_proj.reshape(dev_count, -1, out_proj.shape[1]), DEV, 0...  10.5 us
  transfers between devices with their start and end apart: 6, of which 5 were waited for; matrix products, arithmetic and copies ran while one was open for 2% of the time, Pallas kernels for 0%

profile of v10, /device:TPU:1, one launch (start us, length us, event | category | flops | bytes accessed | tf_op | source)
XLA Modules:
  0.0 276.8 jit_solution(6764212261096850166)
XLA Ops:
  6.5 2.1 copy_bitcast_fusion.1
  8.6 10.5 %all-to-all-start = ((bf16[32,128,64]{1,2,0:T(8,128)(2,1)}), bf16[32,128,64]{1,2,0:T(8,128)(2,1)S(1)}, u32[]{:S(2)}, u32[]{:S(2)}) async-start(bf16[32,128,64]{1,2,0:T(8,128)(2,1)} %copy_bitcast_fusion.1), calls=%async_computation | async-start | bytes 1048576 | tf_op jit(solution)/shard_map/all_to_all | solution.py:165
  19.3 0.6 reduce-window.6
  21.1 25.4 %all_gather.6 = bf16[16,2,8193]{2,1,0:T(2,128)(2,1)S(1)} all-gather(bf16[1,2,8193]{2,1,0:T(2,128)(2,1)S(1)} %pad_maximum_fusion), channel_id=1, replica_groups=mesh['grp'=16,'dev_0'=4,'dev_1'=8] {'grp'}, dimensions={0}, use_global_device_ids=true | all-gather | bytes 557124 | tf_op jit(solution)/shard_map/all_gather | solution.py:18
  46.5 0.7 slice.56
  47.7 0.4 reshape.235
  48.1 0.6 fusion.17
  48.7 0.2 fusion.8
  49.2 0.6 fusion.7
  50.0 0.3 concatenate.28
  50.4 0.5 convolution_convert_fusion
  50.9 1.1 copy.89
  52.0 6.8 %all-to-all-start.1 = ((bf16[8,4,8,2176]{3,2,1,0:T(8,128)(2,1)}), bf16[8,4,8,2176]{3,2,1,0:T(8,128)(2,1)S(1)}, u32[]{:S(2)}, u32[]{:S(2)}) async-start(bf16[8,4,8,2176]{3,2,1,0:T(8,128)(2,1)} %bitcast.80), calls=%async_computation.1 | async-start | bytes 2228224 | tf_op jit(solution)/shard_map/all_to_all | solution.py:186
  59.4 30.0 %all-to-all-done.1 = bf16[8,4,8,2176]{3,2,1,0:T(8,128)(2,1)S(1)} async-done(((bf16[8,4,8,2176]{3,2,1,0:T(8,128)(2,1)}), bf16[8,4,8,2176]{3,2,1,0:T(8,128)(2,1)S(1)}, u32[]{:S(2)}, u32[]{:S(2)}) %all-to-all-start.1) | async-done | bytes 1114144 | tf_op jit(solution)/shard_map/all_to_all | solution.py:186
  89.4 0.8 reduce_sum.87
  90.2 4.0 %all-to-all-start.2 = ((bf16[4,8,2176]{2,1,0:T(8,128)(2,1)}), bf16[4,8,2176]{2,1,0:T(8,128)(2,1)S(1)}, u32[]{:S(2)}, u32[]{:S(2)}) async-start(bf16[4,8,2176]{2,1,0:T(8,128)(2,1)} %reduce_sum.87), calls=%async_computation.2 | async-start | bytes 278528 | tf_op jit(solution)/shard_map/all_to_all | solution.py:194
  94.3 4.8 %all-to-all-done.2 = bf16[4,8,2176]{2,1,0:T(8,128)(2,1)S(1)} async-done(((bf16[4,8,2176]{2,1,0:T(8,128)(2,1)}), bf16[4,8,2176]{2,1,0:T(8,128)(2,1)S(1)}, u32[]{:S(2)}, u32[]{:S(2)}) %all-to-all-start.2) | async-done | bytes 139296 | tf_op jit(solution)/shard_map/all_to_all | solution.py:194
  99.5 0.2 convolution_convert_fusion.2
  99.9 0.3 broadcast_in_dim.79
  100.2 22.8 %all_to_all.25 = bf16[64,2,2048]{2,1,0:T(2,128)(2,1)S(1)} all-to-all(bf16[64,2,2048]{2,1,0:T(2,128)(2,1)S(1)} %bitcast.84), channel_id=1, replica_groups=mesh['grp'=16,'dev_0'=4,'dev_1'=8] {'grp','dev_0'}, dimensions={0} | all-to-all | bytes 1048576 | tf_op jit(solution)/shard_map/all_to_all | solution.py:217
  123.0 1.0 reshape.241
  124.1 48.7 %all-gather.2.cloned.1.call-done = bf16[1024,2048]{1,0:T(8,128)(2,1)} async-done(((bf16[128,2048]{1,0:T(8,128)(2,1)}), bf16[1024,2048]{1,0:T(8,128)(2,1)}) %all-gather.2.cloned.1.call-update) | async-done | bytes 4194320 | tf_op jit(solution)/shard_map/all_gather | solution.py:220
  172.8 4.8 %fusion.2 = f32[1024,512]{1,0:T(8,128)S(1)} fusion(bf16[1024,2048]{1,0:T(8,128)(2,1)} %all-gather.2.cloned.1.call-done, bf16[2048,256]{1,0:T(8,128)(2,1)S(1)} %bitcast.95, bf16[2048,256]{1,0:T(8,128)(2,1)} %bitcast.96), kind=kOutput, calls=%fused_computation.7 | convolution fusion | flops 2151677952 | bytes 8388608 | tf_op jit(solution)/shard_map/dot_general | solution.py:222
  177.6 0.3 fusion.14
  177.9 3.2 %convolution_convert_fusion.1 = bf16[1024,2048]{1,0:T(8,128)(2,1)} fusion(bf16[1024,256]{1,0:T(8,128)(2,1)S(1)} %fusion.14, bf16[1,256,2048]{2,1,0:T(8,128)(2,1)S(1)} %copy-done), kind=kOutput, calls=%fused_computation.1 | convolution fusion | flops 1075838976 | bytes 5767168 | tf_op jit(solution)/shard_map/dot_general | solution.py:229
  181.2 56.8 %reduce-scatter.2.cloned.1.call-done = bf16[128,2048]{1,0:T(8,128)(2,1)} async-done(((bf16[1024,2048]{1,0:T(8,128)(2,1)}), bf16[128,2048]{1,0:T(8,128)(2,1)}) %reduce-scatter.2.cloned.1.call-update) | async-done | bytes 524304 | tf_op jit(solution)/shard_map/reduce_scatter | solution.py:230
  238.0 2.2 reshape.242
  240.2 11.0 %all-to-all-start.4 = ((bf16[64,2,2048]{2,1,0:T(2,128)(2,1)}), bf16[64,2,2048]{2,1,0:T(2,128)(2,1)S(1)}, u32[]{:S(2)}, u32[]{:S(2)}) async-start(bf16[64,2,2048]{2,1,0:T(2,128)(2,1)} %reshape.242), calls=%async_computation.5 | async-start | bytes 1048576 | tf_op jit(solution)/shard_map/all_to_all | solution.py:233
  251.2 0.3 select_reduce_fusion.2
  251.6 16.8 %all-to-all-done.4 = bf16[64,2,2048]{2,1,0:T(2,128)(2,1)S(1)} async-done(((bf16[64,2,2048]{2,1,0:T(2,128)(2,1)}), bf16[64,2,2048]{2,1,0:T(2,128)(2,1)S(1)}, u32[]{:S(2)}, u32[]{:S(2)}) %all-to-all-start.4) | async-done | bytes 524320 | tf_op jit(solution)/shard_map/all_to_all | solution.py:233
  268.4 0.5 convert_reduce_fusion
  269.1 0.9 fusion.1
  (79 shorter events, 3.7 us)
Async XLA Ops:
  6.5 171.4 %copy-start = (bf16[1,256,2048]{2,1,0:T(8,128)(2,1)S(1)}, bf16[1,256,2048]{2,1,0:T(8,128)(2,1)}, u32[]{:S(2)}) copy-start(bf16[1,256,2048]{2,1,0:T(8,128)(2,1)} %param.31) | copy-start | bytes 3145732
  6.5 12.6 %copy-start.7 = (f32[256,2]{0,1:T(2,128)S(1)}, f32[256,2]{0,1:T(2,128)}, u32[]{:S(2)}) copy-start(f32[256,2]{0,1:T(2,128)} %param.18) | copy-start | bytes 6148
  6.5 12.6 %copy-start.10 = (f32[2]{0:T(128)S(1)}, f32[2]{0:T(128)}, u32[]{:S(2)}) copy-start(f32[2]{0:T(128)} %param.19) | copy-start | bytes 28
  6.5 14.0 %copy-start.4 = (bf16[256,128]{1,0:T(8,128)(2,1)S(1)}, bf16[256,128]{1,0:T(8,128)(2,1)}, u32[]{:S(2)}) copy-start(bf16[256,128]{1,0:T(8,128)(2,1)} %param.16) | copy-start | bytes 196612
  6.5 14.2 %copy-start.1 = (bf16[256,128]{1,0:T(8,128)(2,1)S(1)}, bf16[256,128]{1,0:T(8,128)(2,1)}, u32[]{:S(2)}) copy-start(bf16[256,128]{1,0:T(8,128)(2,1)} %param.20) | copy-start | bytes 196612
  8.6 41.4 %all-to-all-start = ((bf16[32,128,64]{1,2,0:T(8,128)(2,1)}), bf16[32,128,64]{1,2,0:T(8,128)(2,1)S(1)}, u32[]{:S(2)}, u32[]{:S(2)}) async-start(bf16[32,128,64]{1,2,0:T(8,128)(2,1)} %copy_bitcast_fusion.1), calls=%async_computation | async-start | bytes 1048576 | tf_op jit(solution)/shard_map/all_to_all | solution.py:165
  19.1 29.5 %copy-start.2 = (bf16[256,128]{1,0:T(8,128)(2,1)S(1)}, bf16[256,128]{1,0:T(8,128)(2,1)}, u32[]{:S(2)}) copy-start(bf16[256,128]{1,0:T(8,128)(2,1)} %param.21) | copy-start | bytes 196612
  20.9 28.2 %copy-start.13 = (f32[2]{0:T(128)S(1)}, f32[2]{0:T(128)}, u32[]{:S(2)}) copy-start(f32[2]{0:T(128)} %param.22) | copy-start | bytes 28
  47.2 2.7 copy-start.3
  47.2 2.7 copy-start.9
  50.9 7.9 %copy-start.8 = (s32[8,2]{0,1:T(2,128)S(1)}, s32[8,2]{0,1:T(2,128)}, u32[]{:S(2)}) copy-start(s32[8,2]{0,1:T(2,128)} %param.28) | copy-start | bytes 196
  52.0 47.3 %copy-start.5 = (bf16[8,2048]{1,0:T(8,128)(2,1)S(1)}, bf16[8,2048]{1,0:T(8,128)(2,1)}, u32[]{:S(2)}) copy-start(bf16[8,2048]{1,0:T(8,128)(2,1)} %param.25) | copy-start | bytes 98308
  52.0 47.5 %copy-start.6 = (f32[2048]{0:T(1024)S(1)}, f32[2048]{0:T(1024)}, u32[]{:S(2)}) copy-start(f32[2048]{0:T(1024)} %param.26) | copy-start | bytes 24580
  52.0 37.5 %all-to-all-start.1 = ((bf16[8,4,8,2176]{3,2,1,0:T(8,128)(2,1)}), bf16[8,4,8,2176]{3,2,1,0:T(8,128)(2,1)S(1)}, u32[]{:S(2)}, u32[]{:S(2)}) async-start(bf16[8,4,8,2176]{3,2,1,0:T(8,128)(2,1)} %bitcast.80), calls=%async_computation.1 | async-start | bytes 2228224 | tf_op jit(solution)/shard_map/all_to_all | solution.py:186
  90.2 8.9 %all-to-all-start.2 = ((bf16[4,8,2176]{2,1,0:T(8,128)(2,1)}), bf16[4,8,2176]{2,1,0:T(8,128)(2,1)S(1)}, u32[]{:S(2)}, u32[]{:S(2)}) async-start(bf16[4,8,2176]{2,1,0:T(8,128)(2,1)} %reduce_sum.87), calls=%async_computation.2 | async-start | bytes 278528 | tf_op jit(solution)/shard_map/all_to_all | solution.py:194
  94.3 78.5 %copy-start.11 = (bf16[1,2048,256]{2,1,0:T(8,128)(2,1)S(1)}, bf16[1,2048,256]{2,1,0:T(8,128)(2,1)}, u32[]{:S(2)}) copy-start(bf16[1,2048,256]{2,1,0:T(8,128)(2,1)} %param.30) | copy-start | bytes 3145732
  94.3 78.5 %all-gather.2.cloned.1.call-start = ((), (), s32[]{:S(2)}) async-start(), calls=%async_computation.6 | async-start | bytes 4718592 | tf_op jit(solution)/shard_map/all_gather | solution.py:220
  124.0 114.0 %reduce-scatter.2.cloned.1.call-start = ((), (), s32[]{:S(2)}) async-start(), calls=%async_computation.7 | async-start | bytes 4718592 | tf_op jit(solution)/shard_map/reduce_scatter | solution.py:230
  181.1 70.1 %copy-start.12 = (f32[2048,16]{0,1:T(8,128)S(1)}, f32[2048,16]{0,1:T(8,128)}, u32[]{:S(2)}) copy-start(f32[2048,16]{0,1:T(8,128)} %param.27) | copy-start | bytes 393220
  240.2 28.2 %all-to-all-start.4 = ((bf16[64,2,2048]{2,1,0:T(2,128)(2,1)}), bf16[64,2,2048]{2,1,0:T(2,128)(2,1)S(1)}, u32[]{:S(2)}, u32[]{:S(2)}) async-start(bf16[64,2,2048]{2,1,0:T(2,128)(2,1)} %reshape.242), calls=%async_computation.5 | async-start | bytes 1048576 | tf_op jit(solution)/shard_map/all_to_all | solution.py:233
Sparse Core Ops, SparseCore 0:
  124.1 48.5 all-gather.1
  181.3 56.6 reduce-scatter.1

commit v11 on v9

--- a/solution.py
+++ b/solution.py
@@ -4,8 +4,9 @@
 from jax.sharding import Mesh
 from jax.sharding import PartitionSpec as P
 
+GRP = ("grp_z", "grp_c")
 DEV = ("dev_0", "dev_1")
-GRP_DEV = ("grp", "dev_0", "dev_1")
+GRP_DEV = (*GRP, "dev_0", "dev_1")
 
 
 EPSILON = 1e-05
@@ -15,7 +16,9 @@
 def side_by_side(arrays, axis, dim, along):
     columns = [a.reshape(*a.shape[:along], -1) for a in arrays]
     both = jnp.concatenate(columns, axis=along)
-    filled, at, finished = (lax.all_gather(both, axis, axis=dim, tiled=True), 0, [])
+    for part in axis[::-1]:
+        both = lax.all_gather(both, part, axis=dim, tiled=True)
+    filled, at, finished = (both, 0, [])
     for a, column in zip(arrays, columns):
         piece = filled[..., at : at + column.shape[along]]
         finished.append(piece.reshape(*piece.shape[:along], *a.shape[along:]))
@@ -115,7 +118,7 @@
     inner_dim = ssm_input.shape[1] * dev_count
     block_rows = residual.shape[0]
     model_dim = residual.shape[1]
-    experts = lax.axis_size("grp")
+    experts = lax.axis_size(GRP)
     slot_cap = max(2, 4 * block_rows // experts)
     group_slots = experts * slot_cap
     inputs_f = ssm_input.astype(jnp.float32).reshape(tok_rows, head_count, head_width)
@@ -137,14 +140,14 @@
             part.astype(jnp.float32)
             for part in side_by_side(
                 (own_log[None].astype(jnp.bfloat16), own_state[None].astype(jnp.bfloat16)),
-                "grp",
+                GRP,
                 0,
                 2,
             )
         )
     )
     group_index = jnp.arange(group_logs.shape[0])
-    my_group = lax.axis_index("grp")
+    my_group = lax.axis_index(GRP)
     inclusive = jnp.cumsum(group_logs, axis=0)
     exclusive = inclusive - group_logs
     before_me = jnp.sum(jnp.where((group_index == my_group)[:, None], exclusive, 0.0), axis=0)
@@ -211,7 +214,7 @@
     outgoing = outgoing.reshape(experts, slot_cap, model_dim)
     outgoing = jnp.broadcast_to(outgoing[:, None], (experts, x_count, slot_cap, model_dim))
     arrived = lax.all_to_all(
-        outgoing.reshape(experts * x_count, slot_cap, model_dim), ("grp", "dev_0"), 0, 0, tiled=True
+        outgoing.reshape(experts * x_count, slot_cap, model_dim), (*GRP, "dev_0"), 0, 0, tiled=True
     )
     all_rows = lax.all_gather(arrived.reshape(-1, model_dim), "dev_1", axis=0, tiled=True)
     hid_units = gate_weight.shape[2]
@@ -227,7 +230,7 @@
         partial_down.astype(jnp.bfloat16), "dev_1", scatter_dimension=0, tiled=True
     )
     landed_back = lax.all_to_all(
-        summed.reshape(experts * x_count, slot_cap, model_dim), ("grp", "dev_0"), 0, 0, tiled=True
+        summed.reshape(experts * x_count, slot_cap, model_dim), (*GRP, "dev_0"), 0, 0, tiled=True
     )
     returned = jnp.sum(
         landed_back.reshape(experts, x_count, slot_cap, model_dim).astype(jnp.float32), axis=1
@@ -242,14 +245,14 @@
 
 
 def solution(mesh):
-    torus = Mesh(mesh.devices.reshape(mesh.shape["grp"], 4, 8), ("grp", "dev_0", "dev_1"))
+    torus = Mesh(mesh.devices.reshape(mesh.shape["grp"] // 2, 2, 4, 8), (*GRP, "dev_0", "dev_1"))
     in_specs = (
-        P("grp", DEV),
-        P("grp", DEV),
-        P("grp", DEV),
+        P(GRP, DEV),
+        P(GRP, DEV),
+        P(GRP, DEV),
         P(DEV),
-        P("grp", None),
-        P("grp", None),
+        P(GRP, None),
+        P(GRP, None),
         P(DEV),
         P(DEV),
         P(None, DEV),
@@ -257,9 +260,9 @@
         P(),
         P(),
         P(GRP_DEV, None),
-        P("grp", None, DEV),
-        P("grp", None, DEV),
-        P("grp", DEV, None),
+        P(GRP, None, DEV),
+        P(GRP, None, DEV),
+        P(GRP, DEV, None),
     )
     out_specs = P(GRP_DEV, None)
     return jax.shard_map(

time: 270 us -> 275 us (1.019)
  blocking collectives: 49.1 us -> 60.1 us
  waiting for transfers between devices: 148 us -> 141 us
    all_to_all x1, blocking collectives: 23.7 us -> 31.2 us  [shards(): lax.all_to_all(outgoing.reshape(experts * x_count, slot_cap, model_dim),...]
    all_to_all x1, waiting for transfers between devices: 15.3 us -> 9.93 us  [shards(): lax.all_to_all(payload.reshape(x_count, y_count, block_rows, payload.shap...]
    all_gather x1 -> x2, blocking collectives: 25.4 us -> 28.9 us  [side_by_side(): both = lax.all_gather(both, part, axis=dim, tiled=True)]
where the time goes in v11:
time: 275 us; the launch traced here: 274 us
  waiting for transfers between devices  141 us (51%)
  blocking collectives  60.1 us (22%)
  starting transfers between devices  32 us (12%)
  between operations  13.7 us (5%)
  matrix products  12.8 us (5%)
  local copies, waits for them, and re-layouts  9.39 us (3%)
  other arithmetic  4.72 us (2%)
    reduce_scatter x1, waiting for transfers between devices, shards(): lax.psum_scatter(partial_down.astype(jnp.bfloat16), 'dev_1', scatter_dime...  56.9 us
    all_gather x1, waiting for transfers between devices, shards(): lax.all_gather(arrived.reshape(-1, model_dim), 'dev_1', axis=0, tiled=True)  48.7 us
    all_to_all x1, blocking collectives, shards(): lax.all_to_all(outgoing.reshape(experts * x_count, slot_cap, model_dim),...  31.2 us
    all_gather x2, blocking collectives, side_by_side(): both = lax.all_gather(both, part, axis=dim, tiled=True)  28.9 us
    all_to_all x1, waiting for transfers between devices, shards(): lax.all_to_all(summed.reshape(experts * x_count, slot_cap, model_dim), (*...  16.8 us
    all_to_all x1, starting transfers between devices, shards(): lax.all_to_all(summed.reshape(experts * x_count, slot_cap, model_dim), (*...  11 us
    all_to_all x1, starting transfers between devices, shards(): lax.all_to_all(out_proj.reshape(dev_count, -1, out_proj.shape[1]), DEV, 0...  10.5 us
    all_to_all x1, waiting for transfers between devices, shards(): lax.all_to_all(payload.reshape(x_count, y_count, block_rows, payload.shap...  9.93 us
  transfers between devices with their start and end apart: 6, of which 5 were waited for; matrix products, arithmetic and copies ran while one was open for 3% of the time, Pallas kernels for 0%

profile of v11, /device:TPU:1, one launch (start us, length us, event | category | flops | bytes accessed | tf_op | source)
XLA Modules:
  0.0 273.9 jit_solution(11497689820521968857)
XLA Ops:
  6.5 2.1 copy_bitcast_fusion
  8.6 10.5 %all-to-all-start = ((bf16[32,128,64]{1,2,0:T(8,128)(2,1)}), bf16[32,128,64]{1,2,0:T(8,128)(2,1)S(1)}, u32[]{:S(2)}, u32[]{:S(2)}) async-start(bf16[32,128,64]{1,2,0:T(8,128)(2,1)} %copy_bitcast_fusion), calls=%async_computation | async-start | bytes 1048576 | tf_op jit(solution)/shard_map/all_to_all | solution.py:168
  19.1 0.8 negate_bitcast_fusion
  19.9 0.6 reduce-window.6
  21.2 0.9 copy.61
  22.6 2.5 all_gather.9
  25.1 26.5 %all_gather.10 = bf16[16,2,8193]{2,1,0:T(2,128)(2,1)S(1)} all-gather(bf16[2,2,8193]{2,1,0:T(2,128)(2,1)S(1)} %all_gather.9), channel_id=1, replica_groups=mesh['grp_z'=8,'grp_c'=2,'dev_0'=4,'dev_1'=8] {'grp_z'}, dimensions={0}, use_global_device_ids=true | all-gather | bytes 589896 | tf_op jit(solution)/shard_map/all_gather | solution.py:20
  51.5 0.7 slice.56
  52.7 0.4 reshape.235
  53.1 0.5 fusion.17
  54.2 0.6 fusion.7
  55.0 0.3 concatenate.28
  55.4 1.5 convolution_convert_fusion
  56.9 4.1 %all-to-all-start.1 = ((bf16[4,8,8,2176]{3,2,1,0:T(8,128)(2,1)}), bf16[4,8,8,2176]{3,2,1,0:T(8,128)(2,1)S(1)}, u32[]{:S(2)}, u32[]{:S(2)}) async-start(bf16[4,8,8,2176]{3,2,1,0:T(8,128)(2,1)} %bitcast.16), calls=%async_computation.1 | async-start | bytes 2228224 | tf_op jit(solution)/shard_map/all_to_all | solution.py:189
  61.1 9.9 %all-to-all-done.1 = bf16[4,8,8,2176]{3,2,1,0:T(8,128)(2,1)S(1)} async-done(((bf16[4,8,8,2176]{3,2,1,0:T(8,128)(2,1)}), bf16[4,8,8,2176]{3,2,1,0:T(8,128)(2,1)S(1)}, u32[]{:S(2)}, u32[]{:S(2)}) %all-to-all-start.1) | async-done | bytes 1114144 | tf_op jit(solution)/shard_map/all_to_all | solution.py:189
  71.1 0.9 reduce_sum.87
  72.0 6.4 %all-to-all-start.2 = ((bf16[8,8,2176]{2,1,0:T(8,128)(2,1)}), bf16[8,8,2176]{2,1,0:T(8,128)(2,1)S(1)}, u32[]{:S(2)}, u32[]{:S(2)}) async-start(bf16[8,8,2176]{2,1,0:T(8,128)(2,1)} %reduce_sum.87), calls=%async_computation.2 | async-start | bytes 557056 | tf_op jit(solution)/shard_map/all_to_all | solution.py:193
  79.0 8.9 %all-to-all-done.2 = bf16[8,8,2176]{2,1,0:T(8,128)(2,1)S(1)} async-done(((bf16[8,8,2176]{2,1,0:T(8,128)(2,1)}), bf16[8,8,2176]{2,1,0:T(8,128)(2,1)S(1)}, u32[]{:S(2)}, u32[]{:S(2)}) %all-to-all-start.2) | async-done | bytes 278560 | tf_op jit(solution)/shard_map/all_to_all | solution.py:193
  88.6 0.3 broadcast_in_dim.79
  88.9 31.2 %all_to_all.25 = bf16[64,2,2048]{2,1,0:T(2,128)(2,1)S(1)} all-to-all(bf16[64,2,2048]{2,1,0:T(2,128)(2,1)S(1)} %bitcast.81), channel_id=1, replica_groups=mesh['grp_z'=8,'grp_c'=2,'dev_0'=4,'dev_1'=8] {'grp_z','grp_c','dev_0'}, dimensions={0} | all-to-all | bytes 1048576 | tf_op jit(solution)/shard_map/all_to_all | solution.py:216
  120.1 1.0 reshape.241
  121.2 48.7 %all-gather.2.cloned.1.call-done = bf16[1024,2048]{1,0:T(8,128)(2,1)} async-done(((bf16[128,2048]{1,0:T(8,128)(2,1)}), bf16[1024,2048]{1,0:T(8,128)(2,1)}) %all-gather.2.cloned.1.call-update) | async-done | bytes 4194320 | tf_op jit(solution)/shard_map/all_gather | solution.py:219
  169.9 4.8 %fusion.2 = f32[1024,512]{1,0:T(8,128)S(1)} fusion(bf16[1024,2048]{1,0:T(8,128)(2,1)} %all-gather.2.cloned.1.call-done, bf16[2048,256]{1,0:T(8,128)(2,1)S(1)} %bitcast.91, bf16[2048,256]{1,0:T(8,128)(2,1)} %bitcast.92), kind=kOutput, calls=%fused_computation.7 | convolution fusion | flops 2151677952 | bytes 8388608 | tf_op jit(solution)/shard_map/dot_general | solution.py:221
  174.7 0.3 fusion.14
  175.0 3.2 %convolution_convert_fusion.1 = bf16[1024,2048]{1,0:T(8,128)(2,1)} fusion(bf16[1024,256]{1,0:T(8,128)(2,1)S(1)} %fusion.14, bf16[1,256,2048]{2,1,0:T(8,128)(2,1)S(1)} %copy-done), kind=kOutput, calls=%fused_computation.1 | convolution fusion | flops 1075838976 | bytes 5767168 | tf_op jit(solution)/shard_map/dot_general | solution.py:228
  178.2 56.9 %reduce-scatter.2.cloned.1.call-done = bf16[128,2048]{1,0:T(8,128)(2,1)} async-done(((bf16[1024,2048]{1,0:T(8,128)(2,1)}), bf16[128,2048]{1,0:T(8,128)(2,1)}) %reduce-scatter.2.cloned.1.call-update) | async-done | bytes 524304 | tf_op jit(solution)/shard_map/reduce_scatter | solution.py:229
  235.1 2.2 reshape.242
  237.3 11.0 %all-to-all-start.4 = ((bf16[64,2,2048]{2,1,0:T(2,128)(2,1)}), bf16[64,2,2048]{2,1,0:T(2,128)(2,1)S(1)}, u32[]{:S(2)}, u32[]{:S(2)}) async-start(bf16[64,2,2048]{2,1,0:T(2,128)(2,1)} %reshape.242), calls=%async_computation.5 | async-start | bytes 1048576 | tf_op jit(solution)/shard_map/all_to_all | solution.py:232
  248.3 0.3 select_reduce_fusion.2
  248.7 16.8 %all-to-all-done.4 = bf16[64,2,2048]{2,1,0:T(2,128)(2,1)S(1)} async-done(((bf16[64,2,2048]{2,1,0:T(2,128)(2,1)}), bf16[64,2,2048]{2,1,0:T(2,128)(2,1)S(1)}, u32[]{:S(2)}, u32[]{:S(2)}) %all-to-all-start.4) | async-done | bytes 524320 | tf_op jit(solution)/shard_map/all_to_all | solution.py:232
  265.5 0.5 convert_reduce_fusion
  266.2 0.9 fusion.1
  (75 shorter events, 4.0 us)
Async XLA Ops:
  6.5 168.5 %copy-start = (bf16[1,256,2048]{2,1,0:T(8,128)(2,1)S(1)}, bf16[1,256,2048]{2,1,0:T(8,128)(2,1)}, u32[]{:S(2)}) copy-start(bf16[1,256,2048]{2,1,0:T(8,128)(2,1)} %param.31) | copy-start | bytes 3145732
  6.5 15.6 %copy-start.6 = (f32[256,2]{0,1:T(2,128)S(1)}, f32[256,2]{0,1:T(2,128)}, u32[]{:S(2)}) copy-start(f32[256,2]{0,1:T(2,128)} %param.18) | copy-start | bytes 6148
  6.5 15.7 %copy-start.1 = (bf16[256,128]{1,0:T(8,128)(2,1)S(1)}, bf16[256,128]{1,0:T(8,128)(2,1)}, u32[]{:S(2)}) copy-start(bf16[256,128]{1,0:T(8,128)(2,1)} %param.20) | copy-start | bytes 196612
  8.6 46.4 %all-to-all-start = ((bf16[32,128,64]{1,2,0:T(8,128)(2,1)}), bf16[32,128,64]{1,2,0:T(8,128)(2,1)S(1)}, u32[]{:S(2)}, u32[]{:S(2)}) async-start(bf16[32,128,64]{1,2,0:T(8,128)(2,1)} %copy_bitcast_fusion), calls=%async_computation | async-start | bytes 1048576 | tf_op jit(solution)/shard_map/all_to_all | solution.py:168
  19.1 34.6 %copy-start.2 = (bf16[256,128]{1,0:T(8,128)(2,1)S(1)}, bf16[256,128]{1,0:T(8,128)(2,1)}, u32[]{:S(2)}) copy-start(bf16[256,128]{1,0:T(8,128)(2,1)} %param.21) | copy-start | bytes 196612
  22.3 31.9 %copy-start.11 = (f32[2]{0:T(128)S(1)}, f32[2]{0:T(128)}, u32[]{:S(2)}) copy-start(f32[2]{0:T(128)} %param.22) | copy-start | bytes 28
  52.2 2.7 copy-start.3
  52.2 2.7 copy-start.8
  55.4 5.6 %copy-start.7 = (s32[8,2]{0,1:T(2,128)S(1)}, s32[8,2]{0,1:T(2,128)}, u32[]{:S(2)}) copy-start(s32[8,2]{0,1:T(2,128)} %param.28) | copy-start | bytes 196
  56.9 31.1 %copy-start.4 = (bf16[8,2048]{1,0:T(8,128)(2,1)S(1)}, bf16[8,2048]{1,0:T(8,128)(2,1)}, u32[]{:S(2)}) copy-start(bf16[8,2048]{1,0:T(8,128)(2,1)} %param.25) | copy-start | bytes 98308
  56.9 31.4 %copy-start.5 = (f32[2048]{0:T(1024)S(1)}, f32[2048]{0:T(1024)}, u32[]{:S(2)}) copy-start(f32[2048]{0:T(1024)} %param.26) | copy-start | bytes 24580
  56.9 14.2 %all-to-all-start.1 = ((bf16[4,8,8,2176]{3,2,1,0:T(8,128)(2,1)}), bf16[4,8,8,2176]{3,2,1,0:T(8,128)(2,1)S(1)}, u32[]{:S(2)}, u32[]{:S(2)}) async-start(bf16[4,8,8,2176]{3,2,1,0:T(8,128)(2,1)} %bitcast.16), calls=%async_computation.1 | async-start | bytes 2228224 | tf_op jit(solution)/shard_map/all_to_all | solution.py:189
  72.0 15.9 %all-to-all-start.2 = ((bf16[8,8,2176]{2,1,0:T(8,128)(2,1)}), bf16[8,8,2176]{2,1,0:T(8,128)(2,1)S(1)}, u32[]{:S(2)}, u32[]{:S(2)}) async-start(bf16[8,8,2176]{2,1,0:T(8,128)(2,1)} %reduce_sum.87), calls=%async_computation.2 | async-start | bytes 557056 | tf_op jit(solution)/shard_map/all_to_all | solution.py:193
  78.4 91.5 %copy-start.9 = (bf16[1,2048,256]{2,1,0:T(8,128)(2,1)S(1)}, bf16[1,2048,256]{2,1,0:T(8,128)(2,1)}, u32[]{:S(2)}) copy-start(bf16[1,2048,256]{2,1,0:T(8,128)(2,1)} %param.30) | copy-start | bytes 3145732
  78.4 91.5 %all-gather.2.cloned.1.call-start = ((), (), s32[]{:S(2)}) async-start(), calls=%async_computation.6 | async-start | bytes 4718592 | tf_op jit(solution)/shard_map/all_gather | solution.py:219
  121.1 114.0 %reduce-scatter.2.cloned.1.call-start = ((), (), s32[]{:S(2)}) async-start(), calls=%async_computation.7 | async-start | bytes 4718592 | tf_op jit(solution)/shard_map/reduce_scatter | solution.py:229
  178.2 70.1 %copy-start.10 = (f32[2048,16]{0,1:T(8,128)S(1)}, f32[2048,16]{0,1:T(8,128)}, u32[]{:S(2)}) copy-start(f32[2048,16]{0,1:T(8,128)} %param.27) | copy-start | bytes 393220
  237.3 28.2 %all-to-all-start.4 = ((bf16[64,2,2048]{2,1,0:T(2,128)(2,1)}), bf16[64,2,2048]{2,1,0:T(2,128)(2,1)S(1)}, u32[]{:S(2)}, u32[]{:S(2)}) async-start(bf16[64,2,2048]{2,1,0:T(2,128)(2,1)} %reshape.242), calls=%async_computation.5 | async-start | bytes 1048576 | tf_op jit(solution)/shard_map/all_to_all | solution.py:232
Sparse Core Ops, SparseCore 0:
  121.2 48.5 all-gather.1
  178.4 56.6 reduce-scatter.1

commit v12 on v9

--- a/solution.py
+++ b/solution.py
@@ -186,6 +186,8 @@
     by_x = lax.all_to_all(
         payload.reshape(x_count, y_count, block_rows, payload.shape[1]), "dev_0", 0, 0, tiled=True
     )
+    both_weight = jnp.concatenate([gate_weight[0], up_weight[0]], axis=1)
+    by_x, both_weight = lax.optimization_barrier((by_x, both_weight))
     by_x = jnp.sum(by_x.astype(jnp.float32), axis=0).astype(jnp.bfloat16)
     landed = lax.all_to_all(by_x, "dev_1", 0, 0, tiled=True)
     landed = jnp.sum(landed.astype(jnp.float32), axis=0)
@@ -217,7 +219,7 @@
     hid_units = gate_weight.shape[2]
     both_act = jnp.dot(
         all_rows,
-        jnp.concatenate([gate_weight[0], up_weight[0]], axis=1),
+        both_weight,
         preferred_element_type=jnp.float32,
     )
     hidden = (jax.nn.silu(both_act[:, :hid_units]) * both_act[:, hid_units:]).astype(jnp.bfloat16)

time: 270 us -> 270 us (level)
  waiting for transfers between devices: 148 us -> 145 us
    all_to_all x1, waiting for transfers between devices: 15.3 us -> 12.6 us  [shards(): lax.all_to_all(payload.reshape(x_count, y_count, block_rows, payload.shap...]
    concatenate x0 -> x1, other arithmetic: none -> 2.72 us  [shards(): both_weight = jnp.concatenate([gate_weight[0], up_weight[0]], axis=1)]
where the time goes in v12:
time: 270 us; the launch traced here: 269 us
  waiting for transfers between devices  145 us (54%)
  blocking collectives  49.4 us (18%)
  starting transfers between devices  32.3 us (12%)
  between operations  13.8 us (5%)
  matrix products  12.5 us (5%)
  local copies, waits for them, and re-layouts  9.64 us (4%)
  other arithmetic  6.72 us (2%)
    reduce_scatter x1, waiting for transfers between devices, shards(): lax.psum_scatter(partial_down.astype(jnp.bfloat16), 'dev_1', scatter_dime...  56.8 us
    all_gather x1, waiting for transfers between devices, shards(): lax.all_gather(arrived.reshape(-1, model_dim), 'dev_1', axis=0, tiled=True)  48.8 us
    all_gather x1, blocking collectives, side_by_side(): lax.all_gather(both, axis, axis=dim, tiled=True)  25.4 us
    all_to_all x1, blocking collectives, shards(): lax.all_to_all(outgoing.reshape(experts * x_count, slot_cap, model_dim),...  24 us
    all_to_all x1, waiting for transfers between devices, shards(): lax.all_to_all(summed.reshape(experts * x_count, slot_cap, model_dim), ('...  16.8 us
    all_to_all x1, waiting for transfers between devices, shards(): lax.all_to_all(payload.reshape(x_count, y_count, block_rows, payload.shap...  12.6 us
    all_to_all x1, starting transfers between devices, shards(): lax.all_to_all(summed.reshape(experts * x_count, slot_cap, model_dim), ('...  11 us
    all_to_all x1, starting transfers between devices, shards(): lax.all_to_all(out_proj.reshape(dev_count, -1, out_proj.shape[1]), DEV, 0...  10.5 us
  transfers between devices with their start and end apart: 6, of which 5 were waited for; matrix products, arithmetic and copies ran while one was open for 3% of the time, Pallas kernels for 0%

profile of v12, /device:TPU:1, one launch (start us, length us, event | category | flops | bytes accessed | tf_op | source)
XLA Modules:
  0.0 269.2 jit_solution(579986233755267181)
XLA Ops:
  6.5 2.1 copy_bitcast_fusion
  8.6 10.5 %all-to-all-start = ((bf16[32,128,64]{1,2,0:T(8,128)(2,1)}), bf16[32,128,64]{1,2,0:T(8,128)(2,1)S(1)}, u32[]{:S(2)}, u32[]{:S(2)}) async-start(bf16[32,128,64]{1,2,0:T(8,128)(2,1)} %copy_bitcast_fusion), calls=%async_computation | async-start | bytes 1048576 | tf_op jit(solution)/shard_map/all_to_all | solution.py:165
  19.3 0.6 reduce-window.6
  21.1 25.4 %all_gather.6 = bf16[16,2,8193]{2,1,0:T(2,128)(2,1)S(1)} all-gather(bf16[1,2,8193]{2,1,0:T(2,128)(2,1)S(1)} %pad_maximum_fusion.1), channel_id=1, replica_groups=mesh['grp'=16,'dev_0'=4,'dev_1'=8] {'grp'}, dimensions={0}, use_global_device_ids=true | all-gather | bytes 557124 | tf_op jit(solution)/shard_map/all_gather | solution.py:18
  46.5 0.7 slice.56
  47.7 0.4 reshape.235
  48.1 0.6 fusion.13
  48.7 0.2 fusion.4
  49.2 0.6 fusion.3
  50.0 0.3 concatenate.28
  50.3 1.5 convolution_convert_fusion
  51.9 4.4 %all-to-all-start.1 = ((bf16[4,8,8,2176]{3,2,1,0:T(8,128)(2,1)}), bf16[4,8,8,2176]{3,2,1,0:T(8,128)(2,1)S(1)}, u32[]{:S(2)}, u32[]{:S(2)}) async-start(bf16[4,8,8,2176]{3,2,1,0:T(8,128)(2,1)} %bitcast.16), calls=%async_computation.1 | async-start | bytes 2228224 | tf_op jit(solution)/shard_map/all_to_all | solution.py:186
  56.5 2.7 %pad_maximum_fusion = bf16[2048,512]{1,0:T(8,128)(2,1)} fusion(bf16[2048,256]{1,0:T(8,128)(2,1)S(1)} %bitcast.83, bf16[2048,256]{1,0:T(8,128)(2,1)} %bitcast.84), kind=kLoop, calls=%fused_computation.7 | loop fusion | flops 4194304 | bytes 4194304 | tf_op jit(solution)/shard_map/concatenate | solution.py:189
  59.2 12.6 %all-to-all-done.1 = bf16[4,8,8,2176]{3,2,1,0:T(8,128)(2,1)S(1)} async-done(((bf16[4,8,8,2176]{3,2,1,0:T(8,128)(2,1)}), bf16[4,8,8,2176]{3,2,1,0:T(8,128)(2,1)S(1)}, u32[]{:S(2)}, u32[]{:S(2)}) %all-to-all-start.1) | async-done | bytes 1114144 | tf_op jit(solution)/shard_map/all_to_all | solution.py:186
  71.8 0.9 reduce_sum.87
  72.7 6.4 %all-to-all-start.2 = ((bf16[8,8,2176]{2,1,0:T(8,128)(2,1)}), bf16[8,8,2176]{2,1,0:T(8,128)(2,1)S(1)}, u32[]{:S(2)}, u32[]{:S(2)}) async-start(bf16[8,8,2176]{2,1,0:T(8,128)(2,1)} %reduce_sum.87), calls=%async_computation.2 | async-start | bytes 557056 | tf_op jit(solution)/shard_map/all_to_all | solution.py:192
  79.6 9.8 %all-to-all-done.2 = bf16[8,8,2176]{2,1,0:T(8,128)(2,1)S(1)} async-done(((bf16[8,8,2176]{2,1,0:T(8,128)(2,1)}), bf16[8,8,2176]{2,1,0:T(8,128)(2,1)S(1)}, u32[]{:S(2)}, u32[]{:S(2)}) %all-to-all-start.2) | async-done | bytes 278560 | tf_op jit(solution)/shard_map/all_to_all | solution.py:192
  89.8 0.2 convolution_convert_fusion.2
  90.2 0.3 broadcast_in_dim.79
  90.5 24.0 %all_to_all.25 = bf16[64,2,2048]{2,1,0:T(2,128)(2,1)} all-to-all(bf16[64,2,2048]{2,1,0:T(2,128)(2,1)S(1)} %bitcast.82), channel_id=1, replica_groups=mesh['grp'=16,'dev_0'=4,'dev_1'=8] {'grp','dev_0'}, dimensions={0} | all-to-all | bytes 1048576 | tf_op jit(solution)/shard_map/all_to_all | solution.py:215
  114.5 2.0 reshape.241
  116.6 48.8 %all-gather.2.cloned.1.call-done = bf16[1024,2048]{1,0:T(8,128)(2,1)} async-done(((bf16[128,2048]{1,0:T(8,128)(2,1)}), bf16[1024,2048]{1,0:T(8,128)(2,1)}) %all-gather.2.cloned.1.call-update) | async-done | bytes 4194320 | tf_op jit(solution)/shard_map/all_gather | solution.py:218
  165.4 4.5 %fusion.63 = f32[1024,512]{1,0:T(8,128)S(1)} fusion(bf16[1024,2048]{1,0:T(8,128)(2,1)} %all-gather.2.cloned.1.call-done, bf16[2048,512]{1,0:T(8,128)(2,1)S(1)} %copy-done.1), kind=kOutput, calls=%fused_computation.114 | convolution fusion | flops 2147483648 | bytes 8388608 | tf_op jit(solution)/shard_map/dot_general | solution.py:220
  169.9 0.3 fusion.10
  170.3 3.2 %convolution_convert_fusion.1 = bf16[1024,2048]{1,0:T(8,128)(2,1)} fusion(bf16[1024,256]{1,0:T(8,128)(2,1)S(1)} %fusion.10, bf16[1,256,2048]{2,1,0:T(8,128)(2,1)S(1)} %copy-done), kind=kOutput, calls=%fused_computation.1 | convolution fusion | flops 1075838976 | bytes 5767168 | tf_op jit(solution)/shard_map/dot_general | solution.py:227
  173.5 56.8 %reduce-scatter.2.cloned.1.call-done = bf16[128,2048]{1,0:T(8,128)(2,1)} async-done(((bf16[1024,2048]{1,0:T(8,128)(2,1)}), bf16[128,2048]{1,0:T(8,128)(2,1)}) %reduce-scatter.2.cloned.1.call-update) | async-done | bytes 524304 | tf_op jit(solution)/shard_map/reduce_scatter | solution.py:228
  230.3 2.2 reshape.242
  232.5 11.0 %all-to-all-start.4 = ((bf16[64,2,2048]{2,1,0:T(2,128)(2,1)}), bf16[64,2,2048]{2,1,0:T(2,128)(2,1)S(1)}, u32[]{:S(2)}, u32[]{:S(2)}) async-start(bf16[64,2,2048]{2,1,0:T(2,128)(2,1)} %reshape.242), calls=%async_computation.5 | async-start | bytes 1048576 | tf_op jit(solution)/shard_map/all_to_all | solution.py:231
  243.6 0.3 select_reduce_fusion.2
  244.0 16.8 %all-to-all-done.4 = bf16[64,2,2048]{2,1,0:T(2,128)(2,1)S(1)} async-done(((bf16[64,2,2048]{2,1,0:T(2,128)(2,1)}), bf16[64,2,2048]{2,1,0:T(2,128)(2,1)S(1)}, u32[]{:S(2)}, u32[]{:S(2)}) %all-to-all-start.4) | async-done | bytes 524320 | tf_op jit(solution)/shard_map/all_to_all | solution.py:231
  260.8 0.5 convert_reduce_fusion
  261.4 0.9 fusion.1
  (81 shorter events, 3.8 us)
Async XLA Ops:
  6.5 163.7 %copy-start = (bf16[1,256,2048]{2,1,0:T(8,128)(2,1)S(1)}, bf16[1,256,2048]{2,1,0:T(8,128)(2,1)}, u32[]{:S(2)}) copy-start(bf16[1,256,2048]{2,1,0:T(8,128)(2,1)} %param.31) | copy-start | bytes 3145732
  6.5 12.6 %copy-start.9 = (f32[256,2]{0,1:T(2,128)S(1)}, f32[256,2]{0,1:T(2,128)}, u32[]{:S(2)}) copy-start(f32[256,2]{0,1:T(2,128)} %param.18) | copy-start | bytes 6148
  6.5 12.6 %copy-start.12 = (f32[2]{0:T(128)S(1)}, f32[2]{0:T(128)}, u32[]{:S(2)}) copy-start(f32[2]{0:T(128)} %param.19) | copy-start | bytes 28
  6.5 14.0 %copy-start.6 = (bf16[256,128]{1,0:T(8,128)(2,1)S(1)}, bf16[256,128]{1,0:T(8,128)(2,1)}, u32[]{:S(2)}) copy-start(bf16[256,128]{1,0:T(8,128)(2,1)} %param.16) | copy-start | bytes 196612
  6.5 14.2 %copy-start.3 = (bf16[256,128]{1,0:T(8,128)(2,1)S(1)}, bf16[256,128]{1,0:T(8,128)(2,1)}, u32[]{:S(2)}) copy-start(bf16[256,128]{1,0:T(8,128)(2,1)} %param.20) | copy-start | bytes 196612
  8.6 41.4 %all-to-all-start = ((bf16[32,128,64]{1,2,0:T(8,128)(2,1)}), bf16[32,128,64]{1,2,0:T(8,128)(2,1)S(1)}, u32[]{:S(2)}, u32[]{:S(2)}) async-start(bf16[32,128,64]{1,2,0:T(8,128)(2,1)} %copy_bitcast_fusion), calls=%async_computation | async-start | bytes 1048576 | tf_op jit(solution)/shard_map/all_to_all | solution.py:165
  19.1 29.5 %copy-start.4 = (bf16[256,128]{1,0:T(8,128)(2,1)S(1)}, bf16[256,128]{1,0:T(8,128)(2,1)}, u32[]{:S(2)}) copy-start(bf16[256,128]{1,0:T(8,128)(2,1)} %param.21) | copy-start | bytes 196612
  20.9 28.2 %copy-start.14 = (f32[2]{0:T(128)S(1)}, f32[2]{0:T(128)}, u32[]{:S(2)}) copy-start(f32[2]{0:T(128)} %param.22) | copy-start | bytes 28
  47.2 2.7 %copy-start.5 = (bf16[256,128]{1,0:T(8,128)(2,1)S(1)}, bf16[256,128]{1,0:T(8,128)(2,1)}, u32[]{:S(2)}) copy-start(bf16[256,128]{1,0:T(8,128)(2,1)} %param.17) | copy-start | bytes 196612
  47.2 2.7 copy-start.11
  51.9 4.4 %copy-start.10 = (s32[8,2]{0,1:T(2,128)S(1)}, s32[8,2]{0,1:T(2,128)}, u32[]{:S(2)}) copy-start(s32[8,2]{0,1:T(2,128)} %param.28) | copy-start | bytes 196
  51.9 4.6 %copy-start.2 = (bf16[1,2048,256]{2,1,0:T(8,128)(2,1)S(1)}, bf16[1,2048,256]{2,1,0:T(8,128)(2,1)}, u32[]{:S(2)}) copy-start(bf16[1,2048,256]{2,1,0:T(8,128)(2,1)} %param.30) | copy-start | bytes 3145732
  51.9 19.9 %all-to-all-start.1 = ((bf16[4,8,8,2176]{3,2,1,0:T(8,128)(2,1)}), bf16[4,8,8,2176]{3,2,1,0:T(8,128)(2,1)S(1)}, u32[]{:S(2)}, u32[]{:S(2)}) async-start(bf16[4,8,8,2176]{3,2,1,0:T(8,128)(2,1)} %bitcast.16), calls=%async_computation.1 | async-start | bytes 2228224 | tf_op jit(solution)/shard_map/all_to_all | solution.py:186
  59.2 30.4 %copy-start.7 = (bf16[8,2048]{1,0:T(8,128)(2,1)S(1)}, bf16[8,2048]{1,0:T(8,128)(2,1)}, u32[]{:S(2)}) copy-start(bf16[8,2048]{1,0:T(8,128)(2,1)} %param.25) | copy-start | bytes 98308
  59.2 30.6 %copy-start.8 = (f32[2048]{0:T(1024)S(1)}, f32[2048]{0:T(1024)}, u32[]{:S(2)}) copy-start(f32[2048]{0:T(1024)} %param.26) | copy-start | bytes 24580
  72.7 16.8 %all-to-all-start.2 = ((bf16[8,8,2176]{2,1,0:T(8,128)(2,1)}), bf16[8,8,2176]{2,1,0:T(8,128)(2,1)S(1)}, u32[]{:S(2)}, u32[]{:S(2)}) async-start(bf16[8,8,2176]{2,1,0:T(8,128)(2,1)} %reduce_sum.87), calls=%async_computation.2 | async-start | bytes 557056 | tf_op jit(solution)/shard_map/all_to_all | solution.py:192
  79.0 86.4 %all-gather.2.cloned.1.call-start = ((), (), s32[]{:S(2)}) async-start(), calls=%async_computation.6 | async-start | bytes 4718592 | tf_op jit(solution)/shard_map/all_gather | solution.py:218
  79.6 85.8 %copy-start.1 = (bf16[2048,512]{1,0:T(8,128)(2,1)S(1)}, bf16[2048,512]{1,0:T(8,128)(2,1)}, u32[]{:S(2)}) copy-start(bf16[2048,512]{1,0:T(8,128)(2,1)} %pad_maximum_fusion) | copy-start | bytes 6291460
  116.6 113.8 %reduce-scatter.2.cloned.1.call-start = ((), (), s32[]{:S(2)}) async-start(), calls=%async_computation.7 | async-start | bytes 4718592 | tf_op jit(solution)/shard_map/reduce_scatter | solution.py:228
  173.5 70.1 %copy-start.13 = (f32[2048,16]{0,1:T(8,128)S(1)}, f32[2048,16]{0,1:T(8,128)}, u32[]{:S(2)}) copy-start(f32[2048,16]{0,1:T(8,128)} %param.27) | copy-start | bytes 393220
  232.5 28.2 %all-to-all-start.4 = ((bf16[64,2,2048]{2,1,0:T(2,128)(2,1)}), bf16[64,2,2048]{2,1,0:T(2,128)(2,1)S(1)}, u32[]{:S(2)}, u32[]{:S(2)}) async-start(bf16[64,2,2048]{2,1,0:T(2,128)(2,1)} %reshape.242), calls=%async_computation.5 | async-start | bytes 1048576 | tf_op jit(solution)/shard_map/all_to_all | solution.py:231
Sparse Core Ops, SparseCore 0:
  116.7 48.6 all-gather.1
  173.6 56.6 reduce-scatter.1
